TPU v7x, 128 devices: a whole 4x4x4 slice. The times are simulated.
128 devices in a mesh: group: 4 (over x), expert: 32 (over y, z, core).
Axes of the slice: x: 4, y: 4, z: 4, core: 2. Of those that a mesh axis runs over, the one named last changes fastest.
Arguments:
- tokens: bfloat16 [16384, 2048], P(('group', 'expert')), may hold values from -6 to 6
- cotangent: bfloat16 [16384, 2048], P(('group', 'expert')), may hold values from -6 to 6
- gate_probs: float32 [16384, 8], P(('group', 'expert')), may hold values from 0.02 to 0.5
- expert_ids: int32 [16384, 8], P(('group', 'expert')), may hold values from 0 to 31, all different within a row; in each aligned block of 128 rows (0 to 127, 128 to 255, ...) at most 72 rows name the same one
- gate_up: bfloat16 [32, 2048, 768], P('expert'), may hold values from -0.125 to 0.125
- down_weight: bfloat16 [32, 384, 2048], P('expert'), may hold values from -0.3125 to 0.3125
- gate_up_moment: float32 [32, 2048, 768], P('expert', 'group'), may hold values from -6 to 6
- gate_up_second: float32 [32, 2048, 768], P('expert', 'group'), may hold values from 0.05 to 20
- down_moment: float32 [32, 384, 2048], P('expert', None, 'group'), may hold values from -6 to 6
- down_second: float32 [32, 384, 2048], P('expert', None, 'group'), may hold values from 0.05 to 20
Outputs:
- token_grad: bfloat16 [16384, 2048], P(('group', 'expert'))
- updated_gate_up: bfloat16 [32, 2048, 768], P('expert')
- updated_down: bfloat16 [32, 384, 2048], P('expert')
- gate_up_moment_out: float32 [32, 2048, 768], P('expert', 'group')
- gate_up_second_out: float32 [32, 2048, 768], P('expert', 'group')
- down_moment_out: float32 [32, 384, 2048], P('expert', None, 'group')
- down_second_out: float32 [32, 384, 2048], P('expert', None, 'group')
Inputs may be any that keep to these rules, and one draw needn't show every extreme that they name: `expert_ids`: each row names 8 different experts. In the rows of one device no expert is named by more than 72 rows, and in every draw some expert is named by exactly 72 rows of some device.
All inputs are finite; a program needn't handle non-finite values.
Results may differ from a plain program's by a relative error of at most 0.015.
Values may be sent and summed in bfloat16 or wider, within the bound.
No kernel may reach another device: no remote copies, remote signals or barrier semaphores. Data moves between devices by JAX's collectives and lax.ppermute only.
A program may use at most 192 MiB of HBM per device.

v0:
```python
import jax
import jax.numpy as jnp
from jax import lax
from jax.sharding import PartitionSpec as P

learn_rate = 0.001
beta_first = 0.9
beta_second = 0.999
adam_eps = 1e-08


def expert_backward(inputs, scaled_grad, weight_gate_up, weight_down):
    hidden_count = weight_down.shape[0]
    projected = jnp.dot(inputs, weight_gate_up, preferred_element_type=jnp.float32)
    gate_part = projected[:, :hidden_count]
    up_part = projected[:, hidden_count:]
    sigmoid_gate = jax.nn.sigmoid(gate_part)
    activated = gate_part * sigmoid_gate
    hidden_act = (activated * up_part).astype(jnp.bfloat16)
    hidden_grad = jnp.dot(scaled_grad, weight_down.T, preferred_element_type=jnp.float32)
    slope = sigmoid_gate * (1.0 + gate_part * (1.0 - sigmoid_gate))
    pair_grad = jnp.concatenate(
        [hidden_grad * up_part * slope, hidden_grad * activated], axis=1
    ).astype(jnp.bfloat16)
    down_grad = jnp.dot(hidden_act.T, scaled_grad, preferred_element_type=jnp.float32)
    gate_up_grad = jnp.dot(inputs.T, pair_grad, preferred_element_type=jnp.float32)
    input_grad = jnp.dot(pair_grad, weight_gate_up.T, preferred_element_type=jnp.float32).astype(
        jnp.bfloat16
    )
    return (gate_up_grad, down_grad, input_grad)


def adam_update(weight, grad, first, second):
    first_new = beta_first * first + (1.0 - beta_first) * grad
    second_new = beta_second * second + (1.0 - beta_second) * grad * grad
    updated = (
        weight.astype(jnp.float32) - learn_rate * first_new / (jnp.sqrt(second_new) + adam_eps)
    ).astype(jnp.bfloat16)
    return (updated, first_new, second_new)


def slot_layout(expert_ids, expert_count, capacity):
    flat_ids = expert_ids.reshape(-1)
    onehot = (flat_ids[:, None] == jnp.arange(expert_count, dtype=jnp.int32)[None, :]).astype(
        jnp.int32
    )
    before = jnp.cumsum(onehot, axis=0) - onehot
    slot_rank = jnp.sum(before * onehot, axis=1)
    return flat_ids * capacity + slot_rank


def local(
    tokens,
    cotangent,
    gate_probs,
    expert_ids,
    gate_up,
    down_weight,
    gate_up_moment,
    gate_up_second,
    down_moment,
    down_second,
):
    expert_count = lax.axis_size("expert")
    local_tokens, model_width = tokens.shape
    top_count = expert_ids.shape[1]
    capacity = min(local_tokens, 9 * local_tokens * top_count // (4 * expert_count))
    slot_total = expert_count * capacity
    slot_index = slot_layout(expert_ids, expert_count, capacity)
    scaled = (gate_probs[:, :, None] * cotangent.astype(jnp.float32)[:, None, :]).astype(
        jnp.bfloat16
    )
    repeated = jnp.broadcast_to(tokens[:, None, :], (local_tokens, top_count, model_width))
    payload = jnp.stack([repeated, scaled], axis=2).reshape(
        local_tokens * top_count, 2, model_width
    )
    outgoing = jnp.zeros((slot_total, 2, model_width), jnp.bfloat16).at[slot_index].set(payload)
    outgoing = outgoing.reshape(expert_count, capacity, 2, model_width)
    received = lax.all_to_all(outgoing, "expert", split_axis=0, concat_axis=0, tiled=True)
    slot_rows = received.reshape(slot_total, 2, model_width)
    weight_pair = gate_up[0]
    weight_down = down_weight[0]
    grad_pair, grad_down, row_grads = expert_backward(
        slot_rows[:, 0], slot_rows[:, 1], weight_pair, weight_down
    )
    returned = lax.all_to_all(
        row_grads.reshape(expert_count, capacity, model_width),
        "expert",
        split_axis=0,
        concat_axis=0,
        tiled=True,
    )
    returned = returned.reshape(slot_total, model_width)
    token_grad = jnp.sum(
        returned[slot_index].reshape(local_tokens, top_count, model_width).astype(jnp.float32),
        axis=1,
    ).astype(jnp.bfloat16)
    sum_pair, sum_down = (
        lax.psum_scatter(
            grad_pair[None].astype(jnp.bfloat16), "group", scatter_dimension=1, tiled=True
        ).astype(jnp.float32),
        lax.psum_scatter(
            grad_down[None].astype(jnp.bfloat16), "group", scatter_dimension=2, tiled=True
        ).astype(jnp.float32),
    )
    group_index = lax.axis_index("group")
    share_rows = model_width // lax.axis_size("group")
    own_pair = lax.dynamic_slice_in_dim(gate_up, group_index * share_rows, share_rows, 1)
    own_down = lax.dynamic_slice_in_dim(down_weight, group_index * share_rows, share_rows, 2)
    new_pair, first_pair, second_pair = adam_update(
        own_pair, sum_pair, gate_up_moment, gate_up_second
    )
    new_down, first_down, second_down = adam_update(own_down, sum_down, down_moment, down_second)
    full_pair, full_down = (
        lax.all_gather(new_pair, "group", axis=1, tiled=True),
        lax.all_gather(new_down, "group", axis=2, tiled=True),
    )
    return (token_grad, full_pair, full_down, first_pair, second_pair, first_down, second_down)


def solution(mesh):
    placed = (
        P(("group", "expert"), None),
        P(("group", "expert"), None),
        P(("group", "expert"), None),
        P(("group", "expert"), None),
        P("expert", None, None),
        P("expert", None, None),
        P("expert", "group", None),
        P("expert", "group", None),
        P("expert", None, "group"),
        P("expert", None, "group"),
    )
    return jax.shard_map(
        local,
        mesh=mesh,
        in_specs=placed,
        out_specs=(
            P(("group", "expert"), None),
            P("expert", None, None),
            P("expert", None, None),
            P("expert", "group", None),
            P("expert", "group", None),
            P("expert", None, "group"),
            P("expert", None, "group"),
        ),
        check_vma=False,
    )
```

profile of v0, /device:TPU:50, one launch (start us, length us, event | category | flops | bytes accessed | tf_op | source)
XLA Modules:
  0.0 650.8 jit_solution(8910196216144405654)
XLA Ops:
  7.2 0.0 copy-start
  7.2 0.0 reduce-scatter.5.cloned.1.call-start
  7.2 0.7 broadcast_multiply_fusion
  8.0 0.8 copy.24
  8.8 0.1 eq.29
  8.8 0.1 eq.25
  8.9 0.1 copy.23
  9.0 0.1 mul.125
  9.1 0.8 copy.28
  9.9 0.1 mul.127
  10.0 9.0 %reduce-window.6 = s32[32,8,128]{2,1,0:T(8,128)S(1)} reduce-window(s32[32,8,128]{2,1,0:T(8,128)S(1)} %fusion.21, s32[]{:T(128)} %constant.16.clone.1), window={size=1x1x128 pad=0_0x0_0x127_0}, to_apply=%region_0.0 | reduce-window | flops 4161536 | bytes 262148 | tf_op jit(solution)/shard_map/reduce-window
  19.1 0.1 slice.26
  19.2 0.1 copy.26
  19.3 0.1 copy.27
  19.4 0.1 broadcast_add_fusion
  19.5 1.1 convert_element_type.62
  20.7 0.0 copy-done
  20.7 0.7 broadcast_bitcast_fusion
  21.3 2.4 fusion
  23.8 6.2 pad_maximum_fusion
  29.9 16.4 %copy.29 = bf16[1024,2,2048]{2,1,0:T(2,128)(2,1)} copy(bf16[1024,2,2048]{2,0,1:T(8,128)(2,1)} %pad_maximum_fusion) | data formatting | bytes 16777216 | tf_op jit(solution)/shard_map/stack | solution.py:74
  46.4 11.2 %broadcast_in_dim.2 = bf16[2304,2,2048]{2,1,0:T(2,128)(2,1)} broadcast(bf16[]{:T(256)} %constant.14.clone.1), dimensions={} | broadcast | bytes 18874370 | tf_op jit(solution)/shard_map/broadcast_in_dim | solution.py:77
  57.6 128.4 %scatter_fusion = bf16[2304,2,2048]{2,1,0:T(2,128)(2,1)} fusion(bf16[2304,2,2048]{2,1,0:T(2,128)(2,1)} %broadcast_in_dim.2, s32[1024]{0:T(1024)S(1)} %bitcast.72, bf16[1024,2,2048]{2,1,0:T(2,128)(2,1)} %copy.29), kind=kCustom, calls=%fused_computation.1 | custom fusion | bytes 25169920 | tf_op jit(solution)/shard_map/scatter | solution.py:77
  185.9 212.7 %all_to_all.10 = bf16[32,72,2,2048]{3,2,1,0:T(2,128)(2,1)S(1)} all-to-all(bf16[32,72,2,2048]{3,2,1,0:T(2,128)(2,1)} %bitcast.65), channel_id=1, replica_groups=mesh['group'=4,'expert'=32] {'expert'}, dimensions={0} | all-to-all | bytes 37748736 | tf_op jit(solution)/shard_map/all_to_all | solution.py:79
  398.7 0.0 copy-start.5
  398.7 9.5 %copy.30 = bf16[32,72,2,2048]{3,1,0,2:T(8,128)(2,1)} copy(bf16[32,72,2,2048]{3,2,1,0:T(2,128)(2,1)S(1)} %all_to_all.10) | data formatting | bytes 37748736 | tf_op jit(solution)/shard_map/all_to_all | solution.py:79
  408.2 0.0 copy-done.5
  408.2 10.0 %fusion.4 = f32[2304,768]{0,1:T(8,128)S(1)} fusion(bf16[2304,2,2048]{2,0,1:T(8,128)(2,1)} %bitcast.66, bf16[1,2048,768]{2,1,0:T(8,128)(2,1)S(1)} %copy-done.5), kind=kOutput, calls=%fused_computation.11 | convolution fusion | flops 7247757312 | bytes 19660800 | tf_op jit(solution)/shard_map/dot_general | solution.py:14
  418.2 0.0 copy-start.7
  418.2 2.9 copy-done.7
  421.1 0.0 copy-start.6
  421.1 8.8 %fusion.11 = bf16[1,384,2048]{2,1,0:T(8,128)(2,1)} fusion(bf16[2304,2,2048]{2,0,1:T(8,128)(2,1)} %bitcast.67, f32[2304,768]{0,1:T(8,128)S(1)} %fusion.4), kind=kOutput, calls=%fused_computation.24 | convolution fusion | flops 3629973504 | bytes 18087936 | tf_op jit(solution)/shard_map/dot_general | solution.py:25
  430.0 0.0 reduce-scatter.5.cloned.1.call-update
  430.0 0.2 reduce-scatter.3.cloned.1.call-start
  430.2 0.0 copy-done.6
  430.2 8.6 %multiply_convert_fusion.2 = (bf16[2304,384]{0,1:T(8,128)(2,1)S(1)}, bf16[2304,384]{0,1:T(8,128)(2,1)S(1)}) fusion(f32[2304,768]{0,1:T(8,128)} %copy-done.7, bf16[1,384,2048]{2,1,0:T(8,128)(2,1)S(1)} %copy-done.6, bf16[2304,2,2048]{2,0,1:T(8,128)(2,1)} %bitcast.68), kind=kOutput, calls=%fused_computation.16 | convolution fusion | flops 3635380224 | bytes 21626880 | tf_op jit(solution)/shard_map/dot_general | solution.py:20
  438.8 0.0 copy-start.8
  438.8 0.0 copy-start.9
  438.8 1.2 copy-done.8
  440.0 0.6 copy-done.9
  440.6 11.3 %fusion.9 = bf16[1,2048,768]{2,1,0:T(8,128)(2,1)} fusion(bf16[2304,2,2048]{2,0,1:T(8,128)(2,1)} %bitcast.69, bf16[2304,384]{0,1:T(8,128)(2,1)S(1)} %get-tuple-element.14, bf16[2304,384]{0,1:T(8,128)(2,1)S(1)} %get-tuple-element.13), kind=kOutput, calls=%fused_computation.22 | convolution fusion | flops 7256408064 | bytes 16121856 | tf_op jit(solution)/shard_map/dot_general | solution.py:26
  451.9 0.0 reduce-scatter.3.cloned.1.call-update
  451.9 12.7 %convolution_convert_fusion = bf16[2304,2048]{1,0:T(8,128)(2,1)} fusion(bf16[1,2048,768]{2,1,0:T(8,128)(2,1)} %param.14, bf16[2304,384]{0,1:T(8,128)(2,1)} %copy-done.9, bf16[2304,384]{0,1:T(8,128)(2,1)} %copy-done.8), kind=kOutput, calls=%fused_computation.2 | convolution fusion | flops 7259553792 | bytes 16121856 | tf_op jit(solution)/shard_map/dot_general | solution.py:27
  464.6 0.0 copy-start.4
  464.6 8.1 %all-to-all-start.1 = ((bf16[32,72,2048]{2,1,0:T(8,128)(2,1)}), bf16[32,72,2048]{2,1,0:T(8,128)(2,1)}, u32[]{:S(2)}, u32[]{:S(2)}) async-start(bf16[32,72,2048]{2,1,0:T(8,128)(2,1)} %bitcast.70), calls=%async_computation.1 | async-start | bytes 18874368 | tf_op jit(solution)/shard_map/all_to_all | solution.py:86
  472.7 0.0 copy-start.3
  472.7 0.0 all-gather.5.cloned.1.call-start
  472.7 0.0 reduce-scatter.5.cloned.1.call-done
  472.8 0.0 copy-done.4
  472.8 3.1 subtract_convert_fusion.1
  475.9 0.0 all-gather.5.cloned.1.call-update
  475.9 0.3 all-gather.3.cloned.1.call-start
  476.2 20.4 %reduce-scatter.3.cloned.1.call-done = bf16[1,512,768]{2,1,0:T(8,128)(2,1)} async-done(((bf16[1,2048,768]{2,1,0:T(8,128)(2,1)}), bf16[1,512,768]{2,1,0:T(8,128)(2,1)}) %reduce-scatter.3.cloned.1.call-update) | async-done | bytes 786448 | tf_op jit(solution)/shard_map/reduce_scatter | solution.py:99
  496.5 0.0 copy-done.3
  496.5 4.4 subtract_convert_fusion
  501.0 0.0 all-gather.3.cloned.1.call-update
  501.0 24.3 %all-gather.5.cloned.1.call-done = bf16[1,384,2048]{2,1,0:T(8,128)(2,1)} async-done(((bf16[1,384,512]{2,1,0:T(8,128)(2,1)}), bf16[1,384,2048]{2,1,0:T(8,128)(2,1)}) %all-gather.5.cloned.1.call-update) | async-done | bytes 1572880 | tf_op jit(solution)/shard_map/all_gather | solution.py:116
  525.3 94.4 %all-to-all-done.1 = bf16[32,72,2048]{2,1,0:T(8,128)(2,1)} async-done(((bf16[32,72,2048]{2,1,0:T(8,128)(2,1)}), bf16[32,72,2048]{2,1,0:T(8,128)(2,1)}, u32[]{:S(2)}, u32[]{:S(2)}) %all-to-all-start.1) | async-done | bytes 9437216 | tf_op jit(solution)/shard_map/all_to_all | solution.py:86
  619.6 13.7 %gather_fusion = bf16[1024,2048]{1,0:T(8,128)(2,1)} fusion(bf16[2304,2048]{1,0:T(8,128)(2,1)} %bitcast.13, s32[1024]{0:T(1024)S(1)} %broadcast_clamp_fusion), kind=kCustom, calls=%fused_computation | custom fusion | bytes 8392704 | tf_op jit(solution)/shard_map/gather | solution.py:95
  633.3 5.9 bitcast_reduce_fusion
  639.2 3.9 copy.36
  643.1 0.0 copy-done.2
  643.1 1.1 copy.37
  644.3 0.0 copy-done.1
  (9 shorter events, 0.1 us)
Async XLA Ops:
  7.2 13.5 %copy-start = (bf16[128,2048]{1,0:T(8,128)(2,1)S(1)}, bf16[128,2048]{1,0:T(8,128)(2,1)}, u32[]{:S(2)}) copy-start(bf16[128,2048]{1,0:T(8,128)(2,1)} %param.10) | copy-start | bytes 1572868
  7.2 465.6 %reduce-scatter.5.cloned.1.call-start = ((), (), s32[]{:S(2)}) async-start(), calls=%async_computation.6 | async-start | bytes 1966080 | tf_op jit(solution)/shard_map/reduce_scatter | solution.py:102
  398.7 9.5 %copy-start.5 = (bf16[1,2048,768]{2,1,0:T(8,128)(2,1)S(1)}, bf16[1,2048,768]{2,1,0:T(8,128)(2,1)}, u32[]{:S(2)}) copy-start(bf16[1,2048,768]{2,1,0:T(8,128)(2,1)} %param.14) | copy-start | bytes 9437188
  418.2 2.9 copy-start.7
  421.1 9.1 %copy-start.6 = (bf16[1,384,2048]{2,1,0:T(8,128)(2,1)S(1)}, bf16[1,384,2048]{2,1,0:T(8,128)(2,1)}, u32[]{:S(2)}) copy-start(bf16[1,384,2048]{2,1,0:T(8,128)(2,1)} %param.15) | copy-start | bytes 4718596
  430.0 66.6 %reduce-scatter.3.cloned.1.call-start = ((), (), s32[]{:S(2)}) async-start(), calls=%async_computation.4 | async-start | bytes 3932160 | tf_op jit(solution)/shard_map/reduce_scatter | solution.py:99
  438.8 1.2 copy-start.8
  438.8 1.8 copy-start.9
  464.6 8.2 %copy-start.4 = (f32[1,384,512]{2,1,0:T(8,128)S(1)}, f32[1,384,512]{2,1,0:T(8,128)}, u32[]{:S(2)}) copy-start(f32[1,384,512]{2,1,0:T(8,128)} %param.18) | copy-start | bytes 2359300
  464.6 155.0 %all-to-all-start.1 = ((bf16[32,72,2048]{2,1,0:T(8,128)(2,1)}), bf16[32,72,2048]{2,1,0:T(8,128)(2,1)}, u32[]{:S(2)}, u32[]{:S(2)}) async-start(bf16[32,72,2048]{2,1,0:T(8,128)(2,1)} %bitcast.70), calls=%async_computation.1 | async-start | bytes 18874368 | tf_op jit(solution)/shard_map/all_to_all | solution.py:86
  472.7 23.9 %copy-start.3 = (f32[1,512,768]{2,1,0:T(8,128)S(1)}, f32[1,512,768]{2,1,0:T(8,128)}, u32[]{:S(2)}) copy-start(f32[1,512,768]{2,1,0:T(8,128)} %param.16) | copy-start | bytes 4718596
  472.7 52.6 %all-gather.5.cloned.1.call-start = ((), (), s32[]{:S(2)}) async-start(), calls=%async_computation.7 | async-start | bytes 1966080 | tf_op jit(solution)/shard_map/all_gather | solution.py:116
  475.9 163.3 %all-gather.3.cloned.1.call-start = ((), (), s32[]{:S(2)}) async-start(), calls=%async_computation.5 | async-start | bytes 3932160 | tf_op jit(solution)/shard_map/all_gather | solution.py:115
  639.2 3.9 copy-start.2
  639.2 5.1 copy-start.1
Sparse Core Ops, SparseCore 0:
  430.1 25.2 reduce-scatter.4
  458.4 38.0 reduce-scatter.2
  498.8 26.4 all-gather.4
  527.4 39.8 all-gather.2
where the time goes:
time: 653 us; the launch traced here: 651 us
  blocking collectives  213 us (33%)
  local copies, waits for them, and re-layouts  192 us (29%)
  waiting for transfers between devices  139 us (21%)
  matrix products  51.4 us (8%)
  other arithmetic  33.1 us (5%)
  between operations  14 us (2%)
  starting transfers between devices  8.62 us (1%)
    all_to_all x1, blocking collectives, local(): lax.all_to_all(outgoing, 'expert', split_axis=0, concat_axis=0, tiled=True)  213 us
    scatter x1, local copies, waits for them, and re-layouts, local(): jnp.zeros((slot_total, 2, model_width), jnp.bfloat16).at[slot_index]  128 us
    all_to_all x1, waiting for transfers between devices, local(): lax.all_to_all(row_grads.reshape(expert_count, capacity, model_width), 'e...  94.4 us
    all_gather x1, waiting for transfers between devices, local(): lax.all_gather(new_down, 'group', axis=2, tiled=True)  24.3 us
    reduce_scatter x1, waiting for transfers between devices, local(): lax.psum_scatter(grad_pair[None].astype(jnp.bfloat16), 'group', scatter_d...  20.4 us
    another operation x2, local copies, waits for them, and re-layouts, local(): jnp.stack([repeated, scaled], axis=2)  17 us
    gather x1, local copies, waits for them, and re-layouts, local(): returned[slot_index].reshape(local_tokens, top_count, model_width)  13.7 us
  transfers between devices with their start and end apart: 5, of which 3 were waited for; matrix products, arithmetic and copies ran while one was open for 9% of the time, Pallas kernels for 0%

commit v1 on v0

--- a/solution.py
+++ b/solution.py
@@ -39,14 +39,10 @@
     return (updated, first_new, second_new)
 
 
-def slot_layout(expert_ids, expert_count, capacity):
-    flat_ids = expert_ids.reshape(-1)
-    onehot = (flat_ids[:, None] == jnp.arange(expert_count, dtype=jnp.int32)[None, :]).astype(
-        jnp.int32
-    )
-    before = jnp.cumsum(onehot, axis=0) - onehot
-    slot_rank = jnp.sum(before * onehot, axis=1)
-    return flat_ids * capacity + slot_rank
+def exclusive_count(flags):
+    n = flags.shape[-1]
+    earlier = (jnp.arange(n)[:, None] < jnp.arange(n)[None, :]).astype(jnp.bfloat16)
+    return jnp.dot(flags.astype(jnp.bfloat16), earlier, preferred_element_type=jnp.float32)
 
 
 def local(
@@ -62,26 +58,42 @@
     down_second,
 ):
     expert_count = lax.axis_size("expert")
+    me = lax.axis_index("expert")
     local_tokens, model_width = tokens.shape
     top_count = expert_ids.shape[1]
     capacity = min(local_tokens, 9 * local_tokens * top_count // (4 * expert_count))
     slot_total = expert_count * capacity
-    slot_index = slot_layout(expert_ids, expert_count, capacity)
-    scaled = (gate_probs[:, :, None] * cotangent.astype(jnp.float32)[:, None, :]).astype(
-        jnp.bfloat16
+
+    all_tokens = lax.all_gather(tokens, "expert", axis=0)
+    all_cot = lax.all_gather(cotangent, "expert", axis=0)
+    meta = jnp.concatenate([expert_ids.astype(jnp.float32), gate_probs], axis=1)
+    all_meta = lax.all_gather(meta, "expert", axis=0)
+    all_ids = all_meta[..., :top_count].astype(jnp.int32)
+    all_gates = all_meta[..., top_count:]
+
+    match = all_ids == me
+    routed = jnp.any(match, axis=-1).astype(jnp.float32)
+    gate_of = jnp.sum(jnp.where(match, all_gates, 0.0), axis=-1)
+    rank = exclusive_count(routed)
+    slots = jnp.arange(capacity, dtype=jnp.float32)
+    pick = (routed[:, None, :] > 0) & (rank[:, None, :] == slots[None, :, None])
+    pick_b = pick.astype(jnp.bfloat16)
+    inputs = jnp.einsum(
+        "srt,stc->src", pick_b, all_tokens, preferred_element_type=jnp.float32
+    ).astype(jnp.bfloat16)
+    cot_rows = jnp.einsum(
+        "srt,stc->src", pick_b, all_cot, preferred_element_type=jnp.float32
     )
-    repeated = jnp.broadcast_to(tokens[:, None, :], (local_tokens, top_count, model_width))
-    payload = jnp.stack([repeated, scaled], axis=2).reshape(
-        local_tokens * top_count, 2, model_width
-    )
-    outgoing = jnp.zeros((slot_total, 2, model_width), jnp.bfloat16).at[slot_index].set(payload)
-    outgoing = outgoing.reshape(expert_count, capacity, 2, model_width)
-    received = lax.all_to_all(outgoing, "expert", split_axis=0, concat_axis=0, tiled=True)
-    slot_rows = received.reshape(slot_total, 2, model_width)
+    slot_gate = jnp.sum(jnp.where(pick, gate_of[:, None, :], 0.0), axis=-1)
+    scaled = (slot_gate[..., None] * cot_rows).astype(jnp.bfloat16)
+
     weight_pair = gate_up[0]
     weight_down = down_weight[0]
     grad_pair, grad_down, row_grads = expert_backward(
-        slot_rows[:, 0], slot_rows[:, 1], weight_pair, weight_down
+        inputs.reshape(slot_total, model_width),
+        scaled.reshape(slot_total, model_width),
+        weight_pair,
+        weight_down,
     )
     returned = lax.all_to_all(
         row_grads.reshape(expert_count, capacity, model_width),
@@ -90,11 +102,20 @@
         concat_axis=0,
         tiled=True,
     )
-    returned = returned.reshape(slot_total, model_width)
-    token_grad = jnp.sum(
-        returned[slot_index].reshape(local_tokens, top_count, model_width).astype(jnp.float32),
-        axis=1,
+
+    own_match = (
+        expert_ids[:, :, None] == jnp.arange(expert_count, dtype=jnp.int32)[None, None, :]
+    )
+    own_routed = jnp.any(own_match, axis=1).astype(jnp.float32)
+    own_rank = exclusive_count(own_routed.T).T
+    own_pick = (own_routed[:, :, None] > 0) & (
+        own_rank[:, :, None] == slots[None, None, :]
+    )
+    own_pick = own_pick.astype(jnp.bfloat16).reshape(local_tokens, slot_total)
+    token_grad = jnp.dot(
+        own_pick, returned.reshape(slot_total, model_width), preferred_element_type=jnp.float32
     ).astype(jnp.bfloat16)
+
     sum_pair, sum_down = (
         lax.psum_scatter(
             grad_pair[None].astype(jnp.bfloat16), "group", scatter_dimension=1, tiled=True
@@ -119,11 +140,12 @@
 
 
 def solution(mesh):
+    rows = P(("group", "expert"), None)
     placed = (
-        P(("group", "expert"), None),
-        P(("group", "expert"), None),
-        P(("group", "expert"), None),
-        P(("group", "expert"), None),
+        rows,
+        rows,
+        rows,
+        rows,
         P("expert", None, None),
         P("expert", None, None),
         P("expert", "group", None),
@@ -136,7 +158,7 @@
         mesh=mesh,
         in_specs=placed,
         out_specs=(
-            P(("group", "expert"), None),
+            rows,
             P("expert", None, None),
             P("expert", None, None),
             P("expert", "group", None),

time: 653 us -> 398 us (0.61)
  blocking collectives: 213 us -> 24.1 us
  local copies, waits for them, and re-layouts: 192 us -> 6.84 us
  waiting for transfers between devices: 139 us -> 250 us
  matrix products: 51.4 us -> 85.9 us
  other arithmetic: 33.1 us -> 9.41 us
    all_to_all x1 -> x0, blocking collectives: 213 us -> none  [local(): lax.all_to_all(outgoing, 'expert', split_axis=0, concat_axis=0, tiled=True)]
    scatter x1 -> x0, local copies, waits for them, and re-layouts: 128 us -> none  [local(): jnp.zeros((slot_total, 2, model_width), jnp.bfloat16).at[slot_index]]
    all_gather x0 -> x2, waiting for transfers between devices: none -> 111 us  [the longest x1 62.3 us: local(): all_cot = lax.all_gather(cotangent, 'expert', axis=0)]
    dot_general x0 -> x5, matrix products: none -> 30.4 us  [the longest x1 12.2 us: local(): jnp.einsum('srt,stc->src', pick_b, all_cot, preferred_element_type=jnp.fl...]
    all_gather x0 -> x1, blocking collectives: none -> 24.1 us  [local(): all_meta = lax.all_gather(meta, 'expert', axis=0)]
    another operation x4 -> x0, local copies, waits for them, and re-layouts: 17.1 us -> none  [the longest x2 17 us: local(): jnp.stack([repeated, scaled], axis=2)]
    another operation x4 -> x0, other arithmetic: 15.3 us -> none
    gather x1 -> x0, local copies, waits for them, and re-layouts: 13.7 us -> none  [local(): returned[slot_index].reshape(local_tokens, top_count, model_width)]
  transfers between devices with their start and end apart: 5 -> 7, of which waited for: 3 -> 5; matrix products, arithmetic and copies ran while one was open for 9% -> 16% of each run, Pallas kernels for 0% -> 0%
where the time goes in v1:
time: 398 us
  waiting for transfers between devices  250 us (63%)
  matrix products  85.9 us (22%)
  blocking collectives  24.1 us (6%)
  between operations  14.2 us (4%)
  other arithmetic  9.41 us (2%)
  starting transfers between devices  7.68 us (2%)
  local copies, waits for them, and re-layouts  6.84 us (2%)
    all_to_all x1, waiting for transfers between devices, local(): lax.all_to_all(row_grads.reshape(expert_count, capacity, model_width), 'e...  93.6 us
    all_gather x1, waiting for transfers between devices, local(): all_cot = lax.all_gather(cotangent, 'expert', axis=0)  62.3 us
    all_gather x1, waiting for transfers between devices, local(): all_tokens = lax.all_gather(tokens, 'expert', axis=0)  48.6 us
    all_gather x1, waiting for transfers between devices, local(): lax.all_gather(new_down, 'group', axis=2, tiled=True)  24.4 us
    all_gather x1, blocking collectives, local(): all_meta = lax.all_gather(meta, 'expert', axis=0)  24.1 us
    reduce_scatter x1, waiting for transfers between devices, local(): lax.psum_scatter(grad_pair[None].astype(jnp.bfloat16), 'group', scatter_d...  19.2 us
    dot_general x1, matrix products, expert_backward(): jnp.dot(inputs, weight_gate_up, preferred_element_type=jnp.float32)  13.1 us
    dot_general x1, matrix products, local(): jnp.einsum('srt,stc->src', pick_b, all_cot, preferred_element_type=jnp.fl...  12.2 us
  transfers between devices with their start and end apart: 7, of which 5 were waited for; matrix products, arithmetic and copies ran while one was open for 16% of the time, Pallas kernels for 0%

profile of v1, /device:TPU:50, one launch (start us, length us, event | category | flops | bytes accessed | tf_op | source)
XLA Modules:
  0.0 397.9 jit_solution(14849885607599489871)
XLA Ops:
  7.2 0.0 all-gather.14.cloned.1.call-start
  7.2 0.7 all-gather.14.cloned.1.call-update
  7.9 0.0 all-gather.12.cloned.1.call-start
  7.9 0.7 all-gather.12.cloned.1.call-update
  8.6 0.0 reduce-scatter.5.cloned.1.call-start
  8.7 0.7 convert_element_type.81
  9.4 0.7 pad_maximum_fusion.3
  10.1 24.1 %all-gather = f32[4096,16]{0,1:T(8,128)S(1)} all-gather(f32[128,16]{0,1:T(8,128)S(1)} %pad_maximum_fusion.3), channel_id=2, replica_groups=mesh['group'=4,'expert'=32] {'expert'}, dimensions={0}, use_global_device_ids=true | all-gather | bytes 270336 | tf_op jit(solution)/shard_map/all_gather | solution.py:70
  34.2 0.1 copy.18
  34.3 0.1 fusion.28
  34.5 0.7 select_reduce_fusion
  35.1 48.6 %all-gather.14.cloned.1.call-done = bf16[4096,2048]{1,0:T(8,128)(2,1)} async-done(((bf16[128,2048]{1,0:T(8,128)(2,1)}), bf16[4096,2048]{1,0:T(8,128)(2,1)}) %all-gather.14.cloned.1.call-update) | async-done | bytes 16777232 | tf_op jit(solution)/shard_map/all_gather | solution.py:67
  83.7 12.0 %convolution_convert_fusion.1 = bf16[32,72,2048]{2,1,0:T(8,128)(2,1)} fusion(bf16[32,128,2048]{2,1,0:T(8,128)(2,1)} %bitcast.35, f32[32,128]{1,0:T(8,128)S(1)} %fusion.28, pred[32,128]{1,0:T(8,128)(4,1)S(1)} %convert_compare_fusion), kind=kOutput, calls=%fused_computation.2 | convolution fusion | flops 1213267968 | bytes 26234880 | tf_op jit(solution)/shard_map/srt,stc->src/dot_general | solution.py:81
  95.7 62.3 %all-gather.12.cloned.1.call-done = bf16[4096,2048]{1,0:T(8,128)(2,1)} async-done(((bf16[128,2048]{1,0:T(8,128)(2,1)}), bf16[4096,2048]{1,0:T(8,128)(2,1)}) %all-gather.12.cloned.1.call-update) | async-done | bytes 16777232 | tf_op jit(solution)/shard_map/all_gather | solution.py:68
  158.0 0.0 copy-start.4
  158.1 12.2 %multiply_convert_fusion = bf16[32,72,2048]{2,1,0:T(8,128)(2,1)} fusion(f32[32,72]{1,0:T(8,128)S(1)} %select_reduce_fusion, bf16[32,128,2048]{2,1,0:T(8,128)(2,1)} %bitcast.34, f32[32,128]{1,0:T(8,128)S(1)} %fusion.28, pred[32,128]{1,0:T(8,128)(4,1)S(1)} %convert_compare_fusion), kind=kOutput, calls=%fused_computation | convolution fusion | flops 1217986560 | bytes 26244096 | tf_op jit(solution)/shard_map/srt,stc->src/dot_general | solution.py:84
  170.2 0.0 copy-done.4
  170.3 0.0 copy-start
  170.3 13.1 %fusion.2 = f32[2304,768]{0,1:T(8,128)} fusion(bf16[2304,2048]{1,0:T(8,128)(2,1)} %bitcast.38, bf16[1,2048,768]{2,1,0:T(8,128)(2,1)S(1)} %copy-done.4), kind=kOutput, calls=%fused_computation.11 | convolution fusion | flops 7247757312 | bytes 19660800 | tf_op jit(solution)/shard_map/dot_general | solution.py:14
  183.3 0.0 copy-done
  183.3 8.1 %fusion.5 = bf16[1,384,2048]{2,1,0:T(8,128)(2,1)} fusion(bf16[2304,2048]{1,0:T(8,128)(2,1)S(1)} %bitcast.37, f32[2304,768]{0,1:T(8,128)} %fusion.2), kind=kOutput, calls=%fused_computation.15 | convolution fusion | flops 3629973504 | bytes 18087936 | tf_op jit(solution)/shard_map/dot_general | solution.py:25
  191.4 0.0 reduce-scatter.5.cloned.1.call-update
  191.5 0.0 reduce-scatter.3.cloned.1.call-start
  191.5 10.9 %multiply_convert_fusion.3 = (bf16[2304,384]{0,1:T(8,128)(2,1)S(1)}, bf16[2304,384]{0,1:T(8,128)(2,1)S(1)}) fusion(f32[2304,768]{0,1:T(8,128)} %fusion.2, bf16[2304,2048]{1,0:T(8,128)(2,1)} %bitcast.36, bf16[1,384,2048]{2,1,0:T(8,128)(2,1)} %param.15), kind=kOutput, calls=%fused_computation.6 | convolution fusion | flops 3635380224 | bytes 21626880 | tf_op jit(solution)/shard_map/dot_general | solution.py:20
  202.4 0.0 copy-start.6
  202.4 0.0 copy-start.7
  202.4 1.2 copy-done.6
  203.6 0.5 copy-done.7
  204.1 11.3 %fusion.4 = bf16[1,2048,768]{2,1,0:T(8,128)(2,1)} fusion(bf16[2304,2048]{1,0:T(8,128)(2,1)} %bitcast.39, bf16[2304,384]{0,1:T(8,128)(2,1)S(1)} %get-tuple-element.16, bf16[2304,384]{0,1:T(8,128)(2,1)S(1)} %get-tuple-element.15), kind=kOutput, calls=%fused_computation.13 | convolution fusion | flops 7256408064 | bytes 16121856 | tf_op jit(solution)/shard_map/dot_general | solution.py:26
  215.4 0.0 reduce-scatter.3.cloned.1.call-update
  215.4 12.2 %convolution_convert_fusion = bf16[2304,2048]{1,0:T(8,128)(2,1)} fusion(bf16[1,2048,768]{2,1,0:T(8,128)(2,1)S(1)} %copy-done.4, bf16[2304,384]{0,1:T(8,128)(2,1)} %copy-done.7, bf16[2304,384]{0,1:T(8,128)(2,1)} %copy-done.6), kind=kOutput, calls=%fused_computation.1 | convolution fusion | flops 7259553792 | bytes 16121856 | tf_op jit(solution)/shard_map/dot_general | solution.py:27
  227.6 7.2 %all-to-all-start = ((bf16[32,72,2048]{2,1,0:T(8,128)(2,1)}), bf16[32,72,2048]{2,1,0:T(8,128)(2,1)}, u32[]{:S(2)}, u32[]{:S(2)}) async-start(bf16[32,72,2048]{2,1,0:T(8,128)(2,1)} %bitcast.40), calls=%async_computation | async-start | bytes 18874368 | tf_op jit(solution)/shard_map/all_to_all | solution.py:98
  234.8 0.0 copy-start.2
  234.8 0.0 copy-start.3
  234.8 0.0 all-gather.10.cloned.1.call-start
  234.9 0.0 reduce-scatter.5.cloned.1.call-done
  234.9 3.4 subtract_convert_fusion.1
  238.3 0.0 all-gather.10.cloned.1.call-update
  238.3 0.0 copy-start.5
  238.3 0.3 all-gather.8.cloned.1.call-start
  238.6 19.2 %reduce-scatter.3.cloned.1.call-done = bf16[1,512,768]{2,1,0:T(8,128)(2,1)} async-done(((bf16[1,2048,768]{2,1,0:T(8,128)(2,1)}), bf16[1,512,768]{2,1,0:T(8,128)(2,1)}) %reduce-scatter.3.cloned.1.call-update) | async-done | bytes 786448 | tf_op jit(solution)/shard_map/reduce_scatter | solution.py:120
  257.9 0.0 copy-done.2
  257.9 0.0 copy-done.3
  257.9 3.9 subtract_convert_fusion
  261.8 0.0 all-gather.8.cloned.1.call-update
  261.8 0.0 copy-done.5
  261.8 0.1 fusion.29
  262.0 24.4 %all-gather.10.cloned.1.call-done = bf16[1,384,2048]{2,1,0:T(8,128)(2,1)} async-done(((bf16[1,384,512]{2,1,0:T(8,128)(2,1)}), bf16[1,384,2048]{2,1,0:T(8,128)(2,1)}) %all-gather.10.cloned.1.call-update) | async-done | bytes 1572880 | tf_op jit(solution)/shard_map/all_gather | solution.py:137
  286.4 93.6 %all-to-all-done = bf16[32,72,2048]{2,1,0:T(8,128)(2,1)} async-done(((bf16[32,72,2048]{2,1,0:T(8,128)(2,1)}), bf16[32,72,2048]{2,1,0:T(8,128)(2,1)}, u32[]{:S(2)}, u32[]{:S(2)}) %all-to-all-start) | async-done | bytes 9437216 | tf_op jit(solution)/shard_map/all_to_all | solution.py:98
  380.0 6.0 %fusion.6 = bf16[128,2048]{1,0:T(8,128)(2,1)} fusion(bf16[32,72,2048]{2,1,0:T(8,128)(2,1)} %all-to-all-done, f32[128,32]{0,1:T(8,128)S(1)} %fusion.29, pred[128,32]{0,1:T(8,128)(4,1)S(1)} %convert_compare_fusion.1), kind=kOutput, calls=%fused_computation.17 | convolution fusion | flops 1208811520 | bytes 9981952 | tf_op jit(solution)/shard_map/dot_general | solution.py:115
  386.0 0.0 copy-start.1
  386.0 0.0 all-gather.8.cloned.1.call-done
  386.0 3.9 copy.21
  389.9 0.0 copy-done.1
  389.9 1.1 copy.22
  (5 shorter events, 0.1 us)
Async XLA Ops:
  7.2 76.6 %all-gather.14.cloned.1.call-start = ((), (), s32[]{:S(2)}) async-start(), calls=%async_computation.8 | async-start | bytes 17301504 | tf_op jit(solution)/shard_map/all_gather | solution.py:67
  7.9 150.1 %all-gather.12.cloned.1.call-start = ((), (), s32[]{:S(2)}) async-start(), calls=%async_computation.7 | async-start | bytes 17301504 | tf_op jit(solution)/shard_map/all_gather | solution.py:68
  8.6 226.3 %reduce-scatter.5.cloned.1.call-start = ((), (), s32[]{:S(2)}) async-start(), calls=%async_computation.5 | async-start | bytes 1966080 | tf_op jit(solution)/shard_map/reduce_scatter | solution.py:123
  158.0 12.2 %copy-start.4 = (bf16[1,2048,768]{2,1,0:T(8,128)(2,1)S(1)}, bf16[1,2048,768]{2,1,0:T(8,128)(2,1)}, u32[]{:S(2)}) copy-start(bf16[1,2048,768]{2,1,0:T(8,128)(2,1)} %param.14) | copy-start | bytes 9437188
  170.3 13.1 %copy-start = (bf16[32,72,2048]{2,1,0:T(8,128)(2,1)S(1)}, bf16[32,72,2048]{2,1,0:T(8,128)(2,1)}, u32[]{:S(2)}) copy-start(bf16[32,72,2048]{2,1,0:T(8,128)(2,1)} %multiply_convert_fusion) | copy-start | bytes 28311556
  191.5 66.4 %reduce-scatter.3.cloned.1.call-start = ((), (), s32[]{:S(2)}) async-start(), calls=%async_computation.3 | async-start | bytes 3932160 | tf_op jit(solution)/shard_map/reduce_scatter | solution.py:120
  202.4 1.2 copy-start.6
  202.4 1.7 copy-start.7
  227.6 152.4 %all-to-all-start = ((bf16[32,72,2048]{2,1,0:T(8,128)(2,1)}), bf16[32,72,2048]{2,1,0:T(8,128)(2,1)}, u32[]{:S(2)}, u32[]{:S(2)}) async-start(bf16[32,72,2048]{2,1,0:T(8,128)(2,1)} %bitcast.40), calls=%async_computation | async-start | bytes 18874368 | tf_op jit(solution)/shard_map/all_to_all | solution.py:98
  234.8 23.0 %copy-start.2 = (f32[1,512,768]{2,1,0:T(8,128)S(1)}, f32[1,512,768]{2,1,0:T(8,128)}, u32[]{:S(2)}) copy-start(f32[1,512,768]{2,1,0:T(8,128)} %param.16) | copy-start | bytes 4718596
  234.8 23.0 %copy-start.3 = (f32[1,512,768]{2,1,0:T(8,128)S(1)}, f32[1,512,768]{2,1,0:T(8,128)}, u32[]{:S(2)}) copy-start(f32[1,512,768]{2,1,0:T(8,128)} %param.17) | copy-start | bytes 4718596
  234.8 51.6 %all-gather.10.cloned.1.call-start = ((), (), s32[]{:S(2)}) async-start(), calls=%async_computation.6 | async-start | bytes 1966080 | tf_op jit(solution)/shard_map/all_gather | solution.py:137
  238.3 23.5 %copy-start.5 = (s32[128,8]{0,1:T(8,128)S(1)}, s32[128,8]{0,1:T(8,128)}, u32[]{:S(2)}) copy-start(s32[128,8]{0,1:T(8,128)} %param.13) | copy-start | bytes 12292
  238.3 147.7 %all-gather.8.cloned.1.call-start = ((), (), s32[]{:S(2)}) async-start(), calls=%async_computation.4 | async-start | bytes 3932160 | tf_op jit(solution)/shard_map/all_gather | solution.py:136
  386.0 3.9 copy-start.1
Sparse Core Ops, SparseCore 0:
  10.3 73.4 all-gather.13
  86.0 71.9 all-gather.11
  191.6 25.2 reduce-scatter.4
  219.7 38.1 reduce-scatter.2
  259.9 26.4 all-gather.9
  288.5 39.8 all-gather.7

commit v2 on v1

--- a/solution.py
+++ b/solution.py
@@ -95,46 +95,54 @@
         weight_pair,
         weight_down,
     )
-    returned = lax.all_to_all(
+    dense = jnp.einsum(
+        "srt,src->stc",
+        pick_b,
         row_grads.reshape(expert_count, capacity, model_width),
+        preferred_element_type=jnp.float32,
+    ).astype(jnp.bfloat16)
+    token_grad = lax.psum_scatter(
+        dense.reshape(expert_count * local_tokens, model_width),
         "expert",
-        split_axis=0,
-        concat_axis=0,
+        scatter_dimension=0,
         tiled=True,
     )
 
-    own_match = (
-        expert_ids[:, :, None] == jnp.arange(expert_count, dtype=jnp.int32)[None, None, :]
+    groups = lax.axis_size("group")
+    share_rows = model_width // groups
+    hidden_count = grad_down.shape[0]
+    pair_size = share_rows * grad_pair.shape[1]
+    down_size = hidden_count * share_rows
+    pair_parts = grad_pair.astype(jnp.bfloat16).reshape(groups, pair_size)
+    down_parts = (
+        grad_down.astype(jnp.bfloat16)
+        .reshape(hidden_count, groups, share_rows)
+        .transpose(1, 0, 2)
+        .reshape(groups, down_size)
     )
-    own_routed = jnp.any(own_match, axis=1).astype(jnp.float32)
-    own_rank = exclusive_count(own_routed.T).T
-    own_pick = (own_routed[:, :, None] > 0) & (
-        own_rank[:, :, None] == slots[None, None, :]
+    parts = lax.all_to_all(
+        jnp.concatenate([pair_parts, down_parts], axis=1), "group", 0, 0, tiled=True
     )
-    own_pick = own_pick.astype(jnp.bfloat16).reshape(local_tokens, slot_total)
-    token_grad = jnp.dot(
-        own_pick, returned.reshape(slot_total, model_width), preferred_element_type=jnp.float32
-    ).astype(jnp.bfloat16)
-
-    sum_pair, sum_down = (
-        lax.psum_scatter(
-            grad_pair[None].astype(jnp.bfloat16), "group", scatter_dimension=1, tiled=True
-        ).astype(jnp.float32),
-        lax.psum_scatter(
-            grad_down[None].astype(jnp.bfloat16), "group", scatter_dimension=2, tiled=True
-        ).astype(jnp.float32),
-    )
+    summed = jnp.sum(parts.astype(jnp.float32), axis=0)
+    sum_pair = summed[:pair_size].reshape(1, share_rows, grad_pair.shape[1])
+    sum_down = summed[pair_size:].reshape(1, hidden_count, share_rows)
     group_index = lax.axis_index("group")
-    share_rows = model_width // lax.axis_size("group")
     own_pair = lax.dynamic_slice_in_dim(gate_up, group_index * share_rows, share_rows, 1)
     own_down = lax.dynamic_slice_in_dim(down_weight, group_index * share_rows, share_rows, 2)
     new_pair, first_pair, second_pair = adam_update(
         own_pair, sum_pair, gate_up_moment, gate_up_second
     )
     new_down, first_down, second_down = adam_update(own_down, sum_down, down_moment, down_second)
-    full_pair, full_down = (
-        lax.all_gather(new_pair, "group", axis=1, tiled=True),
-        lax.all_gather(new_down, "group", axis=2, tiled=True),
+    packed = jnp.concatenate([new_pair.reshape(1, pair_size), new_down.reshape(1, down_size)], axis=1)
+    shared = lax.all_to_all(
+        jnp.broadcast_to(packed, (groups, pair_size + down_size)), "group", 0, 0, tiled=True
+    )
+    full_pair = shared[:, :pair_size].reshape(1, model_width, grad_pair.shape[1])
+    full_down = (
+        shared[:, pair_size:]
+        .reshape(groups, hidden_count, share_rows)
+        .transpose(1, 0, 2)
+        .reshape(1, hidden_count, model_width)
     )
     return (token_grad, full_pair, full_down, first_pair, second_pair, first_down, second_down)
 

time: 398 us -> 594 us (1.49); the launches traced: 398 us -> 584 us
  other arithmetic: 9.41 us -> 155 us
  waiting for transfers between devices: 250 us -> 166 us
  local copies, waits for them, and re-layouts: 6.84 us -> 73.6 us
  blocking collectives: 24.1 us -> 84.6 us
    all_to_all x0 -> x1, blocking collectives: none -> 60.5 us  [local(): lax.all_to_all(jnp.broadcast_to(packed, (groups, pair_size + down_size)),...]
    all_to_all x0 -> x2, other arithmetic: none -> 45.2 us  [local(): lax.all_to_all(jnp.concatenate([pair_parts, down_parts], axis=1), 'group'...]
    concatenate x0 -> x1, other arithmetic: none -> 41.1 us  [local(): jnp.concatenate([new_pair.reshape(1, pair_size), new_down.reshape(1, down...]
    all_to_all x1, waiting for transfers between devices: 93.6 us -> 53.7 us  [local(): lax.all_to_all(jnp.concatenate([pair_parts, down_parts], axis=1), 'group'...]
    unnamed x19 -> x23, local copies, waits for them, and re-layouts: 6.84 us -> 46.5 us
    broadcast_in_dim x0 -> x1, other arithmetic: none -> 32.8 us  [local(): jnp.broadcast_to(packed, (groups, pair_size + down_size))]
    reduce_sum x0 -> x1, other arithmetic: none -> 25.5 us  [local(): summed = jnp.sum(parts.astype(jnp.float32), axis=0)]
    all_gather x2 -> x0, waiting for transfers between devices: 24.4 us -> none  [the longest x1 24.4 us: local(): lax.all_gather(new_down, 'group', axis=2, tiled=True)]
  transfers between devices with their start and end apart: 7 -> 4, of which waited for: 5 -> 3; matrix products, arithmetic and copies ran while one was open for 16% -> 40% of each run, Pallas kernels for 0% -> 0%
where the time goes in v2:
time: 594 us; the launch traced here: 584 us
  waiting for transfers between devices  166 us (28%)
  other arithmetic  155 us (26%)
  matrix products  85 us (14%)
  blocking collectives  84.6 us (14%)
  local copies, waits for them, and re-layouts  73.6 us (12%)
  between operations  14.4 us (2%)
    all_gather x1, waiting for transfers between devices, local(): all_cot = lax.all_gather(cotangent, 'expert', axis=0)  62.4 us
    all_to_all x1, blocking collectives, local(): lax.all_to_all(jnp.broadcast_to(packed, (groups, pair_size + down_size)),...  60.5 us
    all_to_all x1, waiting for transfers between devices, local(): lax.all_to_all(jnp.concatenate([pair_parts, down_parts], axis=1), 'group'...  53.7 us
    all_gather x1, waiting for transfers between devices, local(): all_tokens = lax.all_gather(tokens, 'expert', axis=0)  48.6 us
    unnamed x23, local copies, waits for them, and re-layouts  46.5 us
    all_to_all x2, other arithmetic, local(): lax.all_to_all(jnp.concatenate([pair_parts, down_parts], axis=1), 'group'...  45.2 us
    concatenate x1, other arithmetic, local(): jnp.concatenate([new_pair.reshape(1, pair_size), new_down.reshape(1, down...  41.1 us
    broadcast_in_dim x1, other arithmetic, local(): jnp.broadcast_to(packed, (groups, pair_size + down_size))  32.8 us
  transfers between devices with their start and end apart: 4, of which 3 were waited for; matrix products, arithmetic and copies ran while one was open for 40% of the time, Pallas kernels for 0%

profile of v2, /device:TPU:50, one launch (start us, length us, event | category | flops | bytes accessed | tf_op | source)
XLA Modules:
  0.0 584.3 jit_solution(1862852828731721700)
XLA Ops:
  7.2 0.0 all-gather.8.cloned.1.call-start
  7.2 0.7 all-gather.8.cloned.1.call-update
  7.9 0.0 all-gather.6.cloned.1.call-start
  7.9 0.7 all-gather.6.cloned.1.call-update
  8.6 0.0 reduce-scatter.2.cloned.1.call-start
  8.7 0.7 convert_element_type.56
  9.4 0.7 pad_maximum_fusion.3
  10.1 24.1 %all-gather = f32[4096,16]{0,1:T(8,128)S(1)} all-gather(f32[128,16]{0,1:T(8,128)S(1)} %pad_maximum_fusion.3), channel_id=2, replica_groups=mesh['group'=4,'expert'=32] {'expert'}, dimensions={0}, use_global_device_ids=true | all-gather | bytes 270336 | tf_op jit(solution)/shard_map/all_gather | solution.py:70
  34.2 0.1 copy.21
  34.3 0.1 fusion.25
  34.5 0.7 select_reduce_fusion
  35.1 48.6 %all-gather.8.cloned.1.call-done = bf16[4096,2048]{1,0:T(8,128)(2,1)} async-done(((bf16[128,2048]{1,0:T(8,128)(2,1)}), bf16[4096,2048]{1,0:T(8,128)(2,1)}) %all-gather.8.cloned.1.call-update) | async-done | bytes 16777232 | tf_op jit(solution)/shard_map/all_gather | solution.py:67
  83.7 11.9 %convolution_convert_fusion.2 = bf16[32,72,2048]{2,1,0:T(8,128)(2,1)} fusion(bf16[32,128,2048]{2,1,0:T(8,128)(2,1)} %bitcast.66, f32[32,128]{1,0:T(8,128)S(1)} %fusion.25, pred[32,128]{1,0:T(8,128)(4,1)S(1)} %convert_compare_fusion), kind=kOutput, calls=%fused_computation.4 | convolution fusion | flops 1213267968 | bytes 26234880 | tf_op jit(solution)/shard_map/srt,stc->src/dot_general | solution.py:81
  95.7 62.4 %all-gather.6.cloned.1.call-done = bf16[4096,2048]{1,0:T(8,128)(2,1)} async-done(((bf16[128,2048]{1,0:T(8,128)(2,1)}), bf16[4096,2048]{1,0:T(8,128)(2,1)}) %all-gather.6.cloned.1.call-update) | async-done | bytes 16777232 | tf_op jit(solution)/shard_map/all_gather | solution.py:68
  158.0 12.0 %multiply_convert_fusion = bf16[32,72,2048]{2,1,0:T(8,128)(2,1)} fusion(f32[32,72]{1,0:T(8,128)S(1)} %select_reduce_fusion, bf16[32,128,2048]{2,1,0:T(8,128)(2,1)} %bitcast.65, f32[32,128]{1,0:T(8,128)S(1)} %fusion.25, pred[32,128]{1,0:T(8,128)(4,1)S(1)} %convert_compare_fusion), kind=kOutput, calls=%fused_computation | convolution fusion | flops 1217986560 | bytes 26244096 | tf_op jit(solution)/shard_map/srt,stc->src/dot_general | solution.py:84
  170.0 0.0 copy-start
  170.1 14.0 %fusion.2 = f32[2304,768]{0,1:T(8,128)} fusion(bf16[2304,2048]{1,0:T(8,128)(2,1)} %bitcast.69, bf16[1,2048,768]{2,1,0:T(8,128)(2,1)} %param.14), kind=kOutput, calls=%fused_computation.15 | convolution fusion | flops 7247757312 | bytes 19660800 | tf_op jit(solution)/shard_map/dot_general | solution.py:14
  184.1 0.0 copy-done
  184.1 0.0 slice-start.1
  184.1 8.2 %convolution_convert_fusion.4 = bf16[384,2048]{1,0:T(8,128)(2,1)} fusion(bf16[2304,2048]{1,0:T(8,128)(2,1)S(1)} %bitcast.67, f32[2304,768]{0,1:T(8,128)} %fusion.2), kind=kOutput, calls=%fused_computation.17 | convolution fusion | flops 3629973504 | bytes 18087936 | tf_op jit(solution)/shard_map/dot_general | solution.py:25
  192.3 0.0 copy-done.3
  192.3 9.4 %multiply_convert_fusion.3 = (bf16[2304,384]{0,1:T(8,128)(2,1)S(1)}, bf16[2304,384]{0,1:T(8,128)(2,1)S(1)}) fusion(f32[2304,768]{0,1:T(8,128)} %fusion.2, bf16[2304,2048]{1,0:T(8,128)(2,1)S(1)} %bitcast.68, bf16[1,384,2048]{2,1,0:T(8,128)(2,1)S(1)} %copy-done.3), kind=kOutput, calls=%fused_computation.10 | convolution fusion | flops 3635380224 | bytes 21626880 | tf_op jit(solution)/shard_map/dot_general | solution.py:20
  201.7 0.0 slice-done
  201.7 0.0 slice-done.1
  201.7 0.0 slice-done.2
  201.8 0.0 copy-start.2
  201.8 9.1 %convolution_convert_fusion.3 = bf16[2048,768]{1,0:T(8,128)(2,1)} fusion(bf16[2304,2048]{1,0:T(8,128)(2,1)S(1)} %bitcast.72, bf16[2304,384]{0,1:T(8,128)(2,1)S(1)} %get-tuple-element.16, bf16[2304,384]{0,1:T(8,128)(2,1)S(1)} %get-tuple-element.15), kind=kOutput, calls=%fused_computation.13 | convolution fusion | flops 7256408064 | bytes 16121856 | tf_op jit(solution)/shard_map/dot_general | solution.py:26
  210.9 0.0 copy-done.2
  210.9 9.7 %convolution_convert_fusion.1 = bf16[2304,2048]{1,0:T(8,128)(2,1)} fusion(bf16[1,2048,768]{2,1,0:T(8,128)(2,1)S(1)} %copy-done.2, bf16[2304,384]{0,1:T(8,128)(2,1)S(1)} %get-tuple-element.16, bf16[2304,384]{0,1:T(8,128)(2,1)S(1)} %get-tuple-element.15), kind=kOutput, calls=%fused_computation.2 | convolution fusion | flops 7259553792 | bytes 16121856 | tf_op jit(solution)/shard_map/dot_general | solution.py:27
  220.6 4.3 reshape.109
  224.9 3.9 reshape.110
  228.8 10.5 %convolution_convert_fusion = bf16[32,128,2048]{2,1,0:T(8,128)(2,1)} fusion(bf16[32,72,2048]{2,1,0:T(8,128)(2,1)} %bitcast.73, f32[32,128]{1,0:T(8,128)S(1)} %fusion.25, pred[32,128]{1,0:T(8,128)(4,1)S(1)} %convert_compare_fusion), kind=kOutput, calls=%fused_computation.1 | convolution fusion | flops 1216937984 | bytes 26234880 | tf_op jit(solution)/shard_map/srt,src->stc/dot_general | solution.py:98
  239.3 0.0 reduce-scatter.2.cloned.1.call-update
  239.3 19.6 %maximum_bitcast_fusion = bf16[4,1,589824]{2,0,1:T(4,128)(2,1)} fusion(bf16[4,196608]{1,0:T(4,128)(2,1)} %bitcast.76, bf16[4,393216]{1,0:T(4,128)(2,1)S(1)} %reshape.109), kind=kLoop, calls=%fused_computation.5 | loop fusion | flops 9437184 | bytes 9437184 | tf_op jit(solution)/shard_map/all_to_all | solution.py:123
  258.9 0.5 broadcast.52
  259.5 25.6 %reduce.3 = bf16[4,589824]{1,0:T(4,128)(2,1)} reduce(bf16[4,1,589824]{2,0,1:T(4,128)(2,1)} %maximum_bitcast_fusion, bf16[]{:T(256)} %broadcast.52), dimensions={1}, to_apply=%copy.18.reduce_sub_computation | reduce | bytes 9437186 | tf_op jit(solution)/shard_map/all_to_all | solution.py:123
  285.0 9.2 %reshape.121 = bf16[4,2,294912]{2,1,0:T(2,128)(2,1)} reshape(bf16[4,589824]{1,0:T(4,128)(2,1)} %reduce.3) | data formatting | bytes 9437184
  294.2 5.6 all-to-all-start
  299.9 53.7 %all-to-all-done = bf16[4,2,294912]{2,1,0:T(2,128)(2,1)} async-done(((bf16[4,2,294912]{2,1,0:T(2,128)(2,1)}), bf16[4,2,294912]{2,1,0:T(2,128)(2,1)}, u32[]{:S(2)}, u32[]{:S(2)}) %all-to-all-start) | async-done | bytes 4718624 | tf_op jit(solution)/shard_map/all_to_all | solution.py:123
  353.6 8.1 %reshape.122 = bf16[4,1,589824]{2,1,0:T(2,128)(2,1)} reshape(bf16[4,2,294912]{2,1,0:T(2,128)(2,1)} %all-to-all-done) | data formatting | bytes 9437184
  361.7 25.5 %convert_reduce_fusion = f32[589824]{0:T(1024)S(1)} fusion(bf16[4,1,589824]{2,1,0:T(2,128)(2,1)} %reshape.122), kind=kLoop, calls=%fused_computation.3 | loop fusion | flops 4128768 | bytes 7077888 | tf_op jit(solution)/shard_map/reduce_sum | solution.py:126
  387.3 0.1 slice.66
  387.4 0.9 slice.67
  388.3 0.3 slice.57
  388.6 0.0 copy-start.1
  388.6 4.9 fusion.14
  393.5 1.2 copy.22
  394.7 0.0 copy-done.1
  394.7 0.1 slice.59
  394.9 3.2 fusion.22
  398.0 0.6 copy.23
  398.6 41.1 %maximum_reduce_fusion = bf16[589824]{0:T(1024)(128)(2,1)S(1)} fusion(bf16[1,196608]{1,0:T(2,128)(2,1)S(1)} %bitcast.80, bf16[1,393216]{1,0:T(2,128)(2,1)S(1)} %bitcast.77), kind=kLoop, calls=%fused_computation.19 | loop fusion | flops 2359296 | bytes 2359296 | tf_op jit(solution)/shard_map/concatenate | solution.py:136
  439.7 6.1 %broadcast_in_dim.31 = bf16[4,1,589824]{2,1,0:T(2,128)(2,1)} broadcast(bf16[589824]{0:T(1024)(128)(2,1)S(1)} %maximum_reduce_fusion), dimensions={2} | broadcast | bytes 5898240 | tf_op jit(solution)/shard_map/broadcast_in_dim | solution.py:138
  445.8 32.8 %reduce.4 = bf16[4,589824]{1,0:T(4,128)(2,1)} reduce(bf16[4,1,589824]{2,1,0:T(2,128)(2,1)} %broadcast_in_dim.31, bf16[]{:T(256)} %broadcast.52), dimensions={1}, to_apply=%broadcast_in_dim.31.reduce_sub_computation | reduce | bytes 9437186 | tf_op jit(solution)/shard_map/broadcast_in_dim | solution.py:138
  478.6 9.2 %reshape.123 = bf16[4,2,294912]{2,1,0:T(2,128)(2,1)} reshape(bf16[4,589824]{1,0:T(4,128)(2,1)} %reduce.4) | data formatting | bytes 9437184
  487.8 60.5 %all_to_all.18 = bf16[4,2,294912]{2,1,0:T(2,128)(2,1)} all-to-all(bf16[4,2,294912]{2,1,0:T(2,128)(2,1)} %reshape.123), channel_id=1, replica_groups=mesh['group'=4,'expert'=32] {'group'}, dimensions={0} | all-to-all | bytes 9437184 | tf_op jit(solution)/shard_map/all_to_all | solution.py:137
  548.3 8.1 %reshape.124 = bf16[4,1,589824]{2,1,0:T(2,128)(2,1)} reshape(bf16[4,2,294912]{2,1,0:T(2,128)(2,1)} %all_to_all.18) | data formatting | bytes 9437184
  556.4 8.2 %copy.27 = bf16[4,1,589824]{2,0,1:T(4,128)(2,1)S(1)} copy(bf16[4,1,589824]{2,1,0:T(2,128)(2,1)} %reshape.124) | data formatting | bytes 9437184
  564.7 1.1 slice.68
  565.8 1.5 slice.69
  567.3 4.6 reshape.114
  571.9 1.7 copy.28
  573.6 1.2 copy.19
  574.9 2.4 reshape.116
  (8 shorter events, 0.1 us)
Async XLA Ops:
  7.2 76.6 %all-gather.8.cloned.1.call-start = ((), (), s32[]{:S(2)}) async-start(), calls=%async_computation.5 | async-start | bytes 17301504 | tf_op jit(solution)/shard_map/all_gather | solution.py:67
  7.9 150.1 %all-gather.6.cloned.1.call-start = ((), (), s32[]{:S(2)}) async-start(), calls=%async_computation.4 | async-start | bytes 17301504 | tf_op jit(solution)/shard_map/all_gather | solution.py:68
  8.6 568.6 %reduce-scatter.2.cloned.1.call-start = ((), (), s32[]{:S(2)}) async-start(), calls=%async_computation.3 | async-start | bytes 17301504 | tf_op jit(solution)/shard_map/reduce_scatter | solution.py:104
  170.0 14.0 %copy-start = (bf16[32,72,2048]{2,1,0:T(8,128)(2,1)S(1)}, bf16[32,72,2048]{2,1,0:T(8,128)(2,1)}, u32[]{:S(2)}) copy-start(bf16[32,72,2048]{2,1,0:T(8,128)(2,1)} %multiply_convert_fusion) | copy-start | bytes 28311556
  184.1 8.3 %copy-start.3 = (bf16[1,384,2048]{2,1,0:T(8,128)(2,1)S(1)}, bf16[1,384,2048]{2,1,0:T(8,128)(2,1)}, u32[]{:S(2)}) copy-start(bf16[1,384,2048]{2,1,0:T(8,128)(2,1)} %param.15) | copy-start | bytes 4718596
  184.1 17.7 %slice-start = ((s8[9437184]{0:T(1024)(128)(4,1)}), s8[4194304]{0:T(1024)(128)(4,1)S(1)}, s32[]{:S(2)}) async-start(s8[9437184]{0:T(1024)(128)(4,1)} %bitcast.70), calls=%async_computation.6 | async-start | bytes 8388608
  184.1 17.7 %slice-start.1 = ((s8[9437184]{0:T(1024)(128)(4,1)}), s8[4194304]{0:T(1024)(128)(4,1)S(1)}, s32[]{:S(2)}) async-start(s8[9437184]{0:T(1024)(128)(4,1)} %bitcast.70), calls=%async_computation.7 | async-start | bytes 8388608
  192.3 9.4 %slice-start.2 = ((s8[9437184]{0:T(1024)(128)(4,1)}), s8[1048576]{0:T(1024)(128)(4,1)S(1)}, s32[]{:S(2)}) async-start(s8[9437184]{0:T(1024)(128)(4,1)} %bitcast.70), calls=%async_computation.8 | async-start | bytes 2097152
  201.8 9.1 %copy-start.2 = (bf16[1,2048,768]{2,1,0:T(8,128)(2,1)S(1)}, bf16[1,2048,768]{2,1,0:T(8,128)(2,1)}, u32[]{:S(2)}) copy-start(bf16[1,2048,768]{2,1,0:T(8,128)(2,1)} %param.14) | copy-start | bytes 9437188
  294.2 59.4 %all-to-all-start = ((bf16[4,2,294912]{2,1,0:T(2,128)(2,1)}), bf16[4,2,294912]{2,1,0:T(2,128)(2,1)}, u32[]{:S(2)}, u32[]{:S(2)}) async-start(bf16[4,2,294912]{2,1,0:T(2,128)(2,1)} %reshape.121), calls=%async_computation.1 | async-start | bytes 9437184 | tf_op jit(solution)/shard_map/all_to_all | solution.py:123
  388.6 6.1 %copy-start.1 = (f32[196608]{0:T(1024)S(1)}, f32[196608]{0:T(1024)}, u32[]{:S(2)}) copy-start(f32[196608]{0:T(1024)} %slice.67) | copy-start | bytes 2359300
Sparse Core Ops, SparseCore 0:
  10.3 73.4 all-gather.7
  86.0 71.9 all-gather.5
  239.4 114.7 reduce-scatter.1

commit v3 on v1

--- a/solution.py
+++ b/solution.py
@@ -19,8 +19,11 @@
     hidden_act = (activated * up_part).astype(jnp.bfloat16)
     hidden_grad = jnp.dot(scaled_grad, weight_down.T, preferred_element_type=jnp.float32)
     slope = sigmoid_gate * (1.0 + gate_part * (1.0 - sigmoid_gate))
+    hidden_act, up_slope, activated = lax.optimization_barrier(
+        (hidden_act, up_part * slope, activated)
+    )
     pair_grad = jnp.concatenate(
-        [hidden_grad * up_part * slope, hidden_grad * activated], axis=1
+        [hidden_grad * up_slope, hidden_grad * activated], axis=1
     ).astype(jnp.bfloat16)
     down_grad = jnp.dot(hidden_act.T, scaled_grad, preferred_element_type=jnp.float32)
     gate_up_grad = jnp.dot(inputs.T, pair_grad, preferred_element_type=jnp.float32)

time: 398 us -> 386 us (0.970)
  waiting for transfers between devices: 250 us -> 235 us
    all_gather x1, waiting for transfers between devices: 62.3 us -> 48.2 us  [local(): all_cot = lax.all_gather(cotangent, 'expert', axis=0)]
    unnamed x19 -> x21, local copies, waits for them, and re-layouts: 6.84 us -> 8.78 us
  transfers between devices with their start and end apart: 7 -> 7, of which waited for: 5 -> 5; matrix products, arithmetic and copies ran while one was open for 16% -> 19% of each run, Pallas kernels for 0% -> 0%
where the time goes in v3:
time: 386 us
  waiting for transfers between devices  235 us (61%)
  matrix products  82.6 us (21%)
  blocking collectives  24.1 us (6%)
  between operations  14.3 us (4%)
  other arithmetic  13.3 us (3%)
  local copies, waits for them, and re-layouts  8.78 us (2%)
  starting transfers between devices  7.95 us (2%)
    all_to_all x1, waiting for transfers between devices, local(): lax.all_to_all(row_grads.reshape(expert_count, capacity, model_width), 'e...  93.9 us
    all_gather x1, waiting for transfers between devices, local(): all_cot = lax.all_gather(cotangent, 'expert', axis=0)  48.2 us
    all_gather x1, waiting for transfers between devices, local(): all_tokens = lax.all_gather(tokens, 'expert', axis=0)  48 us
    all_gather x1, waiting for transfers between devices, local(): lax.all_gather(new_down, 'group', axis=2, tiled=True)  24.4 us
    all_gather x1, blocking collectives, local(): all_meta = lax.all_gather(meta, 'expert', axis=0)  24.1 us
    reduce_scatter x1, waiting for transfers between devices, local(): lax.psum_scatter(grad_pair[None].astype(jnp.bfloat16), 'group', scatter_d...  18.9 us
    dot_general x1, matrix products, expert_backward(): jnp.dot(pair_grad, weight_gate_up.T, preferred_element_type=jnp.float32)  12.1 us
    dot_general x1, matrix products, local(): jnp.einsum('srt,stc->src', pick_b, all_tokens, preferred_element_type=jnp...  12.1 us
  transfers between devices with their start and end apart: 7, of which 5 were waited for; matrix products, arithmetic and copies ran while one was open for 19% of the time, Pallas kernels for 0%

profile of v3, /device:TPU:50, one launch (start us, length us, event | category | flops | bytes accessed | tf_op | source)
XLA Modules:
  0.0 386.0 jit_solution(4009859496395451279)
XLA Ops:
  7.2 0.0 all-gather.14.cloned.1.call-start
  7.2 0.7 all-gather.14.cloned.1.call-update
  7.9 0.0 all-gather.12.cloned.1.call-start
  7.9 0.7 all-gather.12.cloned.1.call-update
  8.6 0.0 reduce-scatter.5.cloned.1.call-start
  8.7 0.7 convert_element_type.81
  9.4 0.7 pad_maximum_fusion.3
  10.1 24.1 %all-gather = f32[4096,16]{0,1:T(8,128)S(1)} all-gather(f32[128,16]{0,1:T(8,128)S(1)} %pad_maximum_fusion.3), channel_id=2, replica_groups=mesh['group'=4,'expert'=32] {'expert'}, dimensions={0}, use_global_device_ids=true | all-gather | bytes 270336 | tf_op jit(solution)/shard_map/all_gather | solution.py:73
  34.2 0.1 copy.23
  34.3 0.0 copy-start.3
  34.3 0.1 fusion.27
  34.5 1.3 select_reduce_fusion
  35.7 48.0 %all-gather.14.cloned.1.call-done = bf16[4096,2048]{1,0:T(8,128)(2,1)} async-done(((bf16[128,2048]{1,0:T(8,128)(2,1)}), bf16[4096,2048]{1,0:T(8,128)(2,1)}) %all-gather.14.cloned.1.call-update) | async-done | bytes 16777232 | tf_op jit(solution)/shard_map/all_gather | solution.py:70
  83.7 0.0 copy-start.4
  83.8 12.1 %convolution_convert_fusion.1 = bf16[32,72,2048]{2,1,0:T(8,128)(2,1)} fusion(bf16[32,128,2048]{2,1,0:T(8,128)(2,1)} %bitcast.36, f32[32,128]{1,0:T(8,128)S(1)} %fusion.27, pred[32,128]{1,0:T(8,128)(4,1)S(1)} %convert_compare_fusion), kind=kOutput, calls=%fused_computation.2 | convolution fusion | flops 1213267968 | bytes 26234880 | tf_op jit(solution)/shard_map/srt,stc->src/dot_general | solution.py:84
  95.9 0.0 copy-done.3
  95.9 0.0 copy-done.4
  95.9 10.6 %fusion.2 = f32[2304,768]{0,1:T(8,128)S(1)} fusion(bf16[2304,2048]{1,0:T(8,128)(2,1)} %bitcast.39, bf16[1,2048,768]{2,1,0:T(8,128)(2,1)S(1)} %copy-done.4), kind=kOutput, calls=%fused_computation.12 | convolution fusion | flops 7247757312 | bytes 19660800 | tf_op jit(solution)/shard_map/dot_general | solution.py:14
  106.5 3.3 fusion
  109.8 48.2 %all-gather.12.cloned.1.call-done = bf16[4096,2048]{1,0:T(8,128)(2,1)} async-done(((bf16[128,2048]{1,0:T(8,128)(2,1)}), bf16[4096,2048]{1,0:T(8,128)(2,1)}) %all-gather.12.cloned.1.call-update) | async-done | bytes 16777232 | tf_op jit(solution)/shard_map/all_gather | solution.py:71
  158.0 12.0 %multiply_convert_fusion = bf16[32,72,2048]{2,1,0:T(8,128)(2,1)} fusion(f32[32,72]{1,0:T(8,128)} %select_reduce_fusion, bf16[32,128,2048]{2,1,0:T(8,128)(2,1)} %bitcast.35, f32[32,128]{1,0:T(8,128)S(1)} %fusion.27, pred[32,128]{1,0:T(8,128)(4,1)} %copy-done.3), kind=kOutput, calls=%fused_computation | convolution fusion | flops 1217986560 | bytes 26244096 | tf_op jit(solution)/shard_map/srt,stc->src/dot_general | solution.py:87
  170.1 9.2 %fusion.5 = bf16[1,384,2048]{2,1,0:T(8,128)(2,1)} fusion(bf16[2304,384]{0,1:T(8,128)(2,1)} %get-tuple-element.12, bf16[2304,2048]{1,0:T(8,128)(2,1)} %bitcast.37), kind=kOutput, calls=%fused_computation.16 | convolution fusion | flops 3624665088 | bytes 12779520 | tf_op jit(solution)/shard_map/dot_general | solution.py:28
  179.3 0.0 reduce-scatter.5.cloned.1.call-update
  179.3 0.3 reduce-scatter.3.cloned.1.call-start
  179.6 9.0 %multiply_convert_fusion.2 = (bf16[2304,384]{0,1:T(8,128)(2,1)S(1)}, bf16[2304,384]{0,1:T(8,128)(2,1)S(1)}) fusion(f32[2304,384]{0,1:T(8,128)} %get-tuple-element.10, f32[2304,384]{0,1:T(8,128)S(1)} %get-tuple-element.11, bf16[2304,2048]{1,0:T(8,128)(2,1)} %bitcast.38, bf16[1,384,2048]{2,1,0:T(8,128)(2,1)} %param.15), kind=kOutput, calls=%fused_computation.5 | convolution fusion | flops 3627417600 | bytes 21626880 | tf_op jit(solution)/shard_map/dot_general | solution.py:20
  188.6 0.0 copy-start.7
  188.6 0.0 copy-start.8
  188.6 1.3 copy-done.7
  189.9 0.5 copy-done.8
  190.4 11.2 %fusion.4 = bf16[1,2048,768]{2,1,0:T(8,128)(2,1)} fusion(bf16[2304,2048]{1,0:T(8,128)(2,1)} %bitcast.40, bf16[2304,384]{0,1:T(8,128)(2,1)S(1)} %get-tuple-element.25, bf16[2304,384]{0,1:T(8,128)(2,1)S(1)} %get-tuple-element.24), kind=kOutput, calls=%fused_computation.14 | convolution fusion | flops 7256408064 | bytes 16121856 | tf_op jit(solution)/shard_map/dot_general | solution.py:29
  201.6 0.0 copy-start.5
  201.6 0.0 reduce-scatter.3.cloned.1.call-update
  201.7 1.9 copy-done.5
  203.6 12.1 %convolution_convert_fusion = bf16[2304,2048]{1,0:T(8,128)(2,1)} fusion(bf16[1,2048,768]{2,1,0:T(8,128)(2,1)S(1)} %copy-done.5, bf16[2304,384]{0,1:T(8,128)(2,1)} %copy-done.8, bf16[2304,384]{0,1:T(8,128)(2,1)} %copy-done.7), kind=kOutput, calls=%fused_computation.1 | convolution fusion | flops 7259553792 | bytes 16121856 | tf_op jit(solution)/shard_map/dot_general | solution.py:30
  215.7 7.2 %all-to-all-start = ((bf16[32,72,2048]{2,1,0:T(8,128)(2,1)}), bf16[32,72,2048]{2,1,0:T(8,128)(2,1)}, u32[]{:S(2)}, u32[]{:S(2)}) async-start(bf16[32,72,2048]{2,1,0:T(8,128)(2,1)} %bitcast.41), calls=%async_computation | async-start | bytes 18874368 | tf_op jit(solution)/shard_map/all_to_all | solution.py:101
  222.9 0.0 copy-start.1
  222.9 0.0 copy-start.2
  222.9 0.3 all-gather.10.cloned.1.call-start
  223.3 0.0 reduce-scatter.5.cloned.1.call-done
  223.3 3.4 subtract_convert_fusion.1
  226.7 0.0 all-gather.10.cloned.1.call-update
  226.7 0.0 copy-start.6
  226.7 0.0 all-gather.8.cloned.1.call-start
  226.8 18.9 %reduce-scatter.3.cloned.1.call-done = bf16[1,512,768]{2,1,0:T(8,128)(2,1)} async-done(((bf16[1,2048,768]{2,1,0:T(8,128)(2,1)}), bf16[1,512,768]{2,1,0:T(8,128)(2,1)}) %reduce-scatter.3.cloned.1.call-update) | async-done | bytes 786448 | tf_op jit(solution)/shard_map/reduce_scatter | solution.py:123
  245.7 0.0 copy-done.1
  245.7 0.0 copy-done.2
  245.7 3.9 %subtract_convert_fusion = (bf16[1,512,768]{2,1,0:T(8,128)(2,1)}, f32[1,512,768]{2,1,0:T(8,128)}, f32[1,512,768]{2,1,0:T(8,128)}) fusion(bf16[1,2048,768]{2,1,0:T(8,128)(2,1)} %param.14, s32[]{:T(128)S(6)} %select_n.14, bf16[1,512,768]{2,1,0:T(8,128)(2,1)} %reduce-scatter.3.cloned.1.call-done, f32[1,512,768]{2,1,0:T(8,128)S(1)} %copy-done.1, ...), kind=kLoop, calls=%fused_computation.25 | loop fusion | flops 5505024 | bytes 8650756 | tf_op jit(solution)/shard_map/convert_element_type | solution.py:41
  249.6 0.0 all-gather.8.cloned.1.call-update
  249.6 0.0 copy-done.6
  249.7 0.1 fusion.28
  249.8 24.4 %all-gather.10.cloned.1.call-done = bf16[1,384,2048]{2,1,0:T(8,128)(2,1)} async-done(((bf16[1,384,512]{2,1,0:T(8,128)(2,1)}), bf16[1,384,2048]{2,1,0:T(8,128)(2,1)}) %all-gather.10.cloned.1.call-update) | async-done | bytes 1572880 | tf_op jit(solution)/shard_map/all_gather | solution.py:140
  274.2 93.9 %all-to-all-done = bf16[32,72,2048]{2,1,0:T(8,128)(2,1)} async-done(((bf16[32,72,2048]{2,1,0:T(8,128)(2,1)}), bf16[32,72,2048]{2,1,0:T(8,128)(2,1)}, u32[]{:S(2)}, u32[]{:S(2)}) %all-to-all-start) | async-done | bytes 9437216 | tf_op jit(solution)/shard_map/all_to_all | solution.py:101
  368.1 6.0 %fusion.6 = bf16[128,2048]{1,0:T(8,128)(2,1)} fusion(bf16[32,72,2048]{2,1,0:T(8,128)(2,1)} %all-to-all-done, f32[128,32]{0,1:T(8,128)S(1)} %fusion.28, pred[128,32]{0,1:T(8,128)(4,1)S(1)} %convert_compare_fusion.1), kind=kOutput, calls=%fused_computation.18 | convolution fusion | flops 1208811520 | bytes 9981952 | tf_op jit(solution)/shard_map/dot_general | solution.py:118
  374.1 0.0 all-gather.8.cloned.1.call-done
  374.1 0.0 copy-start
  374.1 3.9 %copy.26 = bf16[1,2048,768]{2,1,0:T(8,128)(2,1)} copy(bf16[1,2048,768]{2,1,0:T(8,128)(2,1)} %all-gather.8.cloned.1.call-done) | data formatting | bytes 6291456
  378.0 0.0 copy-done
  378.0 1.1 copy.27
  (5 shorter events, 0.1 us)
Async XLA Ops:
  7.2 76.6 %all-gather.14.cloned.1.call-start = ((), (), s32[]{:S(2)}) async-start(), calls=%async_computation.8 | async-start | bytes 17301504 | tf_op jit(solution)/shard_map/all_gather | solution.py:70
  7.9 150.1 %all-gather.12.cloned.1.call-start = ((), (), s32[]{:S(2)}) async-start(), calls=%async_computation.7 | async-start | bytes 17301504 | tf_op jit(solution)/shard_map/all_gather | solution.py:71
  8.6 214.6 %reduce-scatter.5.cloned.1.call-start = ((), (), s32[]{:S(2)}) async-start(), calls=%async_computation.5 | async-start | bytes 1966080 | tf_op jit(solution)/shard_map/reduce_scatter | solution.py:126
  34.3 61.5 %copy-start.3 = (pred[32,128]{1,0:T(8,128)(4,1)}, pred[32,128]{1,0:T(8,128)(4,1)S(1)}, u32[]{:S(2)}) copy-start(pred[32,128]{1,0:T(8,128)(4,1)S(1)} %convert_compare_fusion) | copy-start | bytes 12292
  83.7 12.1 %copy-start.4 = (bf16[1,2048,768]{2,1,0:T(8,128)(2,1)S(1)}, bf16[1,2048,768]{2,1,0:T(8,128)(2,1)}, u32[]{:S(2)}) copy-start(bf16[1,2048,768]{2,1,0:T(8,128)(2,1)} %param.14) | copy-start | bytes 9437188
  179.3 66.4 %reduce-scatter.3.cloned.1.call-start = ((), (), s32[]{:S(2)}) async-start(), calls=%async_computation.3 | async-start | bytes 3932160 | tf_op jit(solution)/shard_map/reduce_scatter | solution.py:123
  188.6 1.3 copy-start.7
  188.6 1.8 copy-start.8
  201.6 1.9 copy-start.5
  215.7 152.5 %all-to-all-start = ((bf16[32,72,2048]{2,1,0:T(8,128)(2,1)}), bf16[32,72,2048]{2,1,0:T(8,128)(2,1)}, u32[]{:S(2)}, u32[]{:S(2)}) async-start(bf16[32,72,2048]{2,1,0:T(8,128)(2,1)} %bitcast.41), calls=%async_computation | async-start | bytes 18874368 | tf_op jit(solution)/shard_map/all_to_all | solution.py:101
  222.9 22.8 %copy-start.1 = (f32[1,512,768]{2,1,0:T(8,128)S(1)}, f32[1,512,768]{2,1,0:T(8,128)}, u32[]{:S(2)}) copy-start(f32[1,512,768]{2,1,0:T(8,128)} %param.16) | copy-start | bytes 4718596
  222.9 22.8 %copy-start.2 = (f32[1,512,768]{2,1,0:T(8,128)S(1)}, f32[1,512,768]{2,1,0:T(8,128)}, u32[]{:S(2)}) copy-start(f32[1,512,768]{2,1,0:T(8,128)} %param.17) | copy-start | bytes 4718596
  222.9 51.3 %all-gather.10.cloned.1.call-start = ((), (), s32[]{:S(2)}) async-start(), calls=%async_computation.6 | async-start | bytes 1966080 | tf_op jit(solution)/shard_map/all_gather | solution.py:140
  226.7 22.9 %copy-start.6 = (s32[128,8]{0,1:T(8,128)S(1)}, s32[128,8]{0,1:T(8,128)}, u32[]{:S(2)}) copy-start(s32[128,8]{0,1:T(8,128)} %param.13) | copy-start | bytes 12292
  226.7 147.4 %all-gather.8.cloned.1.call-start = ((), (), s32[]{:S(2)}) async-start(), calls=%async_computation.4 | async-start | bytes 3932160 | tf_op jit(solution)/shard_map/all_gather | solution.py:139
  374.1 3.9 %copy-start = (bf16[1,384,2048]{2,1,0:T(8,128)(2,1)S(1)}, bf16[1,384,2048]{2,1,0:T(8,128)(2,1)}, u32[]{:S(2)}) copy-start(bf16[1,384,2048]{2,1,0:T(8,128)(2,1)} %all-gather.10.cloned.1.call-done) | copy-start | bytes 4718596
Sparse Core Ops, SparseCore 0:
  10.3 73.4 all-gather.13
  86.0 71.9 all-gather.11
  179.4 25.2 reduce-scatter.4
  207.5 38.0 reduce-scatter.2
  247.8 26.4 all-gather.9
  276.3 39.8 all-gather.7

commit v4 on v3

--- a/solution.py
+++ b/solution.py
@@ -9,15 +9,19 @@
 adam_eps = 1e-08
 
 
-def expert_backward(inputs, scaled_grad, weight_gate_up, weight_down):
+def expert_backward(inputs, scaled_parts, weight_gate_up, weight_down):
     hidden_count = weight_down.shape[0]
+    width = scaled_parts[0].shape[1]
     projected = jnp.dot(inputs, weight_gate_up, preferred_element_type=jnp.float32)
     gate_part = projected[:, :hidden_count]
     up_part = projected[:, hidden_count:]
     sigmoid_gate = jax.nn.sigmoid(gate_part)
     activated = gate_part * sigmoid_gate
     hidden_act = (activated * up_part).astype(jnp.bfloat16)
-    hidden_grad = jnp.dot(scaled_grad, weight_down.T, preferred_element_type=jnp.float32)
+    hidden_grad = sum(
+        jnp.dot(part, weight_down[:, i * width : (i + 1) * width].T, preferred_element_type=jnp.float32)
+        for i, part in enumerate(scaled_parts)
+    )
     slope = sigmoid_gate * (1.0 + gate_part * (1.0 - sigmoid_gate))
     hidden_act, up_slope, activated = lax.optimization_barrier(
         (hidden_act, up_part * slope, activated)
@@ -25,7 +29,10 @@
     pair_grad = jnp.concatenate(
         [hidden_grad * up_slope, hidden_grad * activated], axis=1
     ).astype(jnp.bfloat16)
-    down_grad = jnp.dot(hidden_act.T, scaled_grad, preferred_element_type=jnp.float32)
+    down_grad = jnp.concatenate(
+        [jnp.dot(hidden_act.T, part, preferred_element_type=jnp.float32) for part in scaled_parts],
+        axis=1,
+    )
     gate_up_grad = jnp.dot(inputs.T, pair_grad, preferred_element_type=jnp.float32)
     input_grad = jnp.dot(pair_grad, weight_gate_up.T, preferred_element_type=jnp.float32).astype(
         jnp.bfloat16
@@ -67,12 +74,28 @@
     capacity = min(local_tokens, 9 * local_tokens * top_count // (4 * expert_count))
     slot_total = expert_count * capacity
 
-    all_tokens = lax.all_gather(tokens, "expert", axis=0)
-    all_cot = lax.all_gather(cotangent, "expert", axis=0)
-    meta = jnp.concatenate([expert_ids.astype(jnp.float32), gate_probs], axis=1)
-    all_meta = lax.all_gather(meta, "expert", axis=0)
+    half_width = model_width // 2
+    pieces = []
+    rest = gate_probs
+    for _ in range(3):
+        piece = lax.reduce_precision(rest, exponent_bits=8, mantissa_bits=7)
+        pieces.append(piece)
+        rest = rest - piece
+    meta = jnp.concatenate([expert_ids.astype(jnp.float32)] + pieces, axis=1)
+    meta_width = 128
+    meta = jnp.pad(meta, ((0, 0), (0, meta_width - meta.shape[1]))).astype(jnp.bfloat16)
+    first = lax.all_gather(
+        jnp.concatenate([tokens, cotangent[:, :half_width], meta], axis=1), "expert", axis=0
+    )
+    first, cot_after = lax.optimization_barrier((first, cotangent))
+    cot_hi = lax.all_gather(cot_after[:, half_width:], "expert", axis=0)
+    meta_at = model_width + half_width
+    all_meta = first[..., meta_at : meta_at + 4 * top_count].astype(jnp.float32)
     all_ids = all_meta[..., :top_count].astype(jnp.int32)
-    all_gates = all_meta[..., top_count:]
+    all_gates = (
+        all_meta[..., top_count : 2 * top_count] + all_meta[..., 2 * top_count : 3 * top_count]
+    ) + all_meta[..., 3 * top_count :]
+
 
     match = all_ids == me
     routed = jnp.any(match, axis=-1).astype(jnp.float32)
@@ -81,20 +104,21 @@
     slots = jnp.arange(capacity, dtype=jnp.float32)
     pick = (routed[:, None, :] > 0) & (rank[:, None, :] == slots[None, :, None])
     pick_b = pick.astype(jnp.bfloat16)
-    inputs = jnp.einsum(
-        "srt,stc->src", pick_b, all_tokens, preferred_element_type=jnp.float32
-    ).astype(jnp.bfloat16)
-    cot_rows = jnp.einsum(
-        "srt,stc->src", pick_b, all_cot, preferred_element_type=jnp.float32
-    )
+    picked_first = jnp.einsum("srt,stc->src", pick_b, first, preferred_element_type=jnp.float32)
+    inputs = picked_first[..., :model_width].astype(jnp.bfloat16)
+    picked_first = picked_first[..., : model_width + half_width]
     slot_gate = jnp.sum(jnp.where(pick, gate_of[:, None, :], 0.0), axis=-1)
-    scaled = (slot_gate[..., None] * cot_rows).astype(jnp.bfloat16)
+    picked_hi = jnp.einsum("srt,stc->src", pick_b, cot_hi, preferred_element_type=jnp.float32)
+    scaled = [
+        (slot_gate[..., None] * part).astype(jnp.bfloat16).reshape(slot_total, half_width)
+        for part in (picked_first[..., model_width:], picked_hi)
+    ]
 
     weight_pair = gate_up[0]
     weight_down = down_weight[0]
     grad_pair, grad_down, row_grads = expert_backward(
         inputs.reshape(slot_total, model_width),
-        scaled.reshape(slot_total, model_width),
+        scaled,
         weight_pair,
         weight_down,
     )

time: 386 us -> 379 us (0.982)
  blocking collectives: 24.1 us -> 0 us
  other arithmetic: 13.3 us -> 28.2 us
  local copies, waits for them, and re-layouts: 8.78 us -> 19.9 us
  matrix products: 82.6 us -> 75.2 us
    all_gather x1 -> x0, blocking collectives: 24.1 us -> none  [local(): all_meta = lax.all_gather(meta, 'expert', axis=0)]
    slice x0 -> x3, local copies, waits for them, and re-layouts: none -> 8.92 us  [the longest x1 7.22 us: local(): inputs = picked_first[..., :model_width].astype(jnp.bfloat16)]
    convert_element_type x1 -> x2, other arithmetic: 0.69 us -> 6.19 us  [the longest x1 4.72 us: local(): (slot_gate[..., None] * part).astype(jnp.bfloat16)]
    dot_general x4 -> x6, matrix products: 42.4 us -> 37 us  [the longest x1 17.8 us: local(): jnp.einsum('srt,stc->src', pick_b, first, preferred_element_type=jnp.floa...]
    unnamed x21 -> x53, local copies, waits for them, and re-layouts: 8.78 us -> 11 us
  transfers between devices with their start and end apart: 7 -> 7, of which waited for: 5 -> 4; matrix products, arithmetic and copies ran while one was open for 19% -> 26% of each run, Pallas kernels for 0% -> 0%
where the time goes in v4:
time: 379 us; the launch traced here: 378 us
  waiting for transfers between devices  233 us (61%)
  matrix products  75.2 us (20%)
  other arithmetic  28.2 us (7%)
  local copies, waits for them, and re-layouts  19.9 us (5%)
  between operations  14.4 us (4%)
  starting transfers between devices  7.33 us (2%)
    all_gather x1, waiting for transfers between devices, local(): lax.all_gather(jnp.concatenate([tokens, cotangent[:, :half_width], meta],...  95.1 us
    all_to_all x1, waiting for transfers between devices, local(): lax.all_to_all(row_grads.reshape(expert_count, capacity, model_width), 'e...  93 us
    all_gather x1, waiting for transfers between devices, local(): lax.all_gather(new_down, 'group', axis=2, tiled=True)  24.4 us
    reduce_scatter x1, waiting for transfers between devices, local(): lax.psum_scatter(grad_pair[None].astype(jnp.bfloat16), 'group', scatter_d...  20.6 us
    dot_general x1, matrix products, local(): jnp.einsum('srt,stc->src', pick_b, first, preferred_element_type=jnp.floa...  17.8 us
    dot_general x1, matrix products, expert_backward(): jnp.dot(pair_grad, weight_gate_up.T, preferred_element_type=jnp.float32)  11.6 us
    unnamed x53, local copies, waits for them, and re-layouts  11 us
    dot_general x1, matrix products, expert_backward(): jnp.dot(inputs.T, pair_grad, preferred_element_type=jnp.float32)  10.8 us
  transfers between devices with their start and end apart: 7, of which 4 were waited for; matrix products, arithmetic and copies ran while one was open for 26% of the time, Pallas kernels for 0%

profile of v4, /device:TPU:50, one launch (start us, length us, event | category | flops | bytes accessed | tf_op | source)
XLA Modules:
  0.0 378.5 jit_solution(3219271340939462758)
XLA Ops:
  7.2 0.0 copy-start.13
  7.2 0.0 all-gather.11.cloned.1.call-start
  7.2 0.7 reduce-precision_convert_fusion.1
  8.0 0.7 convert_convert_fusion.4
  8.7 0.1 copy.25
  8.8 1.0 slice.42
  9.8 2.0 fusion.21
  11.8 0.0 all-gather.11.cloned.1.call-update
  11.8 0.0 all-gather.13.cloned.1.call-start
  11.8 95.1 %all-gather.11.cloned.1.call-done = bf16[4096,3200]{1,0:T(8,128)(2,1)} async-done(((bf16[128,3200]{1,0:T(8,128)(2,1)}), bf16[4096,3200]{1,0:T(8,128)(2,1)}) %all-gather.11.cloned.1.call-update) | async-done | bytes 26214416 | tf_op jit(solution)/shard_map/all_gather | solution.py:87
  106.9 0.7 slice.50
  107.7 0.0 all-gather.13.cloned.1.call-update
  107.7 0.0 reduce-scatter.5.cloned.1.call-start
  107.7 1.5 slice_convert_fusion.2
  109.2 3.0 fusion.8
  112.2 0.6 reduce_or.19
  112.8 0.0 copy-start.16
  112.8 0.1 fusion.34
  113.0 0.5 copy-done.16
  113.4 17.8 %fusion.19 = f32[32,72,3200]{2,1,0:T(8,128)} fusion(bf16[32,128,3200]{2,1,0:T(8,128)(2,1)} %bitcast.38, f32[32,128]{1,0:T(8,128)S(1)} %fusion.34, pred[32,128]{1,0:T(8,128)(4,1)S(1)} %convert_compare_fusion), kind=kOutput, calls=%fused_computation.44 | convolution fusion | flops 1888026624 | bytes 55726080 | tf_op jit(solution)/shard_map/srt,stc->src/dot_general | solution.py:107
  131.2 7.2 %slice.92 = bf16[32,72,2048]{2,1,0:T(8,128)(2,1)S(1)} slice(f32[32,72,3200]{2,1,0:T(8,128)} %fusion.19), slice={[0:32], [0:72], [0:2048]} | slice | bytes 18874368 | tf_op jit(solution)/shard_map/slice | solution.py:108
  138.4 0.1 copy-done.14
  138.5 9.6 %fusion.3 = f32[2304,768]{0,1:T(8,128)} fusion(bf16[2304,2048]{1,0:T(8,128)(2,1)S(1)} %bitcast.40, bf16[1,2048,768]{2,1,0:T(8,128)(2,1)S(1)} %copy-done.14), kind=kOutput, calls=%fused_computation.15 | convolution fusion | flops 7247757312 | bytes 19660800 | tf_op jit(solution)/shard_map/dot_general | solution.py:15
  148.2 5.8 %fusion.1 = (f32[2304,384]{0,1:T(8,128)S(1)}, f32[2304,384]{0,1:T(8,128)}, bf16[2304,384]{0,1:T(8,128)(2,1)}) fusion(f32[2304,768]{0,1:T(8,128)} %fusion.3), kind=kLoop, calls=%fused_computation.12 | loop fusion | flops 9732096 | bytes 15925248 | tf_op jit(solution)/shard_map/mul | solution.py:19
  153.9 0.6 select_reduce_fusion
  154.6 0.0 copy-start.15
  154.6 0.0 copy-start.7
  154.6 4.7 %fusion = bf16[32,72,1024]{2,1,0:T(8,128)(2,1)S(1)} fusion(f32[32,72,3200]{2,1,0:T(8,128)} %fusion.19, f32[32,72]{1,0:T(8,128)S(1)} %select_reduce_fusion), kind=kLoop, calls=%fused_computation.3 | loop fusion | flops 4718592 | bytes 14164992 | tf_op jit(solution)/shard_map/convert_element_type | solution.py:113
  159.4 2.2 copy-done.6
  161.5 2.9 fusion.13
  164.4 4.9 %multiply_convert_fusion = bf16[32,72,1024]{2,1,0:T(8,128)(2,1)S(1)} fusion(f32[32,72]{1,0:T(8,128)} %copy-done.15, bf16[32,128,1024]{2,1,0:T(8,128)(2,1)} %bitcast.44, f32[32,128]{1,0:T(8,128)S(1)} %fusion.34, pred[32,128]{1,0:T(8,128)(4,1)} %copy-done.16), kind=kOutput, calls=%fused_computation.4 | convolution fusion | flops 609288192 | bytes 13136896 | tf_op jit(solution)/shard_map/srt,stc->src/dot_general | solution.py:111
  169.3 0.0 copy-start.12
  169.3 2.0 fusion.14
  171.3 0.1 copy-done
  171.5 1.2 pad_maximum_fusion.3
  172.7 0.0 reduce-scatter.5.cloned.1.call-update
  172.7 0.0 reduce-scatter.3.cloned.1.call-start
  172.8 0.0 slice-start.1
  172.8 4.7 %fusion.25 = f32[2304,384]{0,1:T(8,128)S(1)} fusion(bf16[2304,1024]{1,0:T(8,128)(2,1)} %bitcast.46, bf16[384,2048]{1,0:T(8,128)(2,1)} %bitcast.47), kind=kOutput, calls=%fused_computation.51 | convolution fusion | flops 1811939328 | bytes 9043968 | tf_op jit(solution)/shard_map/dot_general | solution.py:22
  177.6 0.3 copy-done.1
  177.9 4.7 %multiply_convert_fusion.2 = (bf16[2304,384]{0,1:T(8,128)(2,1)S(1)}, bf16[2304,384]{0,1:T(8,128)(2,1)}) fusion(f32[2304,384]{0,1:T(8,128)S(1)} %copy-done.1, f32[2304,384]{0,1:T(8,128)S(1)} %get-tuple-element.15, f32[2304,384]{0,1:T(8,128)S(1)} %fusion.25, bf16[2304,1024]{1,0:T(8,128)(2,1)S(1)} %bitcast.36, bf16[384,2048]{1,0:T(8,128)(2,1)} %bitcast.48), kind=kOutput, calls=%fused_computation.8 | convolution fusion | flops 1816363008 | bytes 19660800 | tf_op jit(solution)/shard_map/dot_general | solution.py:22
  182.6 1.2 copy-done.3
  183.8 10.8 %fusion.5 = bf16[1,2048,768]{2,1,0:T(8,128)(2,1)} fusion(bf16[2304,2048]{1,0:T(8,128)(2,1)S(1)} %bitcast.43, bf16[2304,384]{0,1:T(8,128)(2,1)} %get-tuple-element.29, bf16[2304,384]{0,1:T(8,128)(2,1)S(1)} %get-tuple-element.28), kind=kOutput, calls=%fused_computation.17 | convolution fusion | flops 7256408064 | bytes 16121856 | tf_op jit(solution)/shard_map/dot_general | solution.py:36
  194.6 0.0 reduce-scatter.3.cloned.1.call-update
  194.6 1.5 copy-done.4
  196.1 11.6 %convolution_convert_fusion = bf16[2304,2048]{1,0:T(8,128)(2,1)} fusion(bf16[1,2048,768]{2,1,0:T(8,128)(2,1)} %param.14, bf16[2304,384]{0,1:T(8,128)(2,1)S(1)} %copy-done.5, bf16[2304,384]{0,1:T(8,128)(2,1)S(1)} %copy-done.4), kind=kOutput, calls=%fused_computation.1 | convolution fusion | flops 7259553792 | bytes 16121856 | tf_op jit(solution)/shard_map/dot_general | solution.py:37
  207.7 7.1 %all-to-all-start = ((bf16[32,72,2048]{2,1,0:T(8,128)(2,1)}), bf16[32,72,2048]{2,1,0:T(8,128)(2,1)}, u32[]{:S(2)}, u32[]{:S(2)}) async-start(bf16[32,72,2048]{2,1,0:T(8,128)(2,1)} %bitcast.39), calls=%async_computation | async-start | bytes 18874368 | tf_op jit(solution)/shard_map/all_to_all | solution.py:125
  214.8 0.0 copy-start.10
  214.8 0.0 copy-start.11
  214.8 0.0 all-gather.9.cloned.1.call-start
  214.9 0.0 reduce-scatter.5.cloned.1.call-done
  214.9 3.4 subtract_convert_fusion.1
  218.3 0.0 all-gather.9.cloned.1.call-update
  218.3 0.0 copy-start.19
  218.4 0.0 all-gather.7.cloned.1.call-start
  218.4 20.6 %reduce-scatter.3.cloned.1.call-done = bf16[1,512,768]{2,1,0:T(8,128)(2,1)} async-done(((bf16[1,2048,768]{2,1,0:T(8,128)(2,1)}), bf16[1,512,768]{2,1,0:T(8,128)(2,1)}) %reduce-scatter.3.cloned.1.call-update) | async-done | bytes 786448 | tf_op jit(solution)/shard_map/reduce_scatter | solution.py:147
  239.0 3.9 %subtract_convert_fusion = (bf16[1,512,768]{2,1,0:T(8,128)(2,1)}, f32[1,512,768]{2,1,0:T(8,128)}, f32[1,512,768]{2,1,0:T(8,128)}) fusion(bf16[1,2048,768]{2,1,0:T(8,128)(2,1)} %param.14, s32[]{:T(128)S(6)} %select_n.14, bf16[1,512,768]{2,1,0:T(8,128)(2,1)} %reduce-scatter.3.cloned.1.call-done, f32[1,512,768]{2,1,0:T(8,128)S(1)} %copy-done.10, ...), kind=kLoop, calls=%fused_computation.33 | loop fusion | flops 5505024 | bytes 8650756 | tf_op jit(solution)/shard_map/convert_element_type | solution.py:48
  242.9 0.0 all-gather.7.cloned.1.call-update
  243.0 0.1 fusion.35
  243.1 24.4 %all-gather.9.cloned.1.call-done = bf16[1,384,2048]{2,1,0:T(8,128)(2,1)} async-done(((bf16[1,384,512]{2,1,0:T(8,128)(2,1)}), bf16[1,384,2048]{2,1,0:T(8,128)(2,1)}) %all-gather.9.cloned.1.call-update) | async-done | bytes 1572880 | tf_op jit(solution)/shard_map/all_gather | solution.py:164
  267.6 93.0 %all-to-all-done = bf16[32,72,2048]{2,1,0:T(8,128)(2,1)} async-done(((bf16[32,72,2048]{2,1,0:T(8,128)(2,1)}), bf16[32,72,2048]{2,1,0:T(8,128)(2,1)}, u32[]{:S(2)}, u32[]{:S(2)}) %all-to-all-start) | async-done | bytes 9437216 | tf_op jit(solution)/shard_map/all_to_all | solution.py:125
  360.6 6.0 %fusion.6 = bf16[128,2048]{1,0:T(8,128)(2,1)} fusion(bf16[32,72,2048]{2,1,0:T(8,128)(2,1)} %all-to-all-done, f32[128,32]{0,1:T(8,128)S(1)} %fusion.35, pred[128,32]{0,1:T(8,128)(4,1)S(1)} %convert_compare_fusion.1), kind=kOutput, calls=%fused_computation.19 | convolution fusion | flops 1208811520 | bytes 9981952 | tf_op jit(solution)/shard_map/dot_general | solution.py:142
  366.6 3.9 %copy.28 = bf16[1,2048,768]{2,1,0:T(8,128)(2,1)} copy(bf16[1,2048,768]{2,1,0:T(8,128)(2,1)} %all-gather.7.cloned.1.call-done) | data formatting | bytes 6291456
  370.5 1.1 copy.29
  (42 shorter events, 0.1 us)
Async XLA Ops:
  7.2 99.8 %copy-start.13 = (bf16[128,2048]{1,0:T(8,128)(2,1)S(1)}, bf16[128,2048]{1,0:T(8,128)(2,1)}, u32[]{:S(2)}) copy-start(bf16[128,2048]{1,0:T(8,128)(2,1)} %param.11) | copy-start | bytes 1572868
  7.2 99.8 %all-gather.11.cloned.1.call-start = ((), (), s32[]{:S(2)}) async-start(), calls=%async_computation.7 | async-start | bytes 27033600 | tf_op jit(solution)/shard_map/all_gather | solution.py:87
  11.8 152.6 %all-gather.13.cloned.1.call-start = ((), (), s32[]{:S(2)}) async-start(), calls=%async_computation.8 | async-start | bytes 8650752 | tf_op jit(solution)/shard_map/all_gather | solution.py:91
  107.7 107.2 %reduce-scatter.5.cloned.1.call-start = ((), (), s32[]{:S(2)}) async-start(), calls=%async_computation.5 | async-start | bytes 1966080 | tf_op jit(solution)/shard_map/reduce_scatter | solution.py:150
  112.8 0.6 copy-start.16
  131.2 7.3 %copy-start.14 = (bf16[1,2048,768]{2,1,0:T(8,128)(2,1)S(1)}, bf16[1,2048,768]{2,1,0:T(8,128)(2,1)}, u32[]{:S(2)}) copy-start(bf16[1,2048,768]{2,1,0:T(8,128)(2,1)} %param.14) | copy-start | bytes 9437188
  138.4 9.7 %copy-start.2 = (bf16[32,72,2048]{2,1,0:T(8,128)(2,1)}, bf16[32,72,2048]{2,1,0:T(8,128)(2,1)S(1)}, u32[]{:S(2)}) copy-start(bf16[32,72,2048]{2,1,0:T(8,128)(2,1)S(1)} %slice.92) | copy-start | bytes 28311556
  148.2 5.8 %copy-start.17 = (pred[32,128]{1,0:T(8,128)(4,1)S(1)}, pred[32,128]{1,0:T(8,128)(4,1)}, u32[]{:S(2)}) copy-start(pred[32,128]{1,0:T(8,128)(4,1)} %copy-done.16) | copy-start | bytes 12292
  148.2 5.8 %copy-start.18 = (f32[32,128]{1,0:T(8,128)S(1)}, f32[32,128]{1,0:T(8,128)}, u32[]{:S(2)}) copy-start(f32[32,128]{1,0:T(8,128)} %get-tuple-element.23) | copy-start | bytes 49156
  154.6 4.8 %copy-start.15 = (f32[32,72]{1,0:T(8,128)}, f32[32,72]{1,0:T(8,128)S(1)}, u32[]{:S(2)}) copy-start(f32[32,72]{1,0:T(8,128)S(1)} %select_reduce_fusion) | copy-start | bytes 27652
  154.6 6.9 %copy-start.7 = (bf16[2304,384]{0,1:T(8,128)(2,1)S(1)}, bf16[2304,384]{0,1:T(8,128)(2,1)}, u32[]{:S(2)}) copy-start(bf16[2304,384]{0,1:T(8,128)(2,1)} %get-tuple-element.16) | copy-start | bytes 5308420
  159.4 2.2 copy-start.6
  164.4 4.9 %copy-start.8 = (bf16[2304,384]{0,1:T(8,128)(2,1)S(1)}, bf16[2304,384]{0,1:T(8,128)(2,1)}, u32[]{:S(2)}) copy-start(bf16[2304,384]{0,1:T(8,128)(2,1)} %get-tuple-element.16) | copy-start | bytes 5308420
  169.3 2.2 copy-start
  169.3 2.1 copy-start.12
  172.7 66.3 %reduce-scatter.3.cloned.1.call-start = ((), (), s32[]{:S(2)}) async-start(), calls=%async_computation.3 | async-start | bytes 3932160 | tf_op jit(solution)/shard_map/reduce_scatter | solution.py:147
  172.8 4.8 %slice-start = ((s8[4718592]{0:T(1024)(128)(4,1)}), s8[4194304]{0:T(1024)(128)(4,1)S(1)}, s32[]{:S(2)}) async-start(s8[4718592]{0:T(1024)(128)(4,1)} %bitcast.34), calls=%async_computation.9 | async-start | bytes 8388608
  172.8 4.8 %slice-start.1 = ((s8[4718592]{0:T(1024)(128)(4,1)}), s8[524288]{0:T(1024)(128)(4,1)S(1)}, s32[]{:S(2)}) async-start(s8[4718592]{0:T(1024)(128)(4,1)} %bitcast.34), calls=%async_computation.10 | async-start | bytes 1048576
  172.8 5.1 %copy-start.1 = (f32[2304,384]{0,1:T(8,128)S(1)}, f32[2304,384]{0,1:T(8,128)}, u32[]{:S(2)}) copy-start(f32[2304,384]{0,1:T(8,128)} %get-tuple-element.14) | copy-start | bytes 10616836
  172.8 11.0 %slice-start.2 = ((s8[9437184]{0:T(1024)(128)(4,1)}), s8[4194304]{0:T(1024)(128)(4,1)S(1)}, s32[]{:S(2)}) async-start(s8[9437184]{0:T(1024)(128)(4,1)} %bitcast.41), calls=%async_computation.11 | async-start | bytes 8388608
  177.9 5.9 %slice-start.3 = ((s8[9437184]{0:T(1024)(128)(4,1)}), s8[4194304]{0:T(1024)(128)(4,1)S(1)}, s32[]{:S(2)}) async-start(s8[9437184]{0:T(1024)(128)(4,1)} %bitcast.41), calls=%async_computation.12 | async-start | bytes 8388608
  177.9 5.9 %slice-start.4 = ((s8[9437184]{0:T(1024)(128)(4,1)}), s8[1048576]{0:T(1024)(128)(4,1)S(1)}, s32[]{:S(2)}) async-start(s8[9437184]{0:T(1024)(128)(4,1)} %bitcast.41), calls=%async_computation.13 | async-start | bytes 2097152
  182.6 1.2 copy-start.3
  183.8 10.8 %copy-start.5 = (bf16[2304,384]{0,1:T(8,128)(2,1)S(1)}, bf16[2304,384]{0,1:T(8,128)(2,1)}, u32[]{:S(2)}) copy-start(bf16[2304,384]{0,1:T(8,128)(2,1)} %get-tuple-element.29) | copy-start | bytes 5308420
  194.6 1.5 copy-start.4
  207.7 152.9 %all-to-all-start = ((bf16[32,72,2048]{2,1,0:T(8,128)(2,1)}), bf16[32,72,2048]{2,1,0:T(8,128)(2,1)}, u32[]{:S(2)}, u32[]{:S(2)}) async-start(bf16[32,72,2048]{2,1,0:T(8,128)(2,1)} %bitcast.39), calls=%async_computation | async-start | bytes 18874368 | tf_op jit(solution)/shard_map/all_to_all | solution.py:125
  214.8 24.2 %copy-start.10 = (f32[1,512,768]{2,1,0:T(8,128)S(1)}, f32[1,512,768]{2,1,0:T(8,128)}, u32[]{:S(2)}) copy-start(f32[1,512,768]{2,1,0:T(8,128)} %param.16) | copy-start | bytes 4718596
  214.8 24.2 %copy-start.11 = (f32[1,512,768]{2,1,0:T(8,128)S(1)}, f32[1,512,768]{2,1,0:T(8,128)}, u32[]{:S(2)}) copy-start(f32[1,512,768]{2,1,0:T(8,128)} %param.17) | copy-start | bytes 4718596
  214.8 52.7 %all-gather.9.cloned.1.call-start = ((), (), s32[]{:S(2)}) async-start(), calls=%async_computation.6 | async-start | bytes 1966080 | tf_op jit(solution)/shard_map/all_gather | solution.py:164
  218.3 24.6 %copy-start.19 = (s32[128,8]{0,1:T(8,128)S(1)}, s32[128,8]{0,1:T(8,128)}, u32[]{:S(2)}) copy-start(s32[128,8]{0,1:T(8,128)} %param.13) | copy-start | bytes 12292
  218.4 148.2 %all-gather.7.cloned.1.call-start = ((), (), s32[]{:S(2)}) async-start(), calls=%async_computation.4 | async-start | bytes 3932160 | tf_op jit(solution)/shard_map/all_gather | solution.py:163
  366.6 3.9 %copy-start.9 = (bf16[1,384,2048]{2,1,0:T(8,128)(2,1)S(1)}, bf16[1,384,2048]{2,1,0:T(8,128)(2,1)}, u32[]{:S(2)}) copy-start(bf16[1,384,2048]{2,1,0:T(8,128)(2,1)} %all-gather.9.cloned.1.call-done) | copy-start | bytes 4718596
Sparse Core Ops, SparseCore 0:
  11.9 94.9 all-gather.10
  109.8 52.5 all-gather.12
  172.9 25.1 reduce-scatter.4
  200.9 38.0 reduce-scatter.2
  241.1 26.4 all-gather.8
  269.7 39.8 all-gather.6

commit v5 on v4

--- a/solution.py
+++ b/solution.py
@@ -104,14 +104,19 @@
     slots = jnp.arange(capacity, dtype=jnp.float32)
     pick = (routed[:, None, :] > 0) & (rank[:, None, :] == slots[None, :, None])
     pick_b = pick.astype(jnp.bfloat16)
-    picked_first = jnp.einsum("srt,stc->src", pick_b, first, preferred_element_type=jnp.float32)
-    inputs = picked_first[..., :model_width].astype(jnp.bfloat16)
-    picked_first = picked_first[..., : model_width + half_width]
+    picked_first = jnp.einsum(
+        "srt,stc->src", pick_b, first, preferred_element_type=jnp.float32
+    ).astype(jnp.bfloat16)
+    inputs = picked_first[..., :model_width]
     slot_gate = jnp.sum(jnp.where(pick, gate_of[:, None, :], 0.0), axis=-1)
-    picked_hi = jnp.einsum("srt,stc->src", pick_b, cot_hi, preferred_element_type=jnp.float32)
+    picked_hi = jnp.einsum(
+        "srt,stc->src", pick_b, cot_hi, preferred_element_type=jnp.float32
+    ).astype(jnp.bfloat16)
     scaled = [
-        (slot_gate[..., None] * part).astype(jnp.bfloat16).reshape(slot_total, half_width)
-        for part in (picked_first[..., model_width:], picked_hi)
+        (slot_gate[..., None] * part.astype(jnp.float32))
+        .astype(jnp.bfloat16)
+        .reshape(slot_total, half_width)
+        for part in (picked_first[..., model_width:meta_at], picked_hi)
     ]
 
     weight_pair = gate_up[0]

time: 379 us -> 375 us (0.989)
  other arithmetic: 28.2 us -> 24 us
  matrix products: 75.2 us -> 71.2 us
    unnamed x53 -> x51, local copies, waits for them, and re-layouts: 11 us -> 11.6 us
  transfers between devices with their start and end apart: 7 -> 7, of which waited for: 4 -> 5; matrix products, arithmetic and copies ran while one was open for 26% -> 25% of each run, Pallas kernels for 0% -> 0%
where the time goes in v5:
time: 375 us; the launch traced here: 374 us
  waiting for transfers between devices  234 us (62%)
  matrix products  71.2 us (19%)
  other arithmetic  24 us (6%)
  local copies, waits for them, and re-layouts  22.7 us (6%)
  between operations  14.4 us (4%)
  starting transfers between devices  7.71 us (2%)
    all_gather x1, waiting for transfers between devices, local(): lax.all_gather(jnp.concatenate([tokens, cotangent[:, :half_width], meta],...  95.1 us
    all_to_all x1, waiting for transfers between devices, local(): lax.all_to_all(row_grads.reshape(expert_count, capacity, model_width), 'e...  90.9 us
    all_gather x1, waiting for transfers between devices, local(): lax.all_gather(new_down, 'group', axis=2, tiled=True)  24.4 us
    reduce_scatter x1, waiting for transfers between devices, local(): lax.psum_scatter(grad_pair[None].astype(jnp.bfloat16), 'group', scatter_d...  21.9 us
    dot_general x1, matrix products, local(): jnp.einsum('srt,stc->src', pick_b, first, preferred_element_type=jnp.floa...  15.5 us
    dot_general x1, matrix products, expert_backward(): jnp.dot(pair_grad, weight_gate_up.T, preferred_element_type=jnp.float32)  12.1 us
    unnamed x51, local copies, waits for them, and re-layouts  11.6 us
    dot_general x1, matrix products, expert_backward(): jnp.dot(inputs, weight_gate_up, preferred_element_type=jnp.float32)  10 us
  transfers between devices with their start and end apart: 7, of which 5 were waited for; matrix products, arithmetic and copies ran while one was open for 25% of the time, Pallas kernels for 0%

profile of v5, /device:TPU:50, one launch (start us, length us, event | category | flops | bytes accessed | tf_op | source)
XLA Modules:
  0.0 374.4 jit_solution(3848247058425894077)
XLA Ops:
  7.2 0.0 copy-start.12
  7.2 0.0 all-gather.11.cloned.1.call-start
  7.2 0.7 reduce-precision_convert_fusion.1
  8.0 0.7 convert_convert_fusion.4
  8.7 0.1 copy.25
  8.8 1.0 slice.39
  9.8 2.0 fusion.19
  11.8 0.0 all-gather.11.cloned.1.call-update
  11.8 0.0 all-gather.13.cloned.1.call-start
  11.8 95.1 %all-gather.11.cloned.1.call-done = bf16[4096,3200]{1,0:T(8,128)(2,1)} async-done(((bf16[128,3200]{1,0:T(8,128)(2,1)}), bf16[4096,3200]{1,0:T(8,128)(2,1)}) %all-gather.11.cloned.1.call-update) | async-done | bytes 26214416 | tf_op jit(solution)/shard_map/all_gather | solution.py:87
  106.9 0.7 slice.47
  107.7 0.0 all-gather.13.cloned.1.call-update
  107.7 0.0 reduce-scatter.5.cloned.1.call-start
  107.7 1.5 slice_convert_fusion.1
  109.2 3.0 fusion.7
  112.2 0.6 reduce_or.19
  112.8 0.0 copy-start.15
  112.8 0.1 fusion.32
  113.0 0.5 copy-done.15
  113.4 15.5 %convolution_convert_fusion = bf16[32,72,3200]{2,1,0:T(8,128)(2,1)} fusion(bf16[32,128,3200]{2,1,0:T(8,128)(2,1)} %bitcast.38, f32[32,128]{1,0:T(8,128)S(1)} %fusion.32, pred[32,128]{1,0:T(8,128)(4,1)S(1)} %convert_compare_fusion), kind=kOutput, calls=%fused_computation | convolution fusion | flops 1895399424 | bytes 40980480 | tf_op jit(solution)/shard_map/srt,stc->src/dot_general | solution.py:107
  128.9 9.5 %slice.59 = bf16[32,72,2048]{2,1,0:T(8,128)(2,1)} slice(bf16[32,72,3200]{2,1,0:T(8,128)(2,1)} %convolution_convert_fusion), slice={[0:32], [0:72], [0:2048]} | slice | bytes 18874368 | tf_op jit(solution)/shard_map/slice | solution.py:110
  138.4 10.0 %fusion.2 = f32[2304,768]{0,1:T(8,128)S(1)} fusion(bf16[2304,2048]{1,0:T(8,128)(2,1)} %bitcast.40, bf16[1,2048,768]{2,1,0:T(8,128)(2,1)S(1)} %copy-done.13), kind=kOutput, calls=%fused_computation.14 | convolution fusion | flops 7247757312 | bytes 19660800 | tf_op jit(solution)/shard_map/dot_general | solution.py:15
  148.4 0.0 copy-start.16
  148.4 0.0 copy-start.17
  148.4 2.9 fusion
  151.3 0.6 select_reduce_fusion
  152.0 0.0 copy-start.14
  152.0 3.4 multiply_convert_fusion.1
  155.5 2.2 copy-done.5
  157.7 2.9 fusion.12
  160.5 1.8 all-gather.13.cloned.1.call-done
  162.3 4.9 %multiply_convert_fusion = bf16[32,72,1024]{2,1,0:T(8,128)(2,1)S(1)} fusion(f32[32,72]{1,0:T(8,128)} %copy-done.14, bf16[32,128,1024]{2,1,0:T(8,128)(2,1)} %bitcast.44, f32[32,128]{1,0:T(8,128)S(1)} %fusion.32, pred[32,128]{1,0:T(8,128)(4,1)} %copy-done.15), kind=kOutput, calls=%fused_computation.2 | convolution fusion | flops 614006784 | bytes 13136896 | tf_op jit(solution)/shard_map/srt,stc->src/dot_general | solution.py:112
  167.3 0.0 copy-start.11
  167.3 2.0 fusion.13
  169.3 0.1 copy-done
  169.4 1.2 pad_maximum_fusion.3
  170.6 0.0 reduce-scatter.5.cloned.1.call-update
  170.7 0.0 reduce-scatter.3.cloned.1.call-start
  170.7 4.7 %fusion.23 = f32[2304,384]{0,1:T(8,128)S(1)} fusion(bf16[2304,1024]{1,0:T(8,128)(2,1)} %bitcast.46, bf16[384,2048]{1,0:T(8,128)(2,1)} %bitcast.47), kind=kOutput, calls=%fused_computation.49 | convolution fusion | flops 1811939328 | bytes 9043968 | tf_op jit(solution)/shard_map/dot_general | solution.py:22
  175.5 0.3 copy-done.1
  175.8 3.7 multiply_convert_fusion.3
  179.5 1.3 copy-done.2
  180.8 0.5 copy-done.4
  181.3 9.2 %fusion.4 = bf16[1,2048,768]{2,1,0:T(8,128)(2,1)} fusion(bf16[2304,2048]{1,0:T(8,128)(2,1)S(1)} %bitcast.43, bf16[2304,384]{0,1:T(8,128)(2,1)S(1)} %get-tuple-element.29, bf16[2304,384]{0,1:T(8,128)(2,1)S(1)} %get-tuple-element.28), kind=kOutput, calls=%fused_computation.16 | convolution fusion | flops 7256408064 | bytes 16121856 | tf_op jit(solution)/shard_map/dot_general | solution.py:36
  190.5 0.0 reduce-scatter.3.cloned.1.call-update
  190.5 1.5 copy-done.3
  192.0 12.1 %convolution_convert_fusion.1 = bf16[2304,2048]{1,0:T(8,128)(2,1)} fusion(bf16[1,2048,768]{2,1,0:T(8,128)(2,1)} %param.14, bf16[2304,384]{0,1:T(8,128)(2,1)} %copy-done.4, bf16[2304,384]{0,1:T(8,128)(2,1)S(1)} %copy-done.3), kind=kOutput, calls=%fused_computation.1 | convolution fusion | flops 7259553792 | bytes 16121856 | tf_op jit(solution)/shard_map/dot_general | solution.py:37
  204.1 7.2 %all-to-all-start = ((bf16[32,72,2048]{2,1,0:T(8,128)(2,1)}), bf16[32,72,2048]{2,1,0:T(8,128)(2,1)}, u32[]{:S(2)}, u32[]{:S(2)}) async-start(bf16[32,72,2048]{2,1,0:T(8,128)(2,1)} %bitcast.39), calls=%async_computation | async-start | bytes 18874368 | tf_op jit(solution)/shard_map/all_to_all | solution.py:130
  211.3 0.0 copy-start.9
  211.3 0.0 copy-start.10
  211.3 0.0 all-gather.9.cloned.1.call-start
  211.4 0.0 reduce-scatter.5.cloned.1.call-done
  211.4 3.4 subtract_convert_fusion.1
  214.8 0.0 all-gather.9.cloned.1.call-update
  214.8 0.3 all-gather.7.cloned.1.call-start
  215.1 21.9 %reduce-scatter.3.cloned.1.call-done = bf16[1,512,768]{2,1,0:T(8,128)(2,1)} async-done(((bf16[1,2048,768]{2,1,0:T(8,128)(2,1)}), bf16[1,512,768]{2,1,0:T(8,128)(2,1)}) %reduce-scatter.3.cloned.1.call-update) | async-done | bytes 786448 | tf_op jit(solution)/shard_map/reduce_scatter | solution.py:152
  237.1 3.9 %subtract_convert_fusion = (bf16[1,512,768]{2,1,0:T(8,128)(2,1)}, f32[1,512,768]{2,1,0:T(8,128)}, f32[1,512,768]{2,1,0:T(8,128)}) fusion(bf16[1,2048,768]{2,1,0:T(8,128)(2,1)} %param.14, s32[]{:T(128)S(6)} %select_n.14, bf16[1,512,768]{2,1,0:T(8,128)(2,1)} %reduce-scatter.3.cloned.1.call-done, f32[1,512,768]{2,1,0:T(8,128)S(1)} %copy-done.9, ...), kind=kLoop, calls=%fused_computation.32 | loop fusion | flops 5505024 | bytes 8650756 | tf_op jit(solution)/shard_map/convert_element_type | solution.py:48
  241.0 0.0 all-gather.7.cloned.1.call-update
  241.1 0.1 fusion.33
  241.2 24.4 %all-gather.9.cloned.1.call-done = bf16[1,384,2048]{2,1,0:T(8,128)(2,1)} async-done(((bf16[1,384,512]{2,1,0:T(8,128)(2,1)}), bf16[1,384,2048]{2,1,0:T(8,128)(2,1)}) %all-gather.9.cloned.1.call-update) | async-done | bytes 1572880 | tf_op jit(solution)/shard_map/all_gather | solution.py:169
  265.6 90.9 %all-to-all-done = bf16[32,72,2048]{2,1,0:T(8,128)(2,1)} async-done(((bf16[32,72,2048]{2,1,0:T(8,128)(2,1)}), bf16[32,72,2048]{2,1,0:T(8,128)(2,1)}, u32[]{:S(2)}, u32[]{:S(2)}) %all-to-all-start) | async-done | bytes 9437216 | tf_op jit(solution)/shard_map/all_to_all | solution.py:130
  356.5 6.0 %fusion.5 = bf16[128,2048]{1,0:T(8,128)(2,1)} fusion(bf16[32,72,2048]{2,1,0:T(8,128)(2,1)} %all-to-all-done, f32[128,32]{0,1:T(8,128)S(1)} %fusion.33, pred[128,32]{0,1:T(8,128)(4,1)S(1)} %convert_compare_fusion.1), kind=kOutput, calls=%fused_computation.18 | convolution fusion | flops 1208811520 | bytes 9981952 | tf_op jit(solution)/shard_map/dot_general | solution.py:147
  362.5 3.9 %copy.28 = bf16[1,2048,768]{2,1,0:T(8,128)(2,1)} copy(bf16[1,2048,768]{2,1,0:T(8,128)(2,1)} %all-gather.7.cloned.1.call-done) | data formatting | bytes 6291456
  366.4 1.1 copy.29
  (40 shorter events, 0.1 us)
Async XLA Ops:
  7.2 99.8 %copy-start.12 = (bf16[128,2048]{1,0:T(8,128)(2,1)S(1)}, bf16[128,2048]{1,0:T(8,128)(2,1)}, u32[]{:S(2)}) copy-start(bf16[128,2048]{1,0:T(8,128)(2,1)} %param.11) | copy-start | bytes 1572868
  7.2 99.8 %all-gather.11.cloned.1.call-start = ((), (), s32[]{:S(2)}) async-start(), calls=%async_computation.7 | async-start | bytes 27033600 | tf_op jit(solution)/shard_map/all_gather | solution.py:87
  11.8 150.5 %all-gather.13.cloned.1.call-start = ((), (), s32[]{:S(2)}) async-start(), calls=%async_computation.8 | async-start | bytes 8650752 | tf_op jit(solution)/shard_map/all_gather | solution.py:91
  107.7 103.7 %reduce-scatter.5.cloned.1.call-start = ((), (), s32[]{:S(2)}) async-start(), calls=%async_computation.5 | async-start | bytes 1966080 | tf_op jit(solution)/shard_map/reduce_scatter | solution.py:155
  112.8 0.6 copy-start.15
  128.9 9.5 %copy-start.13 = (bf16[1,2048,768]{2,1,0:T(8,128)(2,1)S(1)}, bf16[1,2048,768]{2,1,0:T(8,128)(2,1)}, u32[]{:S(2)}) copy-start(bf16[1,2048,768]{2,1,0:T(8,128)(2,1)} %param.14) | copy-start | bytes 9437188
  148.4 2.9 copy-start.16
  148.4 2.9 copy-start.17
  151.3 4.1 %copy-start.6 = (bf16[2304,384]{0,1:T(8,128)(2,1)}, bf16[2304,384]{0,1:T(8,128)(2,1)S(1)}, u32[]{:S(2)}) copy-start(bf16[2304,384]{0,1:T(8,128)(2,1)S(1)} %get-tuple-element.16) | copy-start | bytes 5308420
  152.0 3.4 copy-start.14
  155.4 2.2 copy-start.5
  162.3 4.9 %copy-start.7 = (bf16[2304,384]{0,1:T(8,128)(2,1)S(1)}, bf16[2304,384]{0,1:T(8,128)(2,1)}, u32[]{:S(2)}) copy-start(bf16[2304,384]{0,1:T(8,128)(2,1)} %copy-done.6) | copy-start | bytes 5308420
  167.2 2.1 copy-start
  167.3 2.1 copy-start.11
  170.7 66.4 %reduce-scatter.3.cloned.1.call-start = ((), (), s32[]{:S(2)}) async-start(), calls=%async_computation.3 | async-start | bytes 3932160 | tf_op jit(solution)/shard_map/reduce_scatter | solution.py:152
  170.7 4.8 %slice-start = ((s8[4718592]{0:T(1024)(128)(4,1)}), s8[4194304]{0:T(1024)(128)(4,1)S(1)}, s32[]{:S(2)}) async-start(s8[4718592]{0:T(1024)(128)(4,1)} %bitcast.34), calls=%async_computation.9 | async-start | bytes 8388608
  170.7 4.8 %slice-start.1 = ((s8[4718592]{0:T(1024)(128)(4,1)}), s8[524288]{0:T(1024)(128)(4,1)S(1)}, s32[]{:S(2)}) async-start(s8[4718592]{0:T(1024)(128)(4,1)} %bitcast.34), calls=%async_computation.10 | async-start | bytes 1048576
  170.7 5.1 %copy-start.1 = (f32[2304,384]{0,1:T(8,128)S(1)}, f32[2304,384]{0,1:T(8,128)}, u32[]{:S(2)}) copy-start(f32[2304,384]{0,1:T(8,128)} %get-tuple-element.14) | copy-start | bytes 10616836
  170.7 10.6 %slice-start.2 = ((s8[9437184]{0:T(1024)(128)(4,1)}), s8[4194304]{0:T(1024)(128)(4,1)S(1)}, s32[]{:S(2)}) async-start(s8[9437184]{0:T(1024)(128)(4,1)} %bitcast.41), calls=%async_computation.11 | async-start | bytes 8388608
  175.8 5.5 %slice-start.3 = ((s8[9437184]{0:T(1024)(128)(4,1)}), s8[4194304]{0:T(1024)(128)(4,1)S(1)}, s32[]{:S(2)}) async-start(s8[9437184]{0:T(1024)(128)(4,1)} %bitcast.41), calls=%async_computation.12 | async-start | bytes 8388608
  175.8 5.5 %slice-start.4 = ((s8[9437184]{0:T(1024)(128)(4,1)}), s8[1048576]{0:T(1024)(128)(4,1)S(1)}, s32[]{:S(2)}) async-start(s8[9437184]{0:T(1024)(128)(4,1)} %bitcast.41), calls=%async_computation.13 | async-start | bytes 2097152
  179.5 1.3 copy-start.2
  179.5 1.8 copy-start.4
  190.5 1.5 copy-start.3
  204.1 152.4 %all-to-all-start = ((bf16[32,72,2048]{2,1,0:T(8,128)(2,1)}), bf16[32,72,2048]{2,1,0:T(8,128)(2,1)}, u32[]{:S(2)}, u32[]{:S(2)}) async-start(bf16[32,72,2048]{2,1,0:T(8,128)(2,1)} %bitcast.39), calls=%async_computation | async-start | bytes 18874368 | tf_op jit(solution)/shard_map/all_to_all | solution.py:130
  211.3 25.8 %copy-start.9 = (f32[1,512,768]{2,1,0:T(8,128)S(1)}, f32[1,512,768]{2,1,0:T(8,128)}, u32[]{:S(2)}) copy-start(f32[1,512,768]{2,1,0:T(8,128)} %param.16) | copy-start | bytes 4718596
  211.3 25.8 %copy-start.10 = (f32[1,512,768]{2,1,0:T(8,128)S(1)}, f32[1,512,768]{2,1,0:T(8,128)}, u32[]{:S(2)}) copy-start(f32[1,512,768]{2,1,0:T(8,128)} %param.17) | copy-start | bytes 4718596
  211.3 54.3 %all-gather.9.cloned.1.call-start = ((), (), s32[]{:S(2)}) async-start(), calls=%async_computation.6 | async-start | bytes 1966080 | tf_op jit(solution)/shard_map/all_gather | solution.py:169
  214.8 26.2 %copy-start.18 = (s32[128,8]{0,1:T(8,128)S(1)}, s32[128,8]{0,1:T(8,128)}, u32[]{:S(2)}) copy-start(s32[128,8]{0,1:T(8,128)} %param.13) | copy-start | bytes 12292
  214.8 147.7 %all-gather.7.cloned.1.call-start = ((), (), s32[]{:S(2)}) async-start(), calls=%async_computation.4 | async-start | bytes 3932160 | tf_op jit(solution)/shard_map/all_gather | solution.py:168
  362.5 3.9 %copy-start.8 = (bf16[1,384,2048]{2,1,0:T(8,128)(2,1)S(1)}, bf16[1,384,2048]{2,1,0:T(8,128)(2,1)}, u32[]{:S(2)}) copy-start(bf16[1,384,2048]{2,1,0:T(8,128)(2,1)} %all-gather.9.cloned.1.call-done) | copy-start | bytes 4718596
Sparse Core Ops, SparseCore 0:
  11.9 94.9 all-gather.10
  109.8 52.5 all-gather.12
  170.8 25.2 reduce-scatter.4
  198.9 38.1 reduce-scatter.2
  239.2 26.4 all-gather.8
  267.7 39.8 all-gather.6

commit v6 on v5

--- a/solution.py
+++ b/solution.py
@@ -104,10 +104,12 @@
     slots = jnp.arange(capacity, dtype=jnp.float32)
     pick = (routed[:, None, :] > 0) & (rank[:, None, :] == slots[None, :, None])
     pick_b = pick.astype(jnp.bfloat16)
-    picked_first = jnp.einsum(
-        "srt,stc->src", pick_b, first, preferred_element_type=jnp.float32
-    ).astype(jnp.bfloat16)
-    inputs = picked_first[..., :model_width]
+    inputs = jnp.einsum(
+        "srt,stc->src", pick_b, first[..., :model_width], preferred_element_type=jnp.float32
+    ).astype(jnp.bfloat16)
+    picked_lo = jnp.einsum(
+        "srt,stc->src", pick_b, first[..., model_width:meta_at], preferred_element_type=jnp.float32
+    ).astype(jnp.bfloat16)
     slot_gate = jnp.sum(jnp.where(pick, gate_of[:, None, :], 0.0), axis=-1)
     picked_hi = jnp.einsum(
         "srt,stc->src", pick_b, cot_hi, preferred_element_type=jnp.float32
@@ -116,7 +118,7 @@
         (slot_gate[..., None] * part.astype(jnp.float32))
         .astype(jnp.bfloat16)
         .reshape(slot_total, half_width)
-        for part in (picked_first[..., model_width:meta_at], picked_hi)
+        for part in (picked_lo, picked_hi)
     ]
 
     weight_pair = gate_up[0]

time: 375 us -> 376 us (level)
  local copies, waits for them, and re-layouts: 22.7 us -> 12.1 us
  waiting for transfers between devices: 234 us -> 244 us
  matrix products: 71.2 us -> 75.6 us
    slice x1 -> x0, local copies, waits for them, and re-layouts: 9.46 us -> none  [local(): inputs = picked_first[..., :model_width]]
    all_gather x1, waiting for transfers between devices: 1.8 us -> 11.2 us  [local(): cot_hi = lax.all_gather(cot_after[:, half_width:], 'expert', axis=0)]
    unnamed x51 -> x47, local copies, waits for them, and re-layouts: 11.6 us -> 10.5 us
    dot_general x1 -> x2, matrix products: 15.5 us -> 14.9 us  [the longest x1 9.42 us: local(): jnp.einsum('srt,stc->src', pick_b, first[..., :model_width], preferred_el...]
  transfers between devices with their start and end apart: 7 -> 7, of which waited for: 5 -> 5; matrix products, arithmetic and copies ran while one was open for 25% -> 23% of each run, Pallas kernels for 0% -> 0%
where the time goes in v6:
time: 376 us
  waiting for transfers between devices  244 us (65%)
  matrix products  75.6 us (20%)
  other arithmetic  22.2 us (6%)
  between operations  14.4 us (4%)
  local copies, waits for them, and re-layouts  12.1 us (3%)
  starting transfers between devices  7.93 us (2%)
    all_gather x1, waiting for transfers between devices, local(): lax.all_gather(jnp.concatenate([tokens, cotangent[:, :half_width], meta],...  95.1 us
    all_to_all x1, waiting for transfers between devices, local(): lax.all_to_all(row_grads.reshape(expert_count, capacity, model_width), 'e...  92.4 us
    all_gather x1, waiting for transfers between devices, local(): lax.all_gather(new_down, 'group', axis=2, tiled=True)  24.4 us
    reduce_scatter x1, waiting for transfers between devices, local(): lax.psum_scatter(grad_pair[None].astype(jnp.bfloat16), 'group', scatter_d...  20.4 us
    dot_general x1, matrix products, expert_backward(): jnp.dot(inputs, weight_gate_up, preferred_element_type=jnp.float32)  13.1 us
    dot_general x1, matrix products, expert_backward(): jnp.dot(pair_grad, weight_gate_up.T, preferred_element_type=jnp.float32)  11.6 us
    all_gather x1, waiting for transfers between devices, local(): cot_hi = lax.all_gather(cot_after[:, half_width:], 'expert', axis=0)  11.2 us
    dot_general x1, matrix products, expert_backward(): jnp.dot(inputs.T, pair_grad, preferred_element_type=jnp.float32)  10.5 us
  transfers between devices with their start and end apart: 7, of which 5 were waited for; matrix products, arithmetic and copies ran while one was open for 23% of the time, Pallas kernels for 0%

profile of v6, /device:TPU:50, one launch (start us, length us, event | category | flops | bytes accessed | tf_op | source)
XLA Modules:
  0.0 375.9 jit_solution(17291748473410603889)
XLA Ops:
  7.2 0.0 copy-start.12
  7.2 0.0 all-gather.11.cloned.1.call-start
  7.2 0.7 convert_convert_fusion.4
  8.0 0.7 reduce-precision_convert_fusion.1
  8.7 0.1 copy.25
  8.8 1.0 slice.39
  9.8 2.0 fusion.29
  11.8 0.0 all-gather.11.cloned.1.call-update
  11.8 0.0 all-gather.13.cloned.1.call-start
  11.8 95.1 %all-gather.11.cloned.1.call-done = bf16[4096,3200]{1,0:T(8,128)(2,1)} async-done(((bf16[128,3200]{1,0:T(8,128)(2,1)}), bf16[4096,3200]{1,0:T(8,128)(2,1)}) %all-gather.11.cloned.1.call-update) | async-done | bytes 26214416 | tf_op jit(solution)/shard_map/all_gather | solution.py:87
  106.9 0.0 copy-done.12
  106.9 0.7 slice.47
  107.7 0.0 all-gather.13.cloned.1.call-update
  107.7 0.0 reduce-scatter.5.cloned.1.call-start
  107.7 1.5 slice_convert_fusion.1
  109.2 0.6 fusion.54
  109.9 0.0 copy-start.15
  109.9 0.1 fusion.44
  110.0 9.4 %fusion.4 = bf16[32,72,2048]{2,1,0:T(8,128)(2,1)} fusion(bf16[32,128,3200]{2,1,0:T(8,128)(2,1)} %bitcast.33, f32[32,128]{1,0:T(8,128)S(1)} %fusion.44, pred[32,128]{1,0:T(8,128)(4,1)S(1)} %convert_compare_fusion), kind=kOutput, calls=%fused_computation.7 | convolution fusion | flops 1213267968 | bytes 26234880 | tf_op jit(solution)/shard_map/srt,stc->src/dot_general | solution.py:107
  119.4 13.1 %fusion.9 = f32[2304,768]{0,1:T(8,128)} fusion(bf16[2304,2048]{1,0:T(8,128)(2,1)} %bitcast.39, bf16[1,2048,768]{2,1,0:T(8,128)(2,1)S(1)} %copy-done.13), kind=kOutput, calls=%fused_computation.18 | convolution fusion | flops 7247757312 | bytes 19660800 | tf_op jit(solution)/shard_map/dot_general | solution.py:15
  132.5 5.1 %fusion.7 = (f32[2304,384]{0,1:T(8,128)S(1)}, f32[2304,384]{0,1:T(8,128)}, bf16[2304,384]{0,1:T(8,128)(2,1)S(1)}) fusion(f32[2304,768]{0,1:T(8,128)} %fusion.9), kind=kLoop, calls=%fused_computation.15 | loop fusion | flops 9732096 | bytes 15925248 | tf_op jit(solution)/shard_map/mul | solution.py:19
  137.7 2.3 fusion.16
  140.0 0.6 select_reduce_fusion
  140.6 0.0 copy-start.14
  140.6 5.5 %multiply_convert_fusion.1 = bf16[32,72,1024]{2,1,0:T(8,128)(2,1)S(1)} fusion(f32[32,72]{1,0:T(8,128)S(1)} %select_reduce_fusion, bf16[32,128,3200]{2,1,0:T(8,128)(2,1)} %bitcast.34, f32[32,128]{1,0:T(8,128)S(1)} %fusion.44, pred[32,128]{1,0:T(8,128)(4,1)S(1)} %convert_compare_fusion), kind=kOutput, calls=%fused_computation.4 | convolution fusion | flops 614006784 | bytes 13136896 | tf_op jit(solution)/shard_map/srt,stc->src/dot_general | solution.py:110
  146.2 2.1 copy-done.5
  148.3 2.9 fusion.21
  151.1 11.2 %all-gather.13.cloned.1.call-done = bf16[4096,1024]{1,0:T(8,128)(2,1)} async-done(((bf16[128,1024]{1,0:T(8,128)(2,1)}), bf16[4096,1024]{1,0:T(8,128)(2,1)}) %all-gather.13.cloned.1.call-update) | async-done | bytes 8388624 | tf_op jit(solution)/shard_map/all_gather | solution.py:91
  162.3 4.9 %multiply_convert_fusion = bf16[32,72,1024]{2,1,0:T(8,128)(2,1)S(1)} fusion(f32[32,72]{1,0:T(8,128)} %copy-done.14, bf16[32,128,1024]{2,1,0:T(8,128)(2,1)} %bitcast.44, f32[32,128]{1,0:T(8,128)S(1)} %fusion.44, pred[32,128]{1,0:T(8,128)(4,1)} %copy-done.15), kind=kOutput, calls=%fused_computation.3 | convolution fusion | flops 614006784 | bytes 13136896 | tf_op jit(solution)/shard_map/srt,stc->src/dot_general | solution.py:114
  167.3 0.0 copy-start.11
  167.3 2.0 fusion.22
  169.3 0.2 copy-done
  169.4 1.2 pad_maximum_fusion.3
  170.7 0.0 reduce-scatter.5.cloned.1.call-update
  170.7 0.3 reduce-scatter.3.cloned.1.call-start
  171.0 0.0 slice-start
  171.0 0.0 slice-start.1
  171.0 0.0 slice-start.2
  171.0 4.7 %fusion.33 = f32[2304,384]{0,1:T(8,128)S(1)} fusion(bf16[2304,1024]{1,0:T(8,128)(2,1)} %bitcast.46, bf16[384,2048]{1,0:T(8,128)(2,1)} %bitcast.47), kind=kOutput, calls=%fused_computation.53 | convolution fusion | flops 1811939328 | bytes 9043968 | tf_op jit(solution)/shard_map/dot_general | solution.py:22
  175.8 0.3 copy-done.1
  176.1 4.7 %multiply_convert_fusion.3 = (bf16[2304,384]{0,1:T(8,128)(2,1)S(1)}, bf16[2304,384]{0,1:T(8,128)(2,1)}) fusion(f32[2304,384]{0,1:T(8,128)S(1)} %copy-done.1, f32[2304,384]{0,1:T(8,128)S(1)} %get-tuple-element.15, f32[2304,384]{0,1:T(8,128)S(1)} %fusion.33, bf16[2304,1024]{1,0:T(8,128)(2,1)S(1)} %bitcast.38, bf16[384,2048]{1,0:T(8,128)(2,1)} %bitcast.48), kind=kOutput, calls=%fused_computation.11 | convolution fusion | flops 1816363008 | bytes 19660800 | tf_op jit(solution)/shard_map/dot_general | solution.py:22
  180.8 1.2 copy-done.2
  182.0 10.5 %fusion.11 = bf16[1,2048,768]{2,1,0:T(8,128)(2,1)} fusion(bf16[2304,2048]{1,0:T(8,128)(2,1)S(1)} %bitcast.42, bf16[2304,384]{0,1:T(8,128)(2,1)} %get-tuple-element.29, bf16[2304,384]{0,1:T(8,128)(2,1)S(1)} %get-tuple-element.28), kind=kOutput, calls=%fused_computation.20 | convolution fusion | flops 7256408064 | bytes 16121856 | tf_op jit(solution)/shard_map/dot_general | solution.py:36
  192.5 0.0 reduce-scatter.3.cloned.1.call-update
  192.6 1.5 copy-done.3
  194.0 11.6 %convolution_convert_fusion = bf16[2304,2048]{1,0:T(8,128)(2,1)} fusion(bf16[1,2048,768]{2,1,0:T(8,128)(2,1)} %param.14, bf16[2304,384]{0,1:T(8,128)(2,1)S(1)} %copy-done.4, bf16[2304,384]{0,1:T(8,128)(2,1)S(1)} %copy-done.3), kind=kOutput, calls=%fused_computation.2 | convolution fusion | flops 7259553792 | bytes 16121856 | tf_op jit(solution)/shard_map/dot_general | solution.py:37
  205.6 7.2 %all-to-all-start = ((bf16[32,72,2048]{2,1,0:T(8,128)(2,1)}), bf16[32,72,2048]{2,1,0:T(8,128)(2,1)}, u32[]{:S(2)}, u32[]{:S(2)}) async-start(bf16[32,72,2048]{2,1,0:T(8,128)(2,1)} %bitcast.43), calls=%async_computation | async-start | bytes 18874368 | tf_op jit(solution)/shard_map/all_to_all | solution.py:132
  212.8 0.0 copy-start.9
  212.9 0.0 copy-start.10
  212.9 0.0 all-gather.9.cloned.1.call-start
  212.9 0.0 reduce-scatter.5.cloned.1.call-done
  212.9 3.4 subtract_convert_fusion.1
  216.3 0.0 all-gather.9.cloned.1.call-update
  216.4 0.0 copy-start.16
  216.4 0.3 all-gather.7.cloned.1.call-start
  216.7 20.4 %reduce-scatter.3.cloned.1.call-done = bf16[1,512,768]{2,1,0:T(8,128)(2,1)} async-done(((bf16[1,2048,768]{2,1,0:T(8,128)(2,1)}), bf16[1,512,768]{2,1,0:T(8,128)(2,1)}) %reduce-scatter.3.cloned.1.call-update) | async-done | bytes 786448 | tf_op jit(solution)/shard_map/reduce_scatter | solution.py:154
  237.1 3.9 %subtract_convert_fusion = (bf16[1,512,768]{2,1,0:T(8,128)(2,1)}, f32[1,512,768]{2,1,0:T(8,128)}, f32[1,512,768]{2,1,0:T(8,128)}) fusion(bf16[1,2048,768]{2,1,0:T(8,128)(2,1)} %param.14, s32[]{:T(128)S(6)} %select_n.14, bf16[1,512,768]{2,1,0:T(8,128)(2,1)} %reduce-scatter.3.cloned.1.call-done, f32[1,512,768]{2,1,0:T(8,128)S(1)} %copy-done.9, ...), kind=kLoop, calls=%fused_computation.36 | loop fusion | flops 5505024 | bytes 8650756 | tf_op jit(solution)/shard_map/convert_element_type | solution.py:48
  241.0 0.0 all-gather.7.cloned.1.call-update
  241.1 0.1 fusion.45
  241.2 24.4 %all-gather.9.cloned.1.call-done = bf16[1,384,2048]{2,1,0:T(8,128)(2,1)} async-done(((bf16[1,384,512]{2,1,0:T(8,128)(2,1)}), bf16[1,384,2048]{2,1,0:T(8,128)(2,1)}) %all-gather.9.cloned.1.call-update) | async-done | bytes 1572880 | tf_op jit(solution)/shard_map/all_gather | solution.py:171
  265.7 92.4 %all-to-all-done = bf16[32,72,2048]{2,1,0:T(8,128)(2,1)} async-done(((bf16[32,72,2048]{2,1,0:T(8,128)(2,1)}), bf16[32,72,2048]{2,1,0:T(8,128)(2,1)}, u32[]{:S(2)}, u32[]{:S(2)}) %all-to-all-start) | async-done | bytes 9437216 | tf_op jit(solution)/shard_map/all_to_all | solution.py:132
  358.1 6.0 %fusion.14 = bf16[128,2048]{1,0:T(8,128)(2,1)} fusion(bf16[32,72,2048]{2,1,0:T(8,128)(2,1)} %all-to-all-done, f32[128,32]{0,1:T(8,128)S(1)} %fusion.45, pred[128,32]{0,1:T(8,128)(4,1)S(1)} %convert_compare_fusion.1), kind=kOutput, calls=%fused_computation.22 | convolution fusion | flops 1208811520 | bytes 9981952 | tf_op jit(solution)/shard_map/dot_general | solution.py:149
  364.0 3.9 %copy.28 = bf16[1,2048,768]{2,1,0:T(8,128)(2,1)} copy(bf16[1,2048,768]{2,1,0:T(8,128)(2,1)} %all-gather.7.cloned.1.call-done) | data formatting | bytes 6291456
  367.9 1.1 copy.29
  (35 shorter events, 0.1 us)
Async XLA Ops:
  7.2 99.8 %copy-start.12 = (bf16[128,2048]{1,0:T(8,128)(2,1)S(1)}, bf16[128,2048]{1,0:T(8,128)(2,1)}, u32[]{:S(2)}) copy-start(bf16[128,2048]{1,0:T(8,128)(2,1)} %param.11) | copy-start | bytes 1572868
  7.2 99.8 %all-gather.11.cloned.1.call-start = ((), (), s32[]{:S(2)}) async-start(), calls=%async_computation.7 | async-start | bytes 27033600 | tf_op jit(solution)/shard_map/all_gather | solution.py:87
  11.8 150.5 %all-gather.13.cloned.1.call-start = ((), (), s32[]{:S(2)}) async-start(), calls=%async_computation.8 | async-start | bytes 8650752 | tf_op jit(solution)/shard_map/all_gather | solution.py:91
  107.7 105.2 %reduce-scatter.5.cloned.1.call-start = ((), (), s32[]{:S(2)}) async-start(), calls=%async_computation.5 | async-start | bytes 1966080 | tf_op jit(solution)/shard_map/reduce_scatter | solution.py:157
  109.9 30.8 %copy-start.15 = (pred[32,128]{1,0:T(8,128)(4,1)}, pred[32,128]{1,0:T(8,128)(4,1)S(1)}, u32[]{:S(2)}) copy-start(pred[32,128]{1,0:T(8,128)(4,1)S(1)} %convert_compare_fusion) | copy-start | bytes 12292
  110.0 9.4 %copy-start.13 = (bf16[1,2048,768]{2,1,0:T(8,128)(2,1)S(1)}, bf16[1,2048,768]{2,1,0:T(8,128)(2,1)}, u32[]{:S(2)}) copy-start(bf16[1,2048,768]{2,1,0:T(8,128)(2,1)} %param.14) | copy-start | bytes 9437188
  137.7 8.4 %copy-start.6 = (bf16[2304,384]{0,1:T(8,128)(2,1)}, bf16[2304,384]{0,1:T(8,128)(2,1)S(1)}, u32[]{:S(2)}) copy-start(bf16[2304,384]{0,1:T(8,128)(2,1)S(1)} %get-tuple-element.16) | copy-start | bytes 5308420
  140.6 5.5 %copy-start.14 = (f32[32,72]{1,0:T(8,128)}, f32[32,72]{1,0:T(8,128)S(1)}, u32[]{:S(2)}) copy-start(f32[32,72]{1,0:T(8,128)S(1)} %select_reduce_fusion) | copy-start | bytes 27652
  146.1 2.1 copy-start.5
  162.3 4.9 %copy-start.7 = (bf16[2304,384]{0,1:T(8,128)(2,1)S(1)}, bf16[2304,384]{0,1:T(8,128)(2,1)}, u32[]{:S(2)}) copy-start(bf16[2304,384]{0,1:T(8,128)(2,1)} %copy-done.6) | copy-start | bytes 5308420
  167.2 2.2 copy-start
  167.3 2.2 copy-start.11
  170.7 66.4 %reduce-scatter.3.cloned.1.call-start = ((), (), s32[]{:S(2)}) async-start(), calls=%async_computation.3 | async-start | bytes 3932160 | tf_op jit(solution)/shard_map/reduce_scatter | solution.py:154
  171.0 4.8 %slice-start = ((s8[4718592]{0:T(1024)(128)(4,1)}), s8[4194304]{0:T(1024)(128)(4,1)S(1)}, s32[]{:S(2)}) async-start(s8[4718592]{0:T(1024)(128)(4,1)} %bitcast.36), calls=%async_computation.9 | async-start | bytes 8388608
  171.0 4.8 %slice-start.1 = ((s8[4718592]{0:T(1024)(128)(4,1)}), s8[524288]{0:T(1024)(128)(4,1)S(1)}, s32[]{:S(2)}) async-start(s8[4718592]{0:T(1024)(128)(4,1)} %bitcast.36), calls=%async_computation.10 | async-start | bytes 1048576
  171.0 5.1 %copy-start.1 = (f32[2304,384]{0,1:T(8,128)S(1)}, f32[2304,384]{0,1:T(8,128)}, u32[]{:S(2)}) copy-start(f32[2304,384]{0,1:T(8,128)} %get-tuple-element.14) | copy-start | bytes 10616836
  171.0 11.0 %slice-start.2 = ((s8[9437184]{0:T(1024)(128)(4,1)}), s8[4194304]{0:T(1024)(128)(4,1)S(1)}, s32[]{:S(2)}) async-start(s8[9437184]{0:T(1024)(128)(4,1)} %bitcast.40), calls=%async_computation.11 | async-start | bytes 8388608
  176.1 5.9 %slice-start.3 = ((s8[9437184]{0:T(1024)(128)(4,1)}), s8[4194304]{0:T(1024)(128)(4,1)S(1)}, s32[]{:S(2)}) async-start(s8[9437184]{0:T(1024)(128)(4,1)} %bitcast.40), calls=%async_computation.12 | async-start | bytes 8388608
  176.1 5.9 %slice-start.4 = ((s8[9437184]{0:T(1024)(128)(4,1)}), s8[1048576]{0:T(1024)(128)(4,1)S(1)}, s32[]{:S(2)}) async-start(s8[9437184]{0:T(1024)(128)(4,1)} %bitcast.40), calls=%async_computation.13 | async-start | bytes 2097152
  180.8 1.2 copy-start.2
  182.0 10.6 %copy-start.4 = (bf16[2304,384]{0,1:T(8,128)(2,1)S(1)}, bf16[2304,384]{0,1:T(8,128)(2,1)}, u32[]{:S(2)}) copy-start(bf16[2304,384]{0,1:T(8,128)(2,1)} %get-tuple-element.29) | copy-start | bytes 5308420
  192.5 1.5 copy-start.3
  205.6 152.4 %all-to-all-start = ((bf16[32,72,2048]{2,1,0:T(8,128)(2,1)}), bf16[32,72,2048]{2,1,0:T(8,128)(2,1)}, u32[]{:S(2)}, u32[]{:S(2)}) async-start(bf16[32,72,2048]{2,1,0:T(8,128)(2,1)} %bitcast.43), calls=%async_computation | async-start | bytes 18874368 | tf_op jit(solution)/shard_map/all_to_all | solution.py:132
  212.8 24.3 %copy-start.9 = (f32[1,512,768]{2,1,0:T(8,128)S(1)}, f32[1,512,768]{2,1,0:T(8,128)}, u32[]{:S(2)}) copy-start(f32[1,512,768]{2,1,0:T(8,128)} %param.16) | copy-start | bytes 4718596
  212.9 24.3 %copy-start.10 = (f32[1,512,768]{2,1,0:T(8,128)S(1)}, f32[1,512,768]{2,1,0:T(8,128)}, u32[]{:S(2)}) copy-start(f32[1,512,768]{2,1,0:T(8,128)} %param.17) | copy-start | bytes 4718596
  212.9 52.8 %all-gather.9.cloned.1.call-start = ((), (), s32[]{:S(2)}) async-start(), calls=%async_computation.6 | async-start | bytes 1966080 | tf_op jit(solution)/shard_map/all_gather | solution.py:171
  216.4 24.7 %copy-start.16 = (s32[128,8]{0,1:T(8,128)S(1)}, s32[128,8]{0,1:T(8,128)}, u32[]{:S(2)}) copy-start(s32[128,8]{0,1:T(8,128)} %param.13) | copy-start | bytes 12292
  216.4 147.7 %all-gather.7.cloned.1.call-start = ((), (), s32[]{:S(2)}) async-start(), calls=%async_computation.4 | async-start | bytes 3932160 | tf_op jit(solution)/shard_map/all_gather | solution.py:170
  364.0 3.9 %copy-start.8 = (bf16[1,384,2048]{2,1,0:T(8,128)(2,1)S(1)}, bf16[1,384,2048]{2,1,0:T(8,128)(2,1)}, u32[]{:S(2)}) copy-start(bf16[1,384,2048]{2,1,0:T(8,128)(2,1)} %all-gather.9.cloned.1.call-done) | copy-start | bytes 4718596
Sparse Core Ops, SparseCore 0:
  11.9 94.9 all-gather.10
  109.8 52.5 all-gather.12
  170.8 25.2 reduce-scatter.4
  199.0 38.0 reduce-scatter.2
  239.2 26.4 all-gather.8
  267.8 39.8 all-gather.6

commit v7 on v6

--- a/solution.py
+++ b/solution.py
@@ -11,7 +11,9 @@
 
 def expert_backward(inputs, scaled_parts, weight_gate_up, weight_down):
     hidden_count = weight_down.shape[0]
-    width = scaled_parts[0].shape[1]
+    offsets = [0]
+    for part in scaled_parts:
+        offsets.append(offsets[-1] + part.shape[1])
     projected = jnp.dot(inputs, weight_gate_up, preferred_element_type=jnp.float32)
     gate_part = projected[:, :hidden_count]
     up_part = projected[:, hidden_count:]
@@ -19,7 +21,7 @@
     activated = gate_part * sigmoid_gate
     hidden_act = (activated * up_part).astype(jnp.bfloat16)
     hidden_grad = sum(
-        jnp.dot(part, weight_down[:, i * width : (i + 1) * width].T, preferred_element_type=jnp.float32)
+        jnp.dot(part, weight_down[:, offsets[i] : offsets[i + 1]].T, preferred_element_type=jnp.float32)
         for i, part in enumerate(scaled_parts)
     )
     slope = sigmoid_gate * (1.0 + gate_part * (1.0 - sigmoid_gate))
@@ -74,7 +76,7 @@
     capacity = min(local_tokens, 9 * local_tokens * top_count // (4 * expert_count))
     slot_total = expert_count * capacity
 
-    half_width = model_width // 2
+    half_width = model_width * 3 // 4
     pieces = []
     rest = gate_probs
     for _ in range(3):
@@ -117,7 +119,7 @@
     scaled = [
         (slot_gate[..., None] * part.astype(jnp.float32))
         .astype(jnp.bfloat16)
-        .reshape(slot_total, half_width)
+        .reshape(slot_total, part.shape[-1])
         for part in (picked_lo, picked_hi)
     ]
 

time: 376 us -> 377 us (level)
    all_gather x1, waiting for transfers between devices: 95.1 us -> 106 us  [local(): lax.all_gather(jnp.concatenate([tokens, cotangent[:, :half_width], meta],...]
    all_gather x1, waiting for transfers between devices: 11.2 us -> 1.19 us  [local(): cot_hi = lax.all_gather(cot_after[:, half_width:], 'expert', axis=0)]
    unnamed x47 -> x43, local copies, waits for them, and re-layouts: 10.5 us -> 12.3 us
where the time goes in v7:
time: 377 us
  waiting for transfers between devices  245 us (65%)
  matrix products  72.7 us (19%)
  other arithmetic  22.2 us (6%)
  local copies, waits for them, and re-layouts  14.9 us (4%)
  between operations  14.4 us (4%)
  starting transfers between devices  7.88 us (2%)
    all_gather x1, waiting for transfers between devices, local(): lax.all_gather(jnp.concatenate([tokens, cotangent[:, :half_width], meta],...  106 us
    all_to_all x1, waiting for transfers between devices, local(): lax.all_to_all(row_grads.reshape(expert_count, capacity, model_width), 'e...  90.9 us
    all_gather x1, waiting for transfers between devices, local(): lax.all_gather(new_down, 'group', axis=2, tiled=True)  24.5 us
    reduce_scatter x1, waiting for transfers between devices, local(): lax.psum_scatter(grad_pair[None].astype(jnp.bfloat16), 'group', scatter_d...  22 us
    dot_general x1, matrix products, expert_backward(): jnp.dot(inputs, weight_gate_up, preferred_element_type=jnp.float32)  12.8 us
    unnamed x43, local copies, waits for them, and re-layouts  12.3 us
    dot_general x1, matrix products, expert_backward(): jnp.dot(pair_grad, weight_gate_up.T, preferred_element_type=jnp.float32)  12.1 us
    dot_general x1, matrix products, local(): jnp.einsum('srt,stc->src', pick_b, first[..., :model_width], preferred_el...  9.44 us
  transfers between devices with their start and end apart: 7, of which 5 were waited for; matrix products, arithmetic and copies ran while one was open for 23% of the time, Pallas kernels for 0%

profile of v7, /device:TPU:50, one launch (start us, length us, event | category | flops | bytes accessed | tf_op | source)
XLA Modules:
  0.0 376.8 jit_solution(747245387949996020)
XLA Ops:
  7.2 0.0 all-gather.11.cloned.1.call-start
  7.2 0.7 convert_convert_fusion.4
  7.9 0.7 reduce-precision_convert_fusion.1
  8.6 0.1 copy.25
  8.7 1.0 slice.39
  9.8 2.0 fusion.31
  11.8 0.0 all-gather.11.cloned.1.call-update
  11.8 0.0 all-gather.13.cloned.1.call-start
  11.9 106.0 %all-gather.11.cloned.1.call-done = bf16[4096,3712]{1,0:T(8,128)(2,1)} async-done(((bf16[128,3712]{1,0:T(8,128)(2,1)}), bf16[4096,3712]{1,0:T(8,128)(2,1)}) %all-gather.11.cloned.1.call-update) | async-done | bytes 30408720 | tf_op jit(solution)/shard_map/all_gather | solution.py:89
  117.8 1.6 slice.47
  119.4 0.0 all-gather.13.cloned.1.call-update
  119.4 0.0 reduce-scatter.5.cloned.1.call-start
  119.5 1.5 slice_convert_fusion.1
  121.0 0.6 fusion.54
  121.6 0.0 copy-start.14
  121.6 0.1 fusion.44
  121.8 9.4 %fusion.6 = bf16[32,72,2048]{2,1,0:T(8,128)(2,1)} fusion(bf16[32,128,3712]{2,1,0:T(8,128)(2,1)} %bitcast.33, f32[32,128]{1,0:T(8,128)S(1)} %fusion.44, pred[32,128]{1,0:T(8,128)(4,1)S(1)} %convert_compare_fusion), kind=kOutput, calls=%fused_computation.6 | convolution fusion | flops 1213267968 | bytes 26234880 | tf_op jit(solution)/shard_map/srt,stc->src/dot_general | solution.py:109
  131.2 12.8 %fusion.11 = f32[2304,768]{0,1:T(8,128)} fusion(bf16[2304,2048]{1,0:T(8,128)(2,1)} %bitcast.35, bf16[1,2048,768]{2,1,0:T(8,128)(2,1)S(1)} %copy-done.15), kind=kOutput, calls=%fused_computation.18 | convolution fusion | flops 7247757312 | bytes 19660800 | tf_op jit(solution)/shard_map/dot_general | solution.py:17
  144.0 5.1 %fusion.9 = (f32[2304,384]{0,1:T(8,128)S(1)}, f32[2304,384]{0,1:T(8,128)}, bf16[2304,384]{0,1:T(8,128)(2,1)S(1)}) fusion(f32[2304,768]{0,1:T(8,128)} %fusion.11), kind=kLoop, calls=%fused_computation.15 | loop fusion | flops 9732096 | bytes 15925248 | tf_op jit(solution)/shard_map/mul | solution.py:21
  149.2 2.3 fusion.17
  151.4 0.6 select_reduce_fusion
  152.1 0.0 copy-start.13
  152.1 6.1 %multiply_convert_fusion = bf16[32,72,1536]{2,1,0:T(8,128)(2,1)S(1)} fusion(f32[32,72]{1,0:T(8,128)S(1)} %select_reduce_fusion, bf16[32,128,3712]{2,1,0:T(8,128)(2,1)} %bitcast.34, f32[32,128]{1,0:T(8,128)S(1)} %fusion.44, pred[32,128]{1,0:T(8,128)(4,1)S(1)} %convert_compare_fusion), kind=kOutput, calls=%fused_computation.2 | convolution fusion | flops 920715264 | bytes 19690496 | tf_op jit(solution)/shard_map/srt,stc->src/dot_general | solution.py:112
  158.2 2.8 copy-done
  161.1 3.9 %fusion.14 = bf16[1,384,1536]{2,1,0:T(8,128)(2,1)} fusion(bf16[2304,384]{0,1:T(8,128)(2,1)S(1)} %get-tuple-element.16, bf16[2304,1536]{1,0:T(8,128)(2,1)S(1)} %bitcast.39), kind=kOutput, calls=%fused_computation.22 | convolution fusion | flops 2718498816 | bytes 10027008 | tf_op jit(solution)/shard_map/dot_general | solution.py:35
  165.0 1.2 all-gather.13.cloned.1.call-done
  166.2 3.1 multiply_convert_fusion.1
  169.3 0.0 copy-start.2
  169.3 0.0 copy-start.12
  169.4 1.1 fusion.22
  170.4 0.3 copy-done.2
  170.7 0.7 copy-done.12
  171.5 1.4 pad_maximum_fusion.3
  172.8 0.0 reduce-scatter.5.cloned.1.call-update
  172.9 0.0 reduce-scatter.3.cloned.1.call-start
  172.9 0.0 copy-start.3
  172.9 0.0 slice-start
  172.9 0.0 slice-start.1
  173.0 5.9 %fusion.23 = f32[2304,384]{0,1:T(8,128)S(1)} fusion(bf16[2304,1536]{1,0:T(8,128)(2,1)} %bitcast.40, bf16[384,2048]{1,0:T(8,128)(2,1)} %bitcast.45), kind=kOutput, calls=%fused_computation.42 | convolution fusion | flops 2717908992 | bytes 11796480 | tf_op jit(solution)/shard_map/dot_general | solution.py:24
  178.9 3.1 multiply_convert_fusion.3
  182.0 1.2 copy-done.4
  183.2 0.6 copy-done.6
  183.8 8.9 %fusion.13 = bf16[1,2048,768]{2,1,0:T(8,128)(2,1)} fusion(bf16[2304,2048]{1,0:T(8,128)(2,1)S(1)} %bitcast.38, bf16[2304,384]{0,1:T(8,128)(2,1)S(1)} %get-tuple-element.29, bf16[2304,384]{0,1:T(8,128)(2,1)S(1)} %get-tuple-element.28), kind=kOutput, calls=%fused_computation.20 | convolution fusion | flops 7256408064 | bytes 16121856 | tf_op jit(solution)/shard_map/dot_general | solution.py:38
  192.7 0.0 reduce-scatter.3.cloned.1.call-update
  192.8 1.5 copy-done.5
  194.2 12.1 %convolution_convert_fusion = bf16[2304,2048]{1,0:T(8,128)(2,1)} fusion(bf16[1,2048,768]{2,1,0:T(8,128)(2,1)} %param.14, bf16[2304,384]{0,1:T(8,128)(2,1)} %copy-done.6, bf16[2304,384]{0,1:T(8,128)(2,1)S(1)} %copy-done.5), kind=kOutput, calls=%fused_computation.5 | convolution fusion | flops 7259553792 | bytes 16121856 | tf_op jit(solution)/shard_map/dot_general | solution.py:39
  206.3 7.4 %all-to-all-start = ((bf16[32,72,2048]{2,1,0:T(8,128)(2,1)}), bf16[32,72,2048]{2,1,0:T(8,128)(2,1)}, u32[]{:S(2)}, u32[]{:S(2)}) async-start(bf16[32,72,2048]{2,1,0:T(8,128)(2,1)} %bitcast.41), calls=%async_computation | async-start | bytes 18874368 | tf_op jit(solution)/shard_map/all_to_all | solution.py:134
  213.7 0.0 all-gather.9.cloned.1.call-start
  213.8 0.0 copy-start.10
  213.8 0.0 copy-start.11
  213.8 0.0 reduce-scatter.5.cloned.1.call-done
  213.8 3.4 subtract_convert_fusion.1
  217.2 0.0 all-gather.9.cloned.1.call-update
  217.2 0.0 copy-start.16
  217.2 0.3 all-gather.7.cloned.1.call-start
  217.5 22.0 %reduce-scatter.3.cloned.1.call-done = bf16[1,512,768]{2,1,0:T(8,128)(2,1)} async-done(((bf16[1,2048,768]{2,1,0:T(8,128)(2,1)}), bf16[1,512,768]{2,1,0:T(8,128)(2,1)}) %reduce-scatter.3.cloned.1.call-update) | async-done | bytes 786448 | tf_op jit(solution)/shard_map/reduce_scatter | solution.py:156
  239.5 3.9 %subtract_convert_fusion = (bf16[1,512,768]{2,1,0:T(8,128)(2,1)}, f32[1,512,768]{2,1,0:T(8,128)}, f32[1,512,768]{2,1,0:T(8,128)}) fusion(bf16[1,2048,768]{2,1,0:T(8,128)(2,1)} %param.14, s32[]{:T(128)S(6)} %select_n.14, bf16[1,512,768]{2,1,0:T(8,128)(2,1)} %reduce-scatter.3.cloned.1.call-done, f32[1,512,768]{2,1,0:T(8,128)S(1)} %copy-done.10, ...), kind=kLoop, calls=%fused_computation.38 | loop fusion | flops 5505024 | bytes 8650756 | tf_op jit(solution)/shard_map/convert_element_type | solution.py:50
  243.4 0.0 all-gather.7.cloned.1.call-update
  243.5 0.1 fusion.45
  243.6 24.5 %all-gather.9.cloned.1.call-done = bf16[1,384,2048]{2,1,0:T(8,128)(2,1)} async-done(((bf16[1,384,512]{2,1,0:T(8,128)(2,1)}), bf16[1,384,2048]{2,1,0:T(8,128)(2,1)}) %all-gather.9.cloned.1.call-update) | async-done | bytes 1572880 | tf_op jit(solution)/shard_map/all_gather | solution.py:173
  268.1 90.9 %all-to-all-done = bf16[32,72,2048]{2,1,0:T(8,128)(2,1)} async-done(((bf16[32,72,2048]{2,1,0:T(8,128)(2,1)}), bf16[32,72,2048]{2,1,0:T(8,128)(2,1)}, u32[]{:S(2)}, u32[]{:S(2)}) %all-to-all-start) | async-done | bytes 9437216 | tf_op jit(solution)/shard_map/all_to_all | solution.py:134
  359.0 6.0 %fusion.15 = bf16[128,2048]{1,0:T(8,128)(2,1)} fusion(bf16[32,72,2048]{2,1,0:T(8,128)(2,1)} %all-to-all-done, f32[128,32]{0,1:T(8,128)S(1)} %fusion.45, pred[128,32]{0,1:T(8,128)(4,1)S(1)} %convert_compare_fusion.1), kind=kOutput, calls=%fused_computation.24 | convolution fusion | flops 1208811520 | bytes 9981952 | tf_op jit(solution)/shard_map/dot_general | solution.py:151
  364.9 3.9 %copy.28 = bf16[1,2048,768]{2,1,0:T(8,128)(2,1)} copy(bf16[1,2048,768]{2,1,0:T(8,128)(2,1)} %all-gather.7.cloned.1.call-done) | data formatting | bytes 6291456
  368.8 1.1 copy.29
  (30 shorter events, 0.1 us)
Async XLA Ops:
  7.2 110.7 %all-gather.11.cloned.1.call-start = ((), (), s32[]{:S(2)}) async-start(), calls=%async_computation.7 | async-start | bytes 31358976 | tf_op jit(solution)/shard_map/all_gather | solution.py:89
  11.8 154.4 %all-gather.13.cloned.1.call-start = ((), (), s32[]{:S(2)}) async-start(), calls=%async_computation.8 | async-start | bytes 4325376 | tf_op jit(solution)/shard_map/all_gather | solution.py:93
  119.4 94.4 %reduce-scatter.5.cloned.1.call-start = ((), (), s32[]{:S(2)}) async-start(), calls=%async_computation.5 | async-start | bytes 1966080 | tf_op jit(solution)/shard_map/reduce_scatter | solution.py:159
  121.6 30.5 %copy-start.14 = (pred[32,128]{1,0:T(8,128)(4,1)}, pred[32,128]{1,0:T(8,128)(4,1)S(1)}, u32[]{:S(2)}) copy-start(pred[32,128]{1,0:T(8,128)(4,1)S(1)} %convert_compare_fusion) | copy-start | bytes 12292
  121.8 9.4 %copy-start.15 = (bf16[1,2048,768]{2,1,0:T(8,128)(2,1)S(1)}, bf16[1,2048,768]{2,1,0:T(8,128)(2,1)}, u32[]{:S(2)}) copy-start(bf16[1,2048,768]{2,1,0:T(8,128)(2,1)} %param.14) | copy-start | bytes 9437188
  149.2 9.1 %copy-start.7 = (bf16[2304,384]{0,1:T(8,128)(2,1)}, bf16[2304,384]{0,1:T(8,128)(2,1)S(1)}, u32[]{:S(2)}) copy-start(bf16[2304,384]{0,1:T(8,128)(2,1)S(1)} %get-tuple-element.16) | copy-start | bytes 5308420
  152.1 6.1 %copy-start.13 = (f32[32,72]{1,0:T(8,128)}, f32[32,72]{1,0:T(8,128)S(1)}, u32[]{:S(2)}) copy-start(f32[32,72]{1,0:T(8,128)S(1)} %select_reduce_fusion) | copy-start | bytes 27652
  158.2 2.9 copy-start
  166.2 3.2 copy-start.8
  169.3 1.4 copy-start.2
  169.3 2.1 copy-start.12
  172.9 66.6 %reduce-scatter.3.cloned.1.call-start = ((), (), s32[]{:S(2)}) async-start(), calls=%async_computation.3 | async-start | bytes 3932160 | tf_op jit(solution)/shard_map/reduce_scatter | solution.py:156
  172.9 6.0 %copy-start.1 = (f32[2304,384]{0,1:T(8,128)S(1)}, f32[2304,384]{0,1:T(8,128)}, u32[]{:S(2)}) copy-start(f32[2304,384]{0,1:T(8,128)} %get-tuple-element.14) | copy-start | bytes 10616836
  172.9 6.0 %copy-start.3 = (bf16[32,72,512]{2,1,0:T(8,128)(2,1)S(1)}, bf16[32,72,512]{2,1,0:T(8,128)(2,1)}, u32[]{:S(2)}) copy-start(bf16[32,72,512]{2,1,0:T(8,128)(2,1)} %copy-done.2) | copy-start | bytes 7077892
  172.9 10.9 %slice-start = ((s8[9437184]{0:T(1024)(128)(4,1)}), s8[4194304]{0:T(1024)(128)(4,1)S(1)}, s32[]{:S(2)}) async-start(s8[9437184]{0:T(1024)(128)(4,1)} %bitcast.36), calls=%async_computation.9 | async-start | bytes 8388608
  172.9 10.9 %slice-start.1 = ((s8[9437184]{0:T(1024)(128)(4,1)}), s8[4194304]{0:T(1024)(128)(4,1)S(1)}, s32[]{:S(2)}) async-start(s8[9437184]{0:T(1024)(128)(4,1)} %bitcast.36), calls=%async_computation.10 | async-start | bytes 8388608
  178.9 4.9 %slice-start.2 = ((s8[9437184]{0:T(1024)(128)(4,1)}), s8[1048576]{0:T(1024)(128)(4,1)S(1)}, s32[]{:S(2)}) async-start(s8[9437184]{0:T(1024)(128)(4,1)} %bitcast.36), calls=%async_computation.11 | async-start | bytes 2097152
  182.0 1.2 copy-start.4
  182.0 1.8 copy-start.6
  192.7 1.5 copy-start.5
  206.3 152.6 %all-to-all-start = ((bf16[32,72,2048]{2,1,0:T(8,128)(2,1)}), bf16[32,72,2048]{2,1,0:T(8,128)(2,1)}, u32[]{:S(2)}, u32[]{:S(2)}) async-start(bf16[32,72,2048]{2,1,0:T(8,128)(2,1)} %bitcast.41), calls=%async_computation | async-start | bytes 18874368 | tf_op jit(solution)/shard_map/all_to_all | solution.py:134
  213.7 54.3 %all-gather.9.cloned.1.call-start = ((), (), s32[]{:S(2)}) async-start(), calls=%async_computation.6 | async-start | bytes 1966080 | tf_op jit(solution)/shard_map/all_gather | solution.py:173
  213.8 25.7 %copy-start.10 = (f32[1,512,768]{2,1,0:T(8,128)S(1)}, f32[1,512,768]{2,1,0:T(8,128)}, u32[]{:S(2)}) copy-start(f32[1,512,768]{2,1,0:T(8,128)} %param.16) | copy-start | bytes 4718596
  213.8 25.7 %copy-start.11 = (f32[1,512,768]{2,1,0:T(8,128)S(1)}, f32[1,512,768]{2,1,0:T(8,128)}, u32[]{:S(2)}) copy-start(f32[1,512,768]{2,1,0:T(8,128)} %param.17) | copy-start | bytes 4718596
  217.2 26.2 %copy-start.16 = (s32[128,8]{0,1:T(8,128)S(1)}, s32[128,8]{0,1:T(8,128)}, u32[]{:S(2)}) copy-start(s32[128,8]{0,1:T(8,128)} %param.13) | copy-start | bytes 12292
  217.2 147.7 %all-gather.7.cloned.1.call-start = ((), (), s32[]{:S(2)}) async-start(), calls=%async_computation.4 | async-start | bytes 3932160 | tf_op jit(solution)/shard_map/all_gather | solution.py:172
  364.9 3.9 %copy-start.9 = (bf16[1,384,2048]{2,1,0:T(8,128)(2,1)S(1)}, bf16[1,384,2048]{2,1,0:T(8,128)(2,1)}, u32[]{:S(2)}) copy-start(bf16[1,384,2048]{2,1,0:T(8,128)(2,1)} %all-gather.9.cloned.1.call-done) | copy-start | bytes 4718596
Sparse Core Ops, SparseCore 0:
  11.9 105.8 all-gather.10
  120.7 45.4 all-gather.12
  173.0 25.4 reduce-scatter.4
  201.3 38.0 reduce-scatter.2
  241.6 26.4 all-gather.8
  270.2 39.8 all-gather.6

commit v8 on v5

--- a/solution.py
+++ b/solution.py
@@ -127,17 +127,15 @@
         weight_pair,
         weight_down,
     )
-    returned = lax.all_to_all(
-        row_grads.reshape(expert_count, capacity, model_width),
-        "expert",
-        split_axis=0,
-        concat_axis=0,
-        tiled=True,
-    )
-
-    own_match = (
-        expert_ids[:, :, None] == jnp.arange(expert_count, dtype=jnp.int32)[None, None, :]
-    )
+    rolled = jnp.roll(row_grads.reshape(expert_count, capacity, model_width), -me, axis=0)
+    arrived = [rolled[0]]
+    for shift in range(1, expert_count):
+        pairs = [(i, (i + shift) % expert_count) for i in range(expert_count)]
+        arrived.append(lax.ppermute(rolled[shift], "expert", pairs))
+    returned = jnp.stack(arrived)
+    expert_of = (me - jnp.arange(expert_count, dtype=jnp.int32)) % expert_count
+
+    own_match = expert_ids[:, :, None] == expert_of[None, None, :]
     own_routed = jnp.any(own_match, axis=1).astype(jnp.float32)
     own_rank = exclusive_count(own_routed.T).T
     own_pick = (own_routed[:, :, None] > 0) & (

time: 375 us -> 547 us (1.46)
  the two profiles are of different devices: /device:TPU:50 before, /device:TPU:24 now
where the time goes in v8:
time: 547 us; the launch traced here: 539 us
  waiting for transfers between devices  304 us (56%)
  matrix products  72 us (13%)
  starting transfers between devices  62.9 us (11%)
  local copies, waits for them, and re-layouts  56.4 us (10%)
  other arithmetic  28.9 us (5%)
  between operations  14.9 us (3%)
    ppermute x31, waiting for transfers between devices, local(): arrived.append(lax.ppermute(rolled[shift], 'expert', pairs))  207 us
    all_gather x1, waiting for transfers between devices, local(): lax.all_gather(jnp.concatenate([tokens, cotangent[:, :half_width], meta],...  97 us
    ppermute x31, starting transfers between devices, local(): arrived.append(lax.ppermute(rolled[shift], 'expert', pairs))  62.7 us
    unnamed x75, local copies, waits for them, and re-layouts  36.5 us
    dot_general x1, matrix products, local(): jnp.einsum('srt,stc->src', pick_b, first, preferred_element_type=jnp.floa...  15.3 us
  transfers between devices with their start and end apart: 37, of which 27 were waited for; matrix products, arithmetic and copies ran while one was open for 25% of the time, Pallas kernels for 0%

profile of v8, /device:TPU:24, one launch (start us, length us, event | category | flops | bytes accessed | tf_op | source)
XLA Modules:
  0.0 539.1 jit_solution(599812314568861807)
XLA Ops:
  9.7 2.0 fusion.20
  11.8 97.0 %all-gather.11.cloned.1.call-done = bf16[4096,3200]{1,0:T(8,128)(2,1)} async-done(((bf16[128,3200]{1,0:T(8,128)(2,1)}), bf16[4096,3200]{1,0:T(8,128)(2,1)}) %all-gather.11.cloned.1.call-update) | async-done | bytes 26214416 | tf_op jit(solution)/shard_map/all_gather | solution.py:87
  114.2 3.0 fusion.8
  118.4 15.3 %convolution_convert_fusion = bf16[32,72,3200]{2,1,0:T(8,128)(2,1)} fusion(bf16[32,128,3200]{2,1,0:T(8,128)(2,1)} %bitcast.160, f32[32,128]{1,0:T(8,128)S(1)} %fusion.32, pred[32,128]{1,0:T(8,128)(4,1)S(1)} %convert_compare_fusion), kind=kOutput, calls=%fused_computation.2 | convolution fusion | flops 1895399424 | bytes 40980480 | tf_op jit(solution)/shard_map/srt,stc->src/dot_general | solution.py:107
  133.7 9.6 %slice.187 = bf16[32,72,2048]{2,1,0:T(8,128)(2,1)} slice(bf16[32,72,3200]{2,1,0:T(8,128)(2,1)} %convolution_convert_fusion), slice={[0:32], [0:72], [0:2048]} | slice | bytes 18874368 | tf_op jit(solution)/shard_map/slice | solution.py:110
  143.3 10.0 %fusion.3 = f32[2304,768]{0,1:T(8,128)S(1)} fusion(bf16[2304,2048]{1,0:T(8,128)(2,1)} %bitcast.161, bf16[1,2048,768]{2,1,0:T(8,128)(2,1)S(1)} %copy-done.11), kind=kOutput, calls=%fused_computation.17 | convolution fusion | flops 7247757312 | bytes 19660800 | tf_op jit(solution)/shard_map/dot_general | solution.py:15
  153.3 3.1 fusion.1
  157.1 3.5 multiply_convert_fusion.1
  160.7 3.8 fusion.24
  164.5 2.9 fusion.13
  167.4 4.9 multiply_convert_fusion
  172.3 2.0 fusion.14
  175.8 6.8 %multiply_convert_fusion.3 = (bf16[2304,384]{0,1:T(8,128)(2,1)S(1)}, bf16[2304,384]{0,1:T(8,128)(2,1)S(1)}) fusion(f32[2304,384]{0,1:T(8,128)} %get-tuple-element.14, f32[2304,384]{0,1:T(8,128)S(1)} %get-tuple-element.15, f32[2304,384]{0,1:T(8,128)} %fusion.24, bf16[2304,1024]{1,0:T(8,128)(2,1)} %bitcast.158, bf16[384,2048]{1,0:T(8,128)(2,1)} %bitcast.169), kind=kOutput, calls=%fused_computation.10 | convolution fusion | flops 1816363008 | bytes 19660800 | tf_op jit(solution)/shard_map/dot_general | solution.py:22
  182.6 10.5 %convolution_convert_fusion.1 = bf16[2304,2048]{1,0:T(8,128)(2,1)S(1)} fusion(bf16[1,2048,768]{2,1,0:T(8,128)(2,1)} %param.14, bf16[2304,384]{0,1:T(8,128)(2,1)S(1)} %get-tuple-element.61, bf16[2304,384]{0,1:T(8,128)(2,1)S(1)} %get-tuple-element.60), kind=kOutput, calls=%fused_computation.3 | convolution fusion | flops 7259553792 | bytes 16121856 | tf_op jit(solution)/shard_map/dot_general | solution.py:37
  193.1 3.5 fusion
  196.6 3.6 copy-done
  201.9 9.0 %fusion.5 = bf16[1,2048,768]{2,1,0:T(8,128)(2,1)} fusion(bf16[2304,2048]{1,0:T(8,128)(2,1)S(1)} %bitcast.164, bf16[2304,384]{0,1:T(8,128)(2,1)S(1)} %get-tuple-element.61, bf16[2304,384]{0,1:T(8,128)(2,1)S(1)} %get-tuple-element.60), kind=kOutput, calls=%fused_computation.19 | convolution fusion | flops 7256408064 | bytes 16121856 | tf_op jit(solution)/shard_map/dot_general | solution.py:36
  210.8 4.7 slice_bitcast_fusion
  215.5 3.7 collective-permute-start.30
  219.2 3.6 collective-permute-start.27
  223.7 16.3 %collective-permute-done.1 = bf16[72,2048]{1,0:T(8,128)(2,1)S(1)} collective-permute-done((bf16[72,2048]{1,0:T(8,128)(2,1)}, bf16[72,2048]{1,0:T(8,128)(2,1)S(1)}, u32[]{:S(2)}, u32[]{:S(2)}) %collective-permute-start.1) | collective-permute-done | bytes 294944 | tf_op jit(solution)/shard_map/ppermute | solution.py:134
  240.8 16.2 %collective-permute-done.2 = bf16[72,2048]{1,0:T(8,128)(2,1)S(1)} collective-permute-done((bf16[72,2048]{1,0:T(8,128)(2,1)}, bf16[72,2048]{1,0:T(8,128)(2,1)S(1)}, u32[]{:S(2)}, u32[]{:S(2)}) %collective-permute-start.2) | collective-permute-done | bytes 294944 | tf_op jit(solution)/shard_map/ppermute | solution.py:134
  257.0 4.1 collective-permute-start.3
  261.9 7.0 %collective-permute-done.3 = bf16[72,2048]{1,0:T(8,128)(2,1)S(1)} collective-permute-done((bf16[72,2048]{1,0:T(8,128)(2,1)}, bf16[72,2048]{1,0:T(8,128)(2,1)S(1)}, u32[]{:S(2)}, u32[]{:S(2)}) %collective-permute-start.3) | collective-permute-done | bytes 294944 | tf_op jit(solution)/shard_map/ppermute | solution.py:134
  269.6 6.5 %collective-permute-done.4 = bf16[72,2048]{1,0:T(8,128)(2,1)S(1)} collective-permute-done((bf16[72,2048]{1,0:T(8,128)(2,1)}, bf16[72,2048]{1,0:T(8,128)(2,1)S(1)}, u32[]{:S(2)}, u32[]{:S(2)}) %collective-permute-start.4) | collective-permute-done | bytes 294944 | tf_op jit(solution)/shard_map/ppermute | solution.py:134
  276.2 2.3 collective-permute-start.5
  279.2 7.9 %collective-permute-done.5 = bf16[72,2048]{1,0:T(8,128)(2,1)S(1)} collective-permute-done((bf16[72,2048]{1,0:T(8,128)(2,1)}, bf16[72,2048]{1,0:T(8,128)(2,1)S(1)}, u32[]{:S(2)}, u32[]{:S(2)}) %collective-permute-start.5) | collective-permute-done | bytes 294944 | tf_op jit(solution)/shard_map/ppermute | solution.py:134
  288.1 5.6 %collective-permute-done.6 = bf16[72,2048]{1,0:T(8,128)(2,1)S(1)} collective-permute-done((bf16[72,2048]{1,0:T(8,128)(2,1)}, bf16[72,2048]{1,0:T(8,128)(2,1)S(1)}, u32[]{:S(2)}, u32[]{:S(2)}) %collective-permute-start.6) | collective-permute-done | bytes 294944 | tf_op jit(solution)/shard_map/ppermute | solution.py:134
  293.7 6.3 %collective-permute-start.7 = (bf16[72,2048]{1,0:T(8,128)(2,1)S(1)}, bf16[72,2048]{1,0:T(8,128)(2,1)S(1)}, u32[]{:S(2)}, u32[]{:S(2)}) collective-permute-start(bf16[72,2048]{1,0:T(8,128)(2,1)S(1)} %get-tuple-element.48), channel_id=1, source_target_pairs={{0,8},{1,9},{2,10},{3,11},{4,12},{5,13},{6,14},{7,15},{8,16},{9,17... | collective-permute-start | bytes 884744 | tf_op jit(solution)/shard_map/ppermute | solution.py:134
  300.7 6.4 %collective-permute-done.7 = bf16[72,2048]{1,0:T(8,128)(2,1)S(1)} collective-permute-done((bf16[72,2048]{1,0:T(8,128)(2,1)S(1)}, bf16[72,2048]{1,0:T(8,128)(2,1)S(1)}, u32[]{:S(2)}, u32[]{:S(2)}) %collective-permute-start.7) | collective-permute-done | bytes 294944 | tf_op jit(solution)/shard_map/ppermute | solution.py:134
  307.1 3.1 collective-permute-start.8
  310.9 5.9 %collective-permute-done.8 = bf16[72,2048]{1,0:T(8,128)(2,1)S(1)} collective-permute-done((bf16[72,2048]{1,0:T(8,128)(2,1)S(1)}, bf16[72,2048]{1,0:T(8,128)(2,1)S(1)}, u32[]{:S(2)}, u32[]{:S(2)}) %collective-permute-start.8) | collective-permute-done | bytes 294944 | tf_op jit(solution)/shard_map/ppermute | solution.py:134
  317.6 9.6 %collective-permute-done.9 = bf16[72,2048]{1,0:T(8,128)(2,1)S(1)} collective-permute-done((bf16[72,2048]{1,0:T(8,128)(2,1)S(1)}, bf16[72,2048]{1,0:T(8,128)(2,1)S(1)}, u32[]{:S(2)}, u32[]{:S(2)}) %collective-permute-start.9) | collective-permute-done | bytes 294944 | tf_op jit(solution)/shard_map/ppermute | solution.py:134
  329.0 9.3 %collective-permute-done.10 = bf16[72,2048]{1,0:T(8,128)(2,1)S(1)} collective-permute-done((bf16[72,2048]{1,0:T(8,128)(2,1)S(1)}, bf16[72,2048]{1,0:T(8,128)(2,1)S(1)}, u32[]{:S(2)}, u32[]{:S(2)}) %collective-permute-start.10) | collective-permute-done | bytes 294944 | tf_op jit(solution)/shard_map/ppermute | solution.py:134
  338.2 3.5 collective-permute-start.11
  342.5 7.0 %collective-permute-done.11 = bf16[72,2048]{1,0:T(8,128)(2,1)S(1)} collective-permute-done((bf16[72,2048]{1,0:T(8,128)(2,1)S(1)}, bf16[72,2048]{1,0:T(8,128)(2,1)S(1)}, u32[]{:S(2)}, u32[]{:S(2)}) %collective-permute-start.11) | collective-permute-done | bytes 294944 | tf_op jit(solution)/shard_map/ppermute | solution.py:134
  349.5 1.9 collective-permute-start.12
  352.2 7.8 %collective-permute-done.12 = bf16[72,2048]{1,0:T(8,128)(2,1)S(1)} collective-permute-done((bf16[72,2048]{1,0:T(8,128)(2,1)S(1)}, bf16[72,2048]{1,0:T(8,128)(2,1)S(1)}, u32[]{:S(2)}, u32[]{:S(2)}) %collective-permute-start.12) | collective-permute-done | bytes 294944 | tf_op jit(solution)/shard_map/ppermute | solution.py:134
  359.9 3.3 collective-permute-start.13
  364.0 6.4 %collective-permute-done.13 = bf16[72,2048]{1,0:T(8,128)(2,1)S(1)} collective-permute-done((bf16[72,2048]{1,0:T(8,128)(2,1)S(1)}, bf16[72,2048]{1,0:T(8,128)(2,1)S(1)}, u32[]{:S(2)}, u32[]{:S(2)}) %collective-permute-start.13) | collective-permute-done | bytes 294944 | tf_op jit(solution)/shard_map/ppermute | solution.py:134
  370.4 1.8 collective-permute-start.14
  373.0 5.3 collective-permute-done.14
  378.3 4.9 collective-permute-start.15
  383.9 6.1 %collective-permute-done.15 = bf16[72,2048]{1,0:T(8,128)(2,1)S(1)} collective-permute-done((bf16[72,2048]{1,0:T(8,128)(2,1)S(1)}, bf16[72,2048]{1,0:T(8,128)(2,1)S(1)}, u32[]{:S(2)}, u32[]{:S(2)}) %collective-permute-start.15) | collective-permute-done | bytes 294944 | tf_op jit(solution)/shard_map/ppermute | solution.py:134
  392.4 7.1 %collective-permute-done.16 = bf16[72,2048]{1,0:T(8,128)(2,1)S(1)} collective-permute-done((bf16[72,2048]{1,0:T(8,128)(2,1)S(1)}, bf16[72,2048]{1,0:T(8,128)(2,1)S(1)}, u32[]{:S(2)}, u32[]{:S(2)}) %collective-permute-start.16) | collective-permute-done | bytes 294944 | tf_op jit(solution)/shard_map/ppermute | solution.py:134
  399.5 2.2 collective-permute-start.17
  402.4 3.2 subtract_convert_fusion.1
  405.7 6.7 %collective-permute-done.17 = bf16[72,2048]{1,0:T(8,128)(2,1)} collective-permute-done((bf16[72,2048]{1,0:T(8,128)(2,1)}, bf16[72,2048]{1,0:T(8,128)(2,1)}, u32[]{:S(2)}, u32[]{:S(2)}) %collective-permute-start.17) | collective-permute-done | bytes 294944 | tf_op jit(solution)/shard_map/ppermute | solution.py:134
  415.1 8.8 %collective-permute-done.18 = bf16[72,2048]{1,0:T(8,128)(2,1)S(1)} collective-permute-done((bf16[72,2048]{1,0:T(8,128)(2,1)}, bf16[72,2048]{1,0:T(8,128)(2,1)S(1)}, u32[]{:S(2)}, u32[]{:S(2)}) %collective-permute-start.18) | collective-permute-done | bytes 294944 | tf_op jit(solution)/shard_map/ppermute | solution.py:134
  424.0 5.6 %collective-permute-start.19 = (bf16[72,2048]{1,0:T(8,128)(2,1)}, bf16[72,2048]{1,0:T(8,128)(2,1)S(1)}, u32[]{:S(2)}, u32[]{:S(2)}) collective-permute-start(bf16[72,2048]{1,0:T(8,128)(2,1)} %get-tuple-element.36), channel_id=1, source_target_pairs={{0,20},{1,21},{2,22},{3,23},{4,24},{5,25},{6,26},{7,27},{8,28},{9,... | collective-permute-start | bytes 884744 | tf_op jit(solution)/shard_map/ppermute | solution.py:134
  430.3 5.7 %collective-permute-done.19 = bf16[72,2048]{1,0:T(8,128)(2,1)S(1)} collective-permute-done((bf16[72,2048]{1,0:T(8,128)(2,1)}, bf16[72,2048]{1,0:T(8,128)(2,1)S(1)}, u32[]{:S(2)}, u32[]{:S(2)}) %collective-permute-start.19) | collective-permute-done | bytes 294944 | tf_op jit(solution)/shard_map/ppermute | solution.py:134
  436.0 4.0 collective-permute-start.20
  440.8 6.6 %collective-permute-done.20 = bf16[72,2048]{1,0:T(8,128)(2,1)S(1)} collective-permute-done((bf16[72,2048]{1,0:T(8,128)(2,1)}, bf16[72,2048]{1,0:T(8,128)(2,1)S(1)}, u32[]{:S(2)}, u32[]{:S(2)}) %collective-permute-start.20) | collective-permute-done | bytes 294944 | tf_op jit(solution)/shard_map/ppermute | solution.py:134
  447.4 6.3 %collective-permute-start.21 = (bf16[72,2048]{1,0:T(8,128)(2,1)}, bf16[72,2048]{1,0:T(8,128)(2,1)S(1)}, u32[]{:S(2)}, u32[]{:S(2)}) collective-permute-start(bf16[72,2048]{1,0:T(8,128)(2,1)} %get-tuple-element.34), channel_id=1, source_target_pairs={{0,22},{1,23},{2,24},{3,25},{4,26},{5,27},{6,28},{7,29},{8,30},{9,... | collective-permute-start | bytes 884744 | tf_op jit(solution)/shard_map/ppermute | solution.py:134
  454.5 4.4 collective-permute-done.21
  461.0 3.9 subtract_convert_fusion
  464.9 3.2 collective-permute-done.22
  469.8 10.6 %collective-permute-done.23 = bf16[72,2048]{1,0:T(8,128)(2,1)S(1)} collective-permute-done((bf16[72,2048]{1,0:T(8,128)(2,1)}, bf16[72,2048]{1,0:T(8,128)(2,1)S(1)}, u32[]{:S(2)}, u32[]{:S(2)}) %collective-permute-start.23) | collective-permute-done | bytes 294944 | tf_op jit(solution)/shard_map/ppermute | solution.py:134
  481.2 9.9 %collective-permute-done.24 = bf16[72,2048]{1,0:T(8,128)(2,1)S(1)} collective-permute-done((bf16[72,2048]{1,0:T(8,128)(2,1)}, bf16[72,2048]{1,0:T(8,128)(2,1)S(1)}, u32[]{:S(2)}, u32[]{:S(2)}) %collective-permute-start.24) | collective-permute-done | bytes 294944 | tf_op jit(solution)/shard_map/ppermute | solution.py:134
  492.2 10.1 %collective-permute-done.25 = bf16[72,2048]{1,0:T(8,128)(2,1)S(1)} collective-permute-done((bf16[72,2048]{1,0:T(8,128)(2,1)}, bf16[72,2048]{1,0:T(8,128)(2,1)S(1)}, u32[]{:S(2)}, u32[]{:S(2)}) %collective-permute-start.25) | collective-permute-done | bytes 294944 | tf_op jit(solution)/shard_map/ppermute | solution.py:134
  503.0 10.3 %collective-permute-done.26 = bf16[72,2048]{1,0:T(8,128)(2,1)S(1)} collective-permute-done((bf16[72,2048]{1,0:T(8,128)(2,1)}, bf16[72,2048]{1,0:T(8,128)(2,1)S(1)}, u32[]{:S(2)}, u32[]{:S(2)}) %collective-permute-start.26) | collective-permute-done | bytes 294944 | tf_op jit(solution)/shard_map/ppermute | solution.py:134
  517.5 1.7 bitcast_dynamic-update-slice_fusion.1
  520.9 6.0 %fusion.6 = bf16[128,2048]{1,0:T(8,128)(2,1)} fusion(bf16[32,72,2048]{2,1,0:T(8,128)(2,1)} %bitcast_dynamic-update-slice_fusion, f32[128,32]{0,1:T(8,128)S(1)} %copy-done.17, pred[128,32]{0,1:T(8,128)(4,1)S(1)} %copy-done.16), kind=kOutput, calls=%fused_computation.21 | convolution fusion | flops 1208811520 | bytes 9981952 | tf_op jit(solution)/shard_map/dot_general | solution.py:145
  526.8 3.9 copy.59
  (128 shorter events, 46.9 us)
Async XLA Ops:
  7.2 101.6 %all-gather.11.cloned.1.call-start = ((), (), s32[]{:S(2)}) async-start(), calls=%async_computation.6 | async-start | bytes 27033600 | tf_op jit(solution)/shard_map/all_gather | solution.py:87
  11.7 155.6 %all-gather.13.cloned.1.call-start = ((), (), s32[]{:S(2)}) async-start(), calls=%async_computation.7 | async-start | bytes 8650752 | tf_op jit(solution)/shard_map/all_gather | solution.py:91
  110.5 291.9 %reduce-scatter.5.cloned.1.call-start = ((), (), s32[]{:S(2)}) async-start(), calls=%async_computation.4 | async-start | bytes 1966080 | tf_op jit(solution)/shard_map/reduce_scatter | solution.py:153
  117.8 0.6 copy-start.13
  133.7 9.6 %copy-start.11 = (bf16[1,2048,768]{2,1,0:T(8,128)(2,1)S(1)}, bf16[1,2048,768]{2,1,0:T(8,128)(2,1)}, u32[]{:S(2)}) copy-start(bf16[1,2048,768]{2,1,0:T(8,128)(2,1)} %param.14) | copy-start | bytes 9437188
  153.3 3.1 copy-start.14
  153.3 3.1 copy-start.15
  156.4 8.1 %copy-start.2 = (bf16[2304,384]{0,1:T(8,128)(2,1)}, bf16[2304,384]{0,1:T(8,128)(2,1)S(1)}, u32[]{:S(2)}) copy-start(bf16[2304,384]{0,1:T(8,128)(2,1)S(1)} %get-tuple-element.16) | copy-start | bytes 5308420
  157.1 3.6 copy-start.12
  157.1 3.6 copy-start.7
  167.4 4.9 copy-start.3
  172.3 2.2 copy-start.1
  172.3 2.2 copy-start.8
  175.7 285.2 %reduce-scatter.3.cloned.1.call-start = ((), (), s32[]{:S(2)}) async-start(), calls=%async_computation.2 | async-start | bytes 3932160 | tf_op jit(solution)/shard_map/reduce_scatter | solution.py:150
  182.6 19.2 %slice-start = ((s8[9437184]{0:T(1024)(128)(4,1)}), s8[1048576]{0:T(1024)(128)(4,1)S(1)}, s32[]{:S(2)}) async-start(s8[9437184]{0:T(1024)(128)(4,1)} %bitcast.162), calls=%async_computation.8 | async-start | bytes 2097152
  182.6 19.2 %slice-start.1 = ((s8[9437184]{0:T(1024)(128)(4,1)}), s8[4194304]{0:T(1024)(128)(4,1)S(1)}, s32[]{:S(2)}) async-start(s8[9437184]{0:T(1024)(128)(4,1)} %bitcast.162), calls=%async_computation.9 | async-start | bytes 8388608
  193.1 8.7 %slice-start.2 = ((s8[9437184]{0:T(1024)(128)(4,1)}), s8[4194304]{0:T(1024)(128)(4,1)S(1)}, s32[]{:S(2)}) async-start(s8[9437184]{0:T(1024)(128)(4,1)} %bitcast.162), calls=%async_computation.10 | async-start | bytes 8388608
  196.6 3.7 copy-start
  201.6 21.3 %collective-permute-start = (bf16[72,2048]{1,0:T(8,128)(2,1)S(1)}, bf16[72,2048]{1,0:T(8,128)(2,1)S(1)}, u32[]{:S(2)}, u32[]{:S(2)}) collective-permute-start(bf16[72,2048]{1,0:T(8,128)(2,1)S(1)} %get-tuple-element.55), channel_id=1, source_target_pairs={{0,1},{1,2},{2,3},{3,4},{4,5},{5,6},{6,7},{7,8},{8,9},{9,10},{10,1... | collective-permute-start | bytes 884744 | tf_op jit(solution)/shard_map/ppermute | solution.py:134
  215.5 303.7 %collective-permute-start.30 = (bf16[72,2048]{1,0:T(8,128)(2,1)S(1)}, bf16[72,2048]{1,0:T(8,128)(2,1)}, u32[]{:S(2)}, u32[]{:S(2)}) collective-permute-start(bf16[72,2048]{1,0:T(8,128)(2,1)S(1)} %get-tuple-element.25), channel_id=1, source_target_pairs={{0,31},{1,0},{2,1},{3,2},{4,3},{5,4},{6,5},{7,6},{8,7},{9,8},{10,9... | collective-permute-start | bytes 884744 | tf_op jit(solution)/shard_map/ppermute | solution.py:134
  219.2 298.3 %collective-permute-start.29 = (bf16[72,2048]{1,0:T(8,128)(2,1)}, bf16[72,2048]{1,0:T(8,128)(2,1)}, u32[]{:S(2)}, u32[]{:S(2)}) collective-permute-start(bf16[72,2048]{1,0:T(8,128)(2,1)} %get-tuple-element.26), channel_id=1, source_target_pairs={{0,30},{1,31},{2,0},{3,1},{4,2},{5,3},{6,4},{7,5},{8,6},{9,7},{10,... | collective-permute-start | bytes 884744 | tf_op jit(solution)/shard_map/ppermute | solution.py:134
  219.2 296.6 %collective-permute-start.28 = (bf16[72,2048]{1,0:T(8,128)(2,1)}, bf16[72,2048]{1,0:T(8,128)(2,1)}, u32[]{:S(2)}, u32[]{:S(2)}) collective-permute-start(bf16[72,2048]{1,0:T(8,128)(2,1)} %get-tuple-element.27), channel_id=1, source_target_pairs={{0,29},{1,30},{2,31},{3,0},{4,1},{5,2},{6,3},{7,4},{8,5},{9,6},{10... | collective-permute-start | bytes 884744 | tf_op jit(solution)/shard_map/ppermute | solution.py:134
  219.2 294.9 %collective-permute-start.27 = (bf16[72,2048]{1,0:T(8,128)(2,1)}, bf16[72,2048]{1,0:T(8,128)(2,1)}, u32[]{:S(2)}, u32[]{:S(2)}) collective-permute-start(bf16[72,2048]{1,0:T(8,128)(2,1)} %get-tuple-element.28), channel_id=1, source_target_pairs={{0,28},{1,29},{2,30},{3,31},{4,0},{5,1},{6,2},{7,3},{8,4},{9,5},{1... | collective-permute-start | bytes 884744 | tf_op jit(solution)/shard_map/ppermute | solution.py:134
  222.8 304.0 %all-gather.9.cloned.1.call-start = ((), (), s32[]{:S(2)}) async-start(), calls=%async_computation.5 | async-start | bytes 1966080 | tf_op jit(solution)/shard_map/all_gather | solution.py:167
  222.9 155.4 %copy-start.10 = (bf16[72,2048]{1,0:T(8,128)(2,1)S(1)}, bf16[72,2048]{1,0:T(8,128)(2,1)}, u32[]{:S(2)}) copy-start(bf16[72,2048]{1,0:T(8,128)(2,1)} %get-tuple-element.40) | copy-start | bytes 884740
  222.9 167.1 %copy-start.9 = (bf16[72,2048]{1,0:T(8,128)(2,1)S(1)}, bf16[72,2048]{1,0:T(8,128)(2,1)}, u32[]{:S(2)}) copy-start(bf16[72,2048]{1,0:T(8,128)(2,1)} %get-tuple-element.39) | copy-start | bytes 884740
  222.9 17.2 %collective-permute-start.1 = (bf16[72,2048]{1,0:T(8,128)(2,1)}, bf16[72,2048]{1,0:T(8,128)(2,1)S(1)}, u32[]{:S(2)}, u32[]{:S(2)}) collective-permute-start(bf16[72,2048]{1,0:T(8,128)(2,1)} %get-tuple-element.54), channel_id=1, source_target_pairs={{0,2},{1,3},{2,4},{3,5},{4,6},{5,7},{6,8},{7,9},{8,10},{9,11},{10,... | collective-permute-start | bytes 884744 | tf_op jit(solution)/shard_map/ppermute | solution.py:134
  240.1 16.9 %collective-permute-start.2 = (bf16[72,2048]{1,0:T(8,128)(2,1)}, bf16[72,2048]{1,0:T(8,128)(2,1)S(1)}, u32[]{:S(2)}, u32[]{:S(2)}) collective-permute-start(bf16[72,2048]{1,0:T(8,128)(2,1)} %get-tuple-element.53), channel_id=1, source_target_pairs={{0,3},{1,4},{2,5},{3,6},{4,7},{5,8},{6,9},{7,10},{8,11},{9,12},{10... | collective-permute-start | bytes 884744 | tf_op jit(solution)/shard_map/ppermute | solution.py:134
  257.0 11.9 %collective-permute-start.3 = (bf16[72,2048]{1,0:T(8,128)(2,1)}, bf16[72,2048]{1,0:T(8,128)(2,1)S(1)}, u32[]{:S(2)}, u32[]{:S(2)}) collective-permute-start(bf16[72,2048]{1,0:T(8,128)(2,1)} %get-tuple-element.52), channel_id=1, source_target_pairs={{0,4},{1,5},{2,6},{3,7},{4,8},{5,9},{6,10},{7,11},{8,12},{9,13},{1... | collective-permute-start | bytes 884744 | tf_op jit(solution)/shard_map/ppermute | solution.py:134
  268.9 7.3 %collective-permute-start.4 = (bf16[72,2048]{1,0:T(8,128)(2,1)}, bf16[72,2048]{1,0:T(8,128)(2,1)S(1)}, u32[]{:S(2)}, u32[]{:S(2)}) collective-permute-start(bf16[72,2048]{1,0:T(8,128)(2,1)} %get-tuple-element.51), channel_id=1, source_target_pairs={{0,5},{1,6},{2,7},{3,8},{4,9},{5,10},{6,11},{7,12},{8,13},{9,14},{... | collective-permute-start | bytes 884744 | tf_op jit(solution)/shard_map/ppermute | solution.py:134
  276.2 10.9 %collective-permute-start.5 = (bf16[72,2048]{1,0:T(8,128)(2,1)}, bf16[72,2048]{1,0:T(8,128)(2,1)S(1)}, u32[]{:S(2)}, u32[]{:S(2)}) collective-permute-start(bf16[72,2048]{1,0:T(8,128)(2,1)} %get-tuple-element.50), channel_id=1, source_target_pairs={{0,6},{1,7},{2,8},{3,9},{4,10},{5,11},{6,12},{7,13},{8,14},{9,15},... | collective-permute-start | bytes 884744 | tf_op jit(solution)/shard_map/ppermute | solution.py:134
  287.1 6.6 %collective-permute-start.6 = (bf16[72,2048]{1,0:T(8,128)(2,1)}, bf16[72,2048]{1,0:T(8,128)(2,1)S(1)}, u32[]{:S(2)}, u32[]{:S(2)}) collective-permute-start(bf16[72,2048]{1,0:T(8,128)(2,1)} %get-tuple-element.49), channel_id=1, source_target_pairs={{0,7},{1,8},{2,9},{3,10},{4,11},{5,12},{6,13},{7,14},{8,15},{9,16}... | collective-permute-start | bytes 884744 | tf_op jit(solution)/shard_map/ppermute | solution.py:134
  293.7 13.4 %collective-permute-start.7 = (bf16[72,2048]{1,0:T(8,128)(2,1)S(1)}, bf16[72,2048]{1,0:T(8,128)(2,1)S(1)}, u32[]{:S(2)}, u32[]{:S(2)}) collective-permute-start(bf16[72,2048]{1,0:T(8,128)(2,1)S(1)} %get-tuple-element.48), channel_id=1, source_target_pairs={{0,8},{1,9},{2,10},{3,11},{4,12},{5,13},{6,14},{7,15},{8,16},{9,17... | collective-permute-start | bytes 884744 | tf_op jit(solution)/shard_map/ppermute | solution.py:134
  307.1 9.8 %collective-permute-start.8 = (bf16[72,2048]{1,0:T(8,128)(2,1)S(1)}, bf16[72,2048]{1,0:T(8,128)(2,1)S(1)}, u32[]{:S(2)}, u32[]{:S(2)}) collective-permute-start(bf16[72,2048]{1,0:T(8,128)(2,1)S(1)} %get-tuple-element.47), channel_id=1, source_target_pairs={{0,9},{1,10},{2,11},{3,12},{4,13},{5,14},{6,15},{7,16},{8,17},{9,1... | collective-permute-start | bytes 884744 | tf_op jit(solution)/shard_map/ppermute | solution.py:134
  316.8 10.3 %collective-permute-start.9 = (bf16[72,2048]{1,0:T(8,128)(2,1)S(1)}, bf16[72,2048]{1,0:T(8,128)(2,1)S(1)}, u32[]{:S(2)}, u32[]{:S(2)}) collective-permute-start(bf16[72,2048]{1,0:T(8,128)(2,1)S(1)} %get-tuple-element.46), channel_id=1, source_target_pairs={{0,10},{1,11},{2,12},{3,13},{4,14},{5,15},{6,16},{7,17},{8,18},{9,... | collective-permute-start | bytes 884744 | tf_op jit(solution)/shard_map/ppermute | solution.py:134
  327.2 11.1 %collective-permute-start.10 = (bf16[72,2048]{1,0:T(8,128)(2,1)S(1)}, bf16[72,2048]{1,0:T(8,128)(2,1)S(1)}, u32[]{:S(2)}, u32[]{:S(2)}) collective-permute-start(bf16[72,2048]{1,0:T(8,128)(2,1)S(1)} %get-tuple-element.45), channel_id=1, source_target_pairs={{0,11},{1,12},{2,13},{3,14},{4,15},{5,16},{6,17},{7,18},{8,19},{9,... | collective-permute-start | bytes 884744 | tf_op jit(solution)/shard_map/ppermute | solution.py:134
  338.2 11.3 %collective-permute-start.11 = (bf16[72,2048]{1,0:T(8,128)(2,1)S(1)}, bf16[72,2048]{1,0:T(8,128)(2,1)S(1)}, u32[]{:S(2)}, u32[]{:S(2)}) collective-permute-start(bf16[72,2048]{1,0:T(8,128)(2,1)S(1)} %get-tuple-element.44), channel_id=1, source_target_pairs={{0,12},{1,13},{2,14},{3,15},{4,16},{5,17},{6,18},{7,19},{8,20},{9,... | collective-permute-start | bytes 884744 | tf_op jit(solution)/shard_map/ppermute | solution.py:134
  349.5 10.4 %collective-permute-start.12 = (bf16[72,2048]{1,0:T(8,128)(2,1)S(1)}, bf16[72,2048]{1,0:T(8,128)(2,1)S(1)}, u32[]{:S(2)}, u32[]{:S(2)}) collective-permute-start(bf16[72,2048]{1,0:T(8,128)(2,1)S(1)} %get-tuple-element.43), channel_id=1, source_target_pairs={{0,13},{1,14},{2,15},{3,16},{4,17},{5,18},{6,19},{7,20},{8,21},{9,... | collective-permute-start | bytes 884744 | tf_op jit(solution)/shard_map/ppermute | solution.py:134
  359.9 10.5 %collective-permute-start.13 = (bf16[72,2048]{1,0:T(8,128)(2,1)S(1)}, bf16[72,2048]{1,0:T(8,128)(2,1)S(1)}, u32[]{:S(2)}, u32[]{:S(2)}) collective-permute-start(bf16[72,2048]{1,0:T(8,128)(2,1)S(1)} %get-tuple-element.42), channel_id=1, source_target_pairs={{0,14},{1,15},{2,16},{3,17},{4,18},{5,19},{6,20},{7,21},{8,22},{9,... | collective-permute-start | bytes 884744 | tf_op jit(solution)/shard_map/ppermute | solution.py:134
  370.4 7.9 %collective-permute-start.14 = (bf16[72,2048]{1,0:T(8,128)(2,1)S(1)}, bf16[72,2048]{1,0:T(8,128)(2,1)S(1)}, u32[]{:S(2)}, u32[]{:S(2)}) collective-permute-start(bf16[72,2048]{1,0:T(8,128)(2,1)S(1)} %get-tuple-element.41), channel_id=1, source_target_pairs={{0,15},{1,16},{2,17},{3,18},{4,19},{5,20},{6,21},{7,22},{8,23},{9,... | collective-permute-start | bytes 884744 | tf_op jit(solution)/shard_map/ppermute | solution.py:134
  378.3 82.7 %copy-start.5 = (f32[1,512,768]{2,1,0:T(8,128)S(1)}, f32[1,512,768]{2,1,0:T(8,128)}, u32[]{:S(2)}) copy-start(f32[1,512,768]{2,1,0:T(8,128)} %param.16) | copy-start | bytes 4718596
  378.3 82.7 %copy-start.6 = (f32[1,512,768]{2,1,0:T(8,128)S(1)}, f32[1,512,768]{2,1,0:T(8,128)}, u32[]{:S(2)}) copy-start(f32[1,512,768]{2,1,0:T(8,128)} %param.17) | copy-start | bytes 4718596
  378.3 11.7 %collective-permute-start.15 = (bf16[72,2048]{1,0:T(8,128)(2,1)S(1)}, bf16[72,2048]{1,0:T(8,128)(2,1)S(1)}, u32[]{:S(2)}, u32[]{:S(2)}) collective-permute-start(bf16[72,2048]{1,0:T(8,128)(2,1)S(1)} %copy-done.10), channel_id=1, source_target_pairs={{0,16},{1,17},{2,18},{3,19},{4,20},{5,21},{6,22},{7,23},{8,24},{9,... | collective-permute-start | bytes 884744 | tf_op jit(solution)/shard_map/ppermute | solution.py:134
  390.0 9.5 %collective-permute-start.16 = (bf16[72,2048]{1,0:T(8,128)(2,1)S(1)}, bf16[72,2048]{1,0:T(8,128)(2,1)S(1)}, u32[]{:S(2)}, u32[]{:S(2)}) collective-permute-start(bf16[72,2048]{1,0:T(8,128)(2,1)S(1)} %copy-done.9), channel_id=1, source_target_pairs={{0,17},{1,18},{2,19},{3,20},{4,21},{5,22},{6,23},{7,24},{8,25},{9,... | collective-permute-start | bytes 884744 | tf_op jit(solution)/shard_map/ppermute | solution.py:134
  399.5 13.0 %collective-permute-start.17 = (bf16[72,2048]{1,0:T(8,128)(2,1)}, bf16[72,2048]{1,0:T(8,128)(2,1)}, u32[]{:S(2)}, u32[]{:S(2)}) collective-permute-start(bf16[72,2048]{1,0:T(8,128)(2,1)} %get-tuple-element.38), channel_id=1, source_target_pairs={{0,18},{1,19},{2,20},{3,21},{4,22},{5,23},{6,24},{7,25},{8,26},{9,... | collective-permute-start | bytes 884744 | tf_op jit(solution)/shard_map/ppermute | solution.py:134
  405.7 121.2 %all-gather.7.cloned.1.call-start = ((), (), s32[]{:S(2)}) async-start(), calls=%async_computation.3 | async-start | bytes 3932160 | tf_op jit(solution)/shard_map/all_gather | solution.py:166
  412.4 11.5 %collective-permute-start.18 = (bf16[72,2048]{1,0:T(8,128)(2,1)}, bf16[72,2048]{1,0:T(8,128)(2,1)S(1)}, u32[]{:S(2)}, u32[]{:S(2)}) collective-permute-start(bf16[72,2048]{1,0:T(8,128)(2,1)} %get-tuple-element.37), channel_id=1, source_target_pairs={{0,19},{1,20},{2,21},{3,22},{4,23},{5,24},{6,25},{7,26},{8,27},{9,... | collective-permute-start | bytes 884744 | tf_op jit(solution)/shard_map/ppermute | solution.py:134
  424.0 12.1 %collective-permute-start.19 = (bf16[72,2048]{1,0:T(8,128)(2,1)}, bf16[72,2048]{1,0:T(8,128)(2,1)S(1)}, u32[]{:S(2)}, u32[]{:S(2)}) collective-permute-start(bf16[72,2048]{1,0:T(8,128)(2,1)} %get-tuple-element.36), channel_id=1, source_target_pairs={{0,20},{1,21},{2,22},{3,23},{4,24},{5,25},{6,26},{7,27},{8,28},{9,... | collective-permute-start | bytes 884744 | tf_op jit(solution)/shard_map/ppermute | solution.py:134
  436.0 11.3 %collective-permute-start.20 = (bf16[72,2048]{1,0:T(8,128)(2,1)}, bf16[72,2048]{1,0:T(8,128)(2,1)S(1)}, u32[]{:S(2)}, u32[]{:S(2)}) collective-permute-start(bf16[72,2048]{1,0:T(8,128)(2,1)} %get-tuple-element.35), channel_id=1, source_target_pairs={{0,21},{1,22},{2,23},{3,24},{4,25},{5,26},{6,27},{7,28},{8,29},{9,... | collective-permute-start | bytes 884744 | tf_op jit(solution)/shard_map/ppermute | solution.py:134
  447.4 11.5 %collective-permute-start.21 = (bf16[72,2048]{1,0:T(8,128)(2,1)}, bf16[72,2048]{1,0:T(8,128)(2,1)S(1)}, u32[]{:S(2)}, u32[]{:S(2)}) collective-permute-start(bf16[72,2048]{1,0:T(8,128)(2,1)} %get-tuple-element.34), channel_id=1, source_target_pairs={{0,22},{1,23},{2,24},{3,25},{4,26},{5,27},{6,28},{7,29},{8,30},{9,... | collective-permute-start | bytes 884744 | tf_op jit(solution)/shard_map/ppermute | solution.py:134
  458.9 9.3 %collective-permute-start.22 = (bf16[72,2048]{1,0:T(8,128)(2,1)}, bf16[72,2048]{1,0:T(8,128)(2,1)}, u32[]{:S(2)}, u32[]{:S(2)}) collective-permute-start(bf16[72,2048]{1,0:T(8,128)(2,1)} %get-tuple-element.33), channel_id=1, source_target_pairs={{0,23},{1,24},{2,25},{3,26},{4,27},{5,28},{6,29},{7,30},{8,31},{9,... | collective-permute-start | bytes 884744 | tf_op jit(solution)/shard_map/ppermute | solution.py:134
  464.9 56.0 %copy-start.16 = (pred[128,32]{0,1:T(8,128)(4,1)S(1)}, pred[128,32]{0,1:T(8,128)(4,1)}, u32[]{:S(2)}) copy-start(pred[128,32]{0,1:T(8,128)(4,1)} %convert_compare_fusion.1) | copy-start | bytes 12292
  464.9 56.0 %copy-start.17 = (f32[128,32]{0,1:T(8,128)S(1)}, f32[128,32]{0,1:T(8,128)}, u32[]{:S(2)}) copy-start(f32[128,32]{0,1:T(8,128)} %fusion.33) | copy-start | bytes 49156
  468.1 12.2 %collective-permute-start.23 = (bf16[72,2048]{1,0:T(8,128)(2,1)}, bf16[72,2048]{1,0:T(8,128)(2,1)S(1)}, u32[]{:S(2)}, u32[]{:S(2)}) collective-permute-start(bf16[72,2048]{1,0:T(8,128)(2,1)} %get-tuple-element.32), channel_id=1, source_target_pairs={{0,24},{1,25},{2,26},{3,27},{4,28},{5,29},{6,30},{7,31},{8,0},{9,1... | collective-permute-start | bytes 884744 | tf_op jit(solution)/shard_map/ppermute | solution.py:134
  480.4 10.7 %collective-permute-start.24 = (bf16[72,2048]{1,0:T(8,128)(2,1)}, bf16[72,2048]{1,0:T(8,128)(2,1)S(1)}, u32[]{:S(2)}, u32[]{:S(2)}) collective-permute-start(bf16[72,2048]{1,0:T(8,128)(2,1)} %get-tuple-element.31), channel_id=1, source_target_pairs={{0,25},{1,26},{2,27},{3,28},{4,29},{5,30},{6,31},{7,0},{8,1},{9,2}... | collective-permute-start | bytes 884744 | tf_op jit(solution)/shard_map/ppermute | solution.py:134
  491.1 11.1 %collective-permute-start.25 = (bf16[72,2048]{1,0:T(8,128)(2,1)}, bf16[72,2048]{1,0:T(8,128)(2,1)S(1)}, u32[]{:S(2)}, u32[]{:S(2)}) collective-permute-start(bf16[72,2048]{1,0:T(8,128)(2,1)} %get-tuple-element.30), channel_id=1, source_target_pairs={{0,26},{1,27},{2,28},{3,29},{4,30},{5,31},{6,0},{7,1},{8,2},{9,3},... | collective-permute-start | bytes 884744 | tf_op jit(solution)/shard_map/ppermute | solution.py:134
  502.2 11.1 %collective-permute-start.26 = (bf16[72,2048]{1,0:T(8,128)(2,1)}, bf16[72,2048]{1,0:T(8,128)(2,1)S(1)}, u32[]{:S(2)}, u32[]{:S(2)}) collective-permute-start(bf16[72,2048]{1,0:T(8,128)(2,1)} %get-tuple-element.29), channel_id=1, source_target_pairs={{0,27},{1,28},{2,29},{3,30},{4,31},{5,0},{6,1},{7,2},{8,3},{9,4},{... | collective-permute-start | bytes 884744 | tf_op jit(solution)/shard_map/ppermute | solution.py:134
  526.8 3.9 copy-start.4
Sparse Core Ops, SparseCore 0:
  11.8 96.9 all-gather.10
  111.6 52.3 all-gather.12
  175.9 25.5 reduce-scatter.4
  222.9 37.3 reduce-scatter.2
  405.8 30.7 all-gather.8
  465.0 43.5 all-gather.6

commit v9 on v5

--- a/solution.py
+++ b/solution.py
@@ -127,47 +127,47 @@
         weight_pair,
         weight_down,
     )
-    returned = lax.all_to_all(
+    dense = jnp.einsum(
+        "srt,src->stc",
+        pick_b,
         row_grads.reshape(expert_count, capacity, model_width),
+        preferred_element_type=jnp.float32,
+    ).astype(jnp.bfloat16)
+    token_grad = lax.psum_scatter(
+        dense.reshape(expert_count * local_tokens, model_width),
         "expert",
-        split_axis=0,
-        concat_axis=0,
+        scatter_dimension=0,
         tiled=True,
     )
 
-    own_match = (
-        expert_ids[:, :, None] == jnp.arange(expert_count, dtype=jnp.int32)[None, None, :]
-    )
-    own_routed = jnp.any(own_match, axis=1).astype(jnp.float32)
-    own_rank = exclusive_count(own_routed.T).T
-    own_pick = (own_routed[:, :, None] > 0) & (
-        own_rank[:, :, None] == slots[None, None, :]
-    )
-    own_pick = own_pick.astype(jnp.bfloat16).reshape(local_tokens, slot_total)
-    token_grad = jnp.dot(
-        own_pick, returned.reshape(slot_total, model_width), preferred_element_type=jnp.float32
-    ).astype(jnp.bfloat16)
-
-    sum_pair, sum_down = (
-        lax.psum_scatter(
-            grad_pair[None].astype(jnp.bfloat16), "group", scatter_dimension=1, tiled=True
-        ).astype(jnp.float32),
-        lax.psum_scatter(
-            grad_down[None].astype(jnp.bfloat16), "group", scatter_dimension=2, tiled=True
-        ).astype(jnp.float32),
-    )
+    groups = lax.axis_size("group")
+    share_rows = model_width // groups
+    hidden_count = grad_down.shape[0]
+    pair_width = grad_pair.shape[1]
+    pair_parts = lax.all_to_all(
+        grad_pair.astype(jnp.bfloat16).reshape(groups, share_rows, pair_width),
+        "group", 0, 0, tiled=True,
+    )
+    down_parts = lax.all_to_all(
+        grad_down.astype(jnp.bfloat16).reshape(hidden_count, groups, share_rows),
+        "group", 1, 1, tiled=True,
+    )
+    sum_pair = jnp.sum(pair_parts.astype(jnp.float32), axis=0)[None]
+    sum_down = jnp.sum(down_parts.astype(jnp.float32), axis=1)[None]
     group_index = lax.axis_index("group")
-    share_rows = model_width // lax.axis_size("group")
     own_pair = lax.dynamic_slice_in_dim(gate_up, group_index * share_rows, share_rows, 1)
     own_down = lax.dynamic_slice_in_dim(down_weight, group_index * share_rows, share_rows, 2)
     new_pair, first_pair, second_pair = adam_update(
         own_pair, sum_pair, gate_up_moment, gate_up_second
     )
     new_down, first_down, second_down = adam_update(own_down, sum_down, down_moment, down_second)
-    full_pair, full_down = (
-        lax.all_gather(new_pair, "group", axis=1, tiled=True),
-        lax.all_gather(new_down, "group", axis=2, tiled=True),
-    )
+    full_pair = lax.all_to_all(
+        jnp.broadcast_to(new_pair, (groups, share_rows, pair_width)), "group", 0, 0, tiled=True
+    ).reshape(1, model_width, pair_width)
+    full_down = lax.all_to_all(
+        jnp.broadcast_to(new_down.reshape(hidden_count, 1, share_rows), (hidden_count, groups, share_rows)),
+        "group", 1, 1, tiled=True,
+    ).reshape(1, hidden_count, model_width)
     return (token_grad, full_pair, full_down, first_pair, second_pair, first_down, second_down)
 
 

time: 375 us -> 361 us (0.963); the launches traced: 374 us -> 356 us
  waiting for transfers between devices: 234 us -> 175 us
  local copies, waits for them, and re-layouts: 22.7 us -> 41.2 us
  starting transfers between devices: 7.71 us -> 20.9 us
  matrix products: 71.2 us -> 78.7 us
    all_gather x2 -> x0, waiting for transfers between devices: 24.4 us -> none  [the longest x1 24.4 us: local(): lax.all_gather(new_down, 'group', axis=2, tiled=True)]
    reduce_scatter x2 -> x1, waiting for transfers between devices: 22 us -> 0.01 us  [local(): lax.psum_scatter(dense.reshape(expert_count * local_tokens, model_width),...]
    dot_general x0 -> x2, local copies, waits for them, and re-layouts: none -> 13.8 us  [expert_backward(): jnp.dot(hidden_act.T, part, preferred_element_type=jnp.float32)]
    all_to_all x1 -> x4, starting transfers between devices: 7.2 us -> 20.8 us  [the longest x1 5.76 us: local(): lax.all_to_all(jnp.broadcast_to(new_down.reshape(hidden_count, 1, share_r...]
    all_to_all x1 -> x4, waiting for transfers between devices: 90.9 us -> 79.2 us  [the longest x1 30.8 us: local(): lax.all_to_all(grad_pair.astype(jnp.bfloat16).reshape(groups, share_rows,...]
    convert_element_type x2 -> x0, other arithmetic: 7.27 us -> none  [adam_update(): updated = (weight.astype(jnp.float32) - learn_rate * first_new / (jnp.sqr...]
    broadcast_in_dim x0 -> x2, other arithmetic: none -> 7.05 us  [the longest x1 3.89 us: local(): jnp.broadcast_to(new_pair, (groups, share_rows, pair_width))]
    dot_general x2, matrix products: 4.86 us -> 10.1 us  [expert_backward(): jnp.dot(hidden_act.T, part, preferred_element_type=jnp.float32)]
  transfers between devices with their start and end apart: 7 -> 7, of which waited for: 5 -> 6; matrix products, arithmetic and copies ran while one was open for 25% -> 30% of each run, Pallas kernels for 0% -> 0%
where the time goes in v9:
time: 361 us; the launch traced here: 356 us
  waiting for transfers between devices  175 us (48%)
  matrix products  78.7 us (22%)
  local copies, waits for them, and re-layouts  41.2 us (11%)
  other arithmetic  26.3 us (7%)
  starting transfers between devices  20.9 us (6%)
  between operations  14 us (4%)
    all_gather x1, waiting for transfers between devices, local(): lax.all_gather(jnp.concatenate([tokens, cotangent[:, :half_width], meta],...  95.1 us
    all_to_all x1, waiting for transfers between devices, local(): lax.all_to_all(grad_pair.astype(jnp.bfloat16).reshape(groups, share_rows,...  30.8 us
    all_to_all x1, waiting for transfers between devices, local(): lax.all_to_all(jnp.broadcast_to(new_pair, (groups, share_rows, pair_width...  28.7 us
    dot_general x1, matrix products, local(): jnp.einsum('srt,stc->src', pick_b, first, preferred_element_type=jnp.floa...  15.5 us
    dot_general x2, local copies, waits for them, and re-layouts, expert_backward(): jnp.dot(hidden_act.T, part, preferred_element_type=jnp.float32)  13.8 us
    dot_general x1, matrix products, expert_backward(): jnp.dot(inputs.T, pair_grad, preferred_element_type=jnp.float32)  12.5 us
    all_to_all x1, waiting for transfers between devices, local(): lax.all_to_all(jnp.broadcast_to(new_down.reshape(hidden_count, 1, share_r...  12.3 us
    dot_general x1, matrix products, expert_backward(): jnp.dot(pair_grad, weight_gate_up.T, preferred_element_type=jnp.float32)  11.2 us
  transfers between devices with their start and end apart: 7, of which 6 were waited for; matrix products, arithmetic and copies ran while one was open for 30% of the time, Pallas kernels for 0%

profile of v9, /device:TPU:50, one launch (start us, length us, event | category | flops | bytes accessed | tf_op | source)
XLA Modules:
  0.0 356.1 jit_solution(2787619116331366528)
XLA Ops:
  7.2 0.0 copy-start.14
  7.2 0.0 all-gather.5.cloned.1.call-start
  7.2 0.7 reduce-precision_convert_fusion.1
  8.0 0.7 convert_convert_fusion.2
  8.7 0.1 copy.35
  8.8 1.0 slice.39
  9.8 2.0 fusion.24
  11.8 0.0 all-gather.5.cloned.1.call-update
  11.8 0.0 all-gather.7.cloned.1.call-start
  11.8 95.1 %all-gather.5.cloned.1.call-done = bf16[4096,3200]{1,0:T(8,128)(2,1)} async-done(((bf16[128,3200]{1,0:T(8,128)(2,1)}), bf16[4096,3200]{1,0:T(8,128)(2,1)}) %all-gather.5.cloned.1.call-update) | async-done | bytes 26214416 | tf_op jit(solution)/shard_map/all_gather | solution.py:87
  106.9 0.7 slice.47
  107.7 0.0 all-gather.7.cloned.1.call-update
  107.7 0.0 reduce-scatter.2.cloned.1.call-start
  107.7 1.5 slice_convert_fusion.1
  109.2 3.0 fusion.5
  112.2 0.6 reduce_or.9
  112.8 0.0 copy-start.17
  112.8 0.1 fusion.38
  113.0 0.5 copy-done.17
  113.4 15.5 %convolution_convert_fusion.1 = bf16[32,72,3200]{2,1,0:T(8,128)(2,1)} fusion(bf16[32,128,3200]{2,1,0:T(8,128)(2,1)} %bitcast.62, f32[32,128]{1,0:T(8,128)S(1)} %fusion.38, pred[32,128]{1,0:T(8,128)(4,1)S(1)} %convert_compare_fusion), kind=kOutput, calls=%fused_computation.1 | convolution fusion | flops 1895399424 | bytes 40980480 | tf_op jit(solution)/shard_map/srt,stc->src/dot_general | solution.py:107
  128.9 9.5 %slice.59 = bf16[32,72,2048]{2,1,0:T(8,128)(2,1)} slice(bf16[32,72,3200]{2,1,0:T(8,128)(2,1)} %convolution_convert_fusion.1), slice={[0:32], [0:72], [0:2048]} | slice | bytes 18874368 | tf_op jit(solution)/shard_map/slice | solution.py:110
  138.4 10.0 %fusion.2 = f32[2304,768]{0,1:T(8,128)S(1)} fusion(bf16[2304,2048]{1,0:T(8,128)(2,1)} %bitcast.67, bf16[1,2048,768]{2,1,0:T(8,128)(2,1)S(1)} %copy-done.15), kind=kOutput, calls=%fused_computation.16 | convolution fusion | flops 7247757312 | bytes 19660800 | tf_op jit(solution)/shard_map/dot_general | solution.py:15
  148.4 0.0 copy-start.18
  148.4 0.0 copy-start.20
  148.4 3.2 fusion
  151.7 0.6 select_reduce_fusion
  152.3 0.0 copy-start.16
  152.3 3.5 multiply_convert_fusion.1
  155.8 2.1 copy-done.2
  157.9 3.8 %fusion.27 = f32[2304,384]{0,1:T(8,128)} fusion(bf16[2304,1024]{1,0:T(8,128)(2,1)S(1)} %bitcast.64, bf16[384,2048]{1,0:T(8,128)(2,1)S(1)} %bitcast.74), kind=kOutput, calls=%fused_computation.47 | convolution fusion | flops 1811939328 | bytes 9043968 | tf_op jit(solution)/shard_map/dot_general | solution.py:22
  161.7 0.6 all-gather.7.cloned.1.call-done
  162.3 4.9 %multiply_convert_fusion = bf16[32,72,1024]{2,1,0:T(8,128)(2,1)S(1)} fusion(f32[32,72]{1,0:T(8,128)} %copy-done.16, bf16[32,128,1024]{2,1,0:T(8,128)(2,1)} %bitcast.69, f32[32,128]{1,0:T(8,128)S(1)} %fusion.38, pred[32,128]{1,0:T(8,128)(4,1)} %copy-done.17), kind=kOutput, calls=%fused_computation.3 | convolution fusion | flops 614006784 | bytes 13136896 | tf_op jit(solution)/shard_map/srt,stc->src/dot_general | solution.py:112
  167.3 0.5 copy-done.3
  167.8 0.4 copy-done.12
  168.2 2.4 multiply_convert_fusion.3
  170.7 11.2 %convolution_convert_fusion.2 = bf16[2304,2048]{1,0:T(8,128)(2,1)S(1)} fusion(bf16[1,2048,768]{2,1,0:T(8,128)(2,1)} %param.14, bf16[2304,384]{0,1:T(8,128)(2,1)S(1)} %get-tuple-element.36, bf16[2304,384]{0,1:T(8,128)(2,1)S(1)} %get-tuple-element.35), kind=kOutput, calls=%fused_computation.2 | convolution fusion | flops 7259553792 | bytes 16121856 | tf_op jit(solution)/shard_map/dot_general | solution.py:37
  181.9 8.2 %convolution_convert_fusion = bf16[32,128,2048]{2,1,0:T(8,128)(2,1)} fusion(bf16[32,72,2048]{2,1,0:T(8,128)(2,1)S(1)} %bitcast.63, f32[32,128]{1,0:T(8,128)S(1)} %fusion.38, pred[32,128]{1,0:T(8,128)(4,1)S(1)} %copy-done.19), kind=kOutput, calls=%fused_computation | convolution fusion | flops 1216937984 | bytes 26234880 | tf_op jit(solution)/shard_map/srt,src->stc/dot_general | solution.py:130
  190.1 0.0 reduce-scatter.2.cloned.1.call-update
  190.1 6.9 %copy.30 = bf16[1024,2304]{1,0:T(8,128)(2,1)} copy(bf16[1024,2304]{0,1:T(8,128)(2,1)} %bitcast.65) | data formatting | bytes 9437184 | tf_op jit(solution)/shard_map/dot_general | solution.py:33
  197.0 5.2 %fusion.14 = bf16[384,2,512]{2,0,1:T(8,128)(2,1)} fusion(bf16[2,512,2304]{2,1,0:T(8,128)(2,1)} %bitcast.72, bf16[2304,384]{0,1:T(8,128)(2,1)S(1)} %copy-done.8), kind=kOutput, calls=%fused_computation.37 | convolution fusion | flops 1812332544 | bytes 7274496 | tf_op jit(solution)/shard_map/dot_general | solution.py:33
  202.2 6.9 %copy.31 = bf16[1024,2304]{1,0:T(8,128)(2,1)} copy(bf16[1024,2304]{0,1:T(8,128)(2,1)} %bitcast.60) | data formatting | bytes 9437184 | tf_op jit(solution)/shard_map/dot_general | solution.py:33
  209.2 4.9 %fusion.17 = bf16[384,2,512]{2,0,1:T(8,128)(2,1)S(1)} fusion(bf16[2,512,2304]{2,1,0:T(8,128)(2,1)} %bitcast.71, bf16[2304,384]{0,1:T(8,128)(2,1)S(1)} %copy-done.8), kind=kOutput, calls=%fused_computation.38 | convolution fusion | flops 1812332544 | bytes 7274496 | tf_op jit(solution)/shard_map/dot_general | solution.py:33
  214.1 1.3 pad_maximum_fusion.3
  215.4 4.8 %all-to-all-start.2 = ((bf16[384,4,512]{2,0,1:T(8,128)(2,1)}), bf16[384,4,512]{2,0,1:T(8,128)(2,1)S(1)}, u32[]{:S(2)}, u32[]{:S(2)}) async-start(bf16[384,4,512]{2,0,1:T(8,128)(2,1)} %pad_maximum_fusion.3), calls=%async_computation.3 | async-start | bytes 3145728 | tf_op jit(solution)/shard_map/all_to_all | solution.py:151
  220.2 12.5 %convolution_convert_fusion.3 = bf16[2048,768]{1,0:T(8,128)(2,1)} fusion(bf16[2304,2048]{1,0:T(8,128)(2,1)} %bitcast.68, bf16[2304,384]{0,1:T(8,128)(2,1)} %copy-done.7, bf16[2304,384]{0,1:T(8,128)(2,1)S(1)} %copy-done.6), kind=kOutput, calls=%fused_computation.14 | convolution fusion | flops 7256408064 | bytes 16121856 | tf_op jit(solution)/shard_map/dot_general | solution.py:36
  232.6 7.3 %all-to-all-done.2 = bf16[384,4,512]{2,0,1:T(8,128)(2,1)S(1)} async-done(((bf16[384,4,512]{2,0,1:T(8,128)(2,1)}), bf16[384,4,512]{2,0,1:T(8,128)(2,1)S(1)}, u32[]{:S(2)}, u32[]{:S(2)}) %all-to-all-start.2) | async-done | bytes 1572896 | tf_op jit(solution)/shard_map/all_to_all | solution.py:151
  239.9 1.1 copy-done.4
  241.0 5.1 %all-to-all-start = ((bf16[4,512,768]{2,1,0:T(8,128)(2,1)}), bf16[4,512,768]{2,1,0:T(8,128)(2,1)S(1)}, u32[]{:S(2)}, u32[]{:S(2)}) async-start(bf16[4,512,768]{2,1,0:T(8,128)(2,1)} %bitcast.73), calls=%async_computation.1 | async-start | bytes 6291456 | tf_op jit(solution)/shard_map/all_to_all | solution.py:147
  246.2 1.8 convert_reduce_fusion.1
  247.9 3.2 fusion.37
  251.1 30.8 %all-to-all-done = bf16[4,512,768]{2,1,0:T(8,128)(2,1)S(1)} async-done(((bf16[4,512,768]{2,1,0:T(8,128)(2,1)}), bf16[4,512,768]{2,1,0:T(8,128)(2,1)S(1)}, u32[]{:S(2)}, u32[]{:S(2)}) %all-to-all-start) | async-done | bytes 3145760 | tf_op jit(solution)/shard_map/all_to_all | solution.py:147
  281.9 1.3 broadcast_in_dim.46
  283.2 5.8 %all-to-all-start.3 = ((bf16[384,4,512]{2,0,1:T(8,128)(2,1)}), bf16[384,4,512]{2,0,1:T(8,128)(2,1)}, u32[]{:S(2)}, u32[]{:S(2)}) async-start(bf16[384,4,512]{2,0,1:T(8,128)(2,1)} %broadcast_in_dim.46), calls=%async_computation.4 | async-start | bytes 3145728 | tf_op jit(solution)/shard_map/all_to_all | solution.py:167
  289.0 0.4 convert_reduce_fusion
  289.4 1.0 copy-done.9
  290.4 0.5 copy-done.10
  290.8 3.9 %fusion.30 = (bf16[512,768]{1,0:T(8,128)(2,1)S(1)}, f32[1,512,768]{2,1,0:T(8,128)}, f32[1,512,768]{2,1,0:T(8,128)}) fusion(bf16[1,2048,768]{2,1,0:T(8,128)(2,1)} %param.14, s32[]{:T(128)S(6)} %select_n.14, f32[512,768]{1,0:T(8,128)S(1)} %convert_reduce_fusion, f32[1,512,768]{2,1,0:T(8,128)S(1)} %copy-done.9, f32[1,512,768]{2,1,0:T(8,128)S(1)} %copy-done.10), kind=kLoop, calls=%fused_computation.52 | loop fusion | flops 5111808 | bytes 9437188 | tf_op jit(solution)/shard_map/broadcast_in_dim | solution.py:165
  294.7 12.3 %all-to-all-done.3 = bf16[384,4,512]{2,0,1:T(8,128)(2,1)} async-done(((bf16[384,4,512]{2,0,1:T(8,128)(2,1)}), bf16[384,4,512]{2,0,1:T(8,128)(2,1)}, u32[]{:S(2)}, u32[]{:S(2)}) %all-to-all-start.3) | async-done | bytes 1572896 | tf_op jit(solution)/shard_map/all_to_all | solution.py:167
  307.0 1.9 broadcast_in_dim.44
  308.9 5.1 %all-to-all-start.1 = ((bf16[4,512,768]{2,1,0:T(8,128)(2,1)}), bf16[4,512,768]{2,1,0:T(8,128)(2,1)S(1)}, u32[]{:S(2)}, u32[]{:S(2)}) async-start(bf16[4,512,768]{2,1,0:T(8,128)(2,1)} %broadcast_in_dim.44), calls=%async_computation.2 | async-start | bytes 6291456 | tf_op jit(solution)/shard_map/all_to_all | solution.py:164
  314.0 2.6 copy.32
  316.6 2.6 copy.33
  319.2 28.7 %all-to-all-done.1 = bf16[4,512,768]{2,1,0:T(8,128)(2,1)S(1)} async-done(((bf16[4,512,768]{2,1,0:T(8,128)(2,1)}), bf16[4,512,768]{2,1,0:T(8,128)(2,1)S(1)}, u32[]{:S(2)}, u32[]{:S(2)}) %all-to-all-start.1) | async-done | bytes 3145760 | tf_op jit(solution)/shard_map/all_to_all | solution.py:164
  347.9 1.7 copy.37
  (33 shorter events, 0.1 us)
Async XLA Ops:
  7.2 99.8 %copy-start.14 = (bf16[128,2048]{1,0:T(8,128)(2,1)S(1)}, bf16[128,2048]{1,0:T(8,128)(2,1)}, u32[]{:S(2)}) copy-start(bf16[128,2048]{1,0:T(8,128)(2,1)} %param.11) | copy-start | bytes 1572868
  7.2 99.8 %all-gather.5.cloned.1.call-start = ((), (), s32[]{:S(2)}) async-start(), calls=%async_computation.6 | async-start | bytes 27033600 | tf_op jit(solution)/shard_map/all_gather | solution.py:87
  11.8 150.5 %all-gather.7.cloned.1.call-start = ((), (), s32[]{:S(2)}) async-start(), calls=%async_computation.7 | async-start | bytes 8650752 | tf_op jit(solution)/shard_map/all_gather | solution.py:91
  107.7 240.3 %reduce-scatter.2.cloned.1.call-start = ((), (), s32[]{:S(2)}) async-start(), calls=%async_computation.5 | async-start | bytes 17301504 | tf_op jit(solution)/shard_map/reduce_scatter | solution.py:136
  112.8 0.6 copy-start.17
  128.9 9.5 %copy-start.15 = (bf16[1,2048,768]{2,1,0:T(8,128)(2,1)S(1)}, bf16[1,2048,768]{2,1,0:T(8,128)(2,1)}, u32[]{:S(2)}) copy-start(bf16[1,2048,768]{2,1,0:T(8,128)(2,1)} %param.14) | copy-start | bytes 9437188
  148.4 3.2 copy-start.18
  148.4 3.2 copy-start.20
  152.3 3.5 copy-start.16
  152.3 5.6 %copy-start.11 = (bf16[1,384,2048]{2,1,0:T(8,128)(2,1)S(1)}, bf16[1,384,2048]{2,1,0:T(8,128)(2,1)}, u32[]{:S(2)}) copy-start(bf16[1,384,2048]{2,1,0:T(8,128)(2,1)} %param.15) | copy-start | bytes 4718596
  155.8 2.1 copy-start.2
  162.3 5.0 %copy-start.1 = (f32[2304,384]{0,1:T(8,128)S(1)}, f32[2304,384]{0,1:T(8,128)}, u32[]{:S(2)}) copy-start(f32[2304,384]{0,1:T(8,128)} %get-tuple-element.14) | copy-start | bytes 10616836
  162.3 5.5 %copy-start.3 = (f32[2304,384]{0,1:T(8,128)S(1)}, f32[2304,384]{0,1:T(8,128)}, u32[]{:S(2)}) copy-start(f32[2304,384]{0,1:T(8,128)} %fusion.27) | copy-start | bytes 10616836
  162.3 5.9 %copy-start.12 = (bf16[1,384,2048]{2,1,0:T(8,128)(2,1)S(1)}, bf16[1,384,2048]{2,1,0:T(8,128)(2,1)}, u32[]{:S(2)}) copy-start(bf16[1,384,2048]{2,1,0:T(8,128)(2,1)} %param.15) | copy-start | bytes 4718596
  167.3 3.4 copy-start
  170.6 11.2 %copy-start.5 = (bf16[2304,384]{0,1:T(8,128)(2,1)}, bf16[2304,384]{0,1:T(8,128)(2,1)S(1)}, u32[]{:S(2)}) copy-start(bf16[2304,384]{0,1:T(8,128)(2,1)S(1)} %get-tuple-element.35) | copy-start | bytes 5308420
  170.7 11.2 %copy-start.7 = (bf16[2304,384]{0,1:T(8,128)(2,1)}, bf16[2304,384]{0,1:T(8,128)(2,1)S(1)}, u32[]{:S(2)}) copy-start(bf16[2304,384]{0,1:T(8,128)(2,1)S(1)} %get-tuple-element.36) | copy-start | bytes 5308420
  170.7 11.2 %copy-start.19 = (pred[32,128]{1,0:T(8,128)(4,1)S(1)}, pred[32,128]{1,0:T(8,128)(4,1)}, u32[]{:S(2)}) copy-start(pred[32,128]{1,0:T(8,128)(4,1)} %copy-done.17) | copy-start | bytes 12292
  190.1 6.9 %copy-start.8 = (bf16[2304,384]{0,1:T(8,128)(2,1)S(1)}, bf16[2304,384]{0,1:T(8,128)(2,1)}, u32[]{:S(2)}) copy-start(bf16[2304,384]{0,1:T(8,128)(2,1)} %get-tuple-element.16) | copy-start | bytes 5308420
  209.2 4.9 %copy-start.13 = (bf16[384,2,512]{2,0,1:T(8,128)(2,1)S(1)}, bf16[384,2,512]{2,0,1:T(8,128)(2,1)}, u32[]{:S(2)}) copy-start(bf16[384,2,512]{2,0,1:T(8,128)(2,1)} %fusion.14) | copy-start | bytes 2359300
  214.1 6.1 %copy-start.6 = (bf16[2304,384]{0,1:T(8,128)(2,1)S(1)}, bf16[2304,384]{0,1:T(8,128)(2,1)}, u32[]{:S(2)}) copy-start(bf16[2304,384]{0,1:T(8,128)(2,1)} %copy-done.5) | copy-start | bytes 5308420
  215.4 24.5 %all-to-all-start.2 = ((bf16[384,4,512]{2,0,1:T(8,128)(2,1)}), bf16[384,4,512]{2,0,1:T(8,128)(2,1)S(1)}, u32[]{:S(2)}, u32[]{:S(2)}) async-start(bf16[384,4,512]{2,0,1:T(8,128)(2,1)} %pad_maximum_fusion.3), calls=%async_computation.3 | async-start | bytes 3145728 | tf_op jit(solution)/shard_map/all_to_all | solution.py:151
  239.9 1.1 copy-start.4
  241.0 40.9 %all-to-all-start = ((bf16[4,512,768]{2,1,0:T(8,128)(2,1)}), bf16[4,512,768]{2,1,0:T(8,128)(2,1)S(1)}, u32[]{:S(2)}, u32[]{:S(2)}) async-start(bf16[4,512,768]{2,1,0:T(8,128)(2,1)} %bitcast.73), calls=%async_computation.1 | async-start | bytes 6291456 | tf_op jit(solution)/shard_map/all_to_all | solution.py:147
  283.2 23.8 %all-to-all-start.3 = ((bf16[384,4,512]{2,0,1:T(8,128)(2,1)}), bf16[384,4,512]{2,0,1:T(8,128)(2,1)}, u32[]{:S(2)}, u32[]{:S(2)}) async-start(bf16[384,4,512]{2,0,1:T(8,128)(2,1)} %broadcast_in_dim.46), calls=%async_computation.4 | async-start | bytes 3145728 | tf_op jit(solution)/shard_map/all_to_all | solution.py:167
  289.0 1.4 copy-start.9
  289.0 1.9 copy-start.10
  308.9 39.0 %all-to-all-start.1 = ((bf16[4,512,768]{2,1,0:T(8,128)(2,1)}), bf16[4,512,768]{2,1,0:T(8,128)(2,1)S(1)}, u32[]{:S(2)}, u32[]{:S(2)}) async-start(bf16[4,512,768]{2,1,0:T(8,128)(2,1)} %broadcast_in_dim.44), calls=%async_computation.2 | async-start | bytes 6291456 | tf_op jit(solution)/shard_map/all_to_all | solution.py:164
Sparse Core Ops, SparseCore 0:
  11.9 94.9 all-gather.4
  109.8 52.5 all-gather.6
  190.3 114.6 reduce-scatter.1

commit v10 on v9

--- a/solution.py
+++ b/solution.py
@@ -164,10 +164,7 @@
     full_pair = lax.all_to_all(
         jnp.broadcast_to(new_pair, (groups, share_rows, pair_width)), "group", 0, 0, tiled=True
     ).reshape(1, model_width, pair_width)
-    full_down = lax.all_to_all(
-        jnp.broadcast_to(new_down.reshape(hidden_count, 1, share_rows), (hidden_count, groups, share_rows)),
-        "group", 1, 1, tiled=True,
-    ).reshape(1, hidden_count, model_width)
+    full_down = lax.all_gather(new_down, "group", axis=2, tiled=True)
     return (token_grad, full_pair, full_down, first_pair, second_pair, first_down, second_down)
 
 

time: 361 us -> 379 us (1.050)
  blocking collectives: 0 us -> 40.1 us
  starting transfers between devices: 20.9 us -> 10.1 us
  local copies, waits for them, and re-layouts: 41.2 us -> 33.3 us
  waiting for transfers between devices: 175 us -> 168 us
    all_to_all x2 -> x0, waiting for transfers between devices: 43.2 us -> none  [the longest x1 30.8 us: local(): lax.all_to_all(grad_pair.astype(jnp.bfloat16).reshape(groups, share_rows,...]
    all_to_all x0 -> x1, blocking collectives: none -> 40.1 us  [local(): lax.all_to_all(grad_pair.astype(jnp.bfloat16).reshape(groups, share_rows,...]
    reduce_scatter x1, waiting for transfers between devices: 0.01 us -> 27.4 us  [local(): lax.psum_scatter(dense.reshape(expert_count * local_tokens, model_width),...]
    all_to_all x2 -> x0, starting transfers between devices: 10.9 us -> none  [the longest x1 5.76 us: local(): lax.all_to_all(jnp.broadcast_to(new_down.reshape(hidden_count, 1, share_r...]
    all_to_all x1, waiting for transfers between devices: 28.7 us -> 35.2 us  [local(): lax.all_to_all(jnp.broadcast_to(new_pair, (groups, share_rows, pair_width...]
    unnamed x45 -> x35, local copies, waits for them, and re-layouts: 10.5 us -> 6.75 us
  transfers between devices with their start and end apart: 7 -> 6, of which waited for: 6 -> 4; matrix products, arithmetic and copies ran while one was open for 30% -> 28% of each run, Pallas kernels for 0% -> 0%
where the time goes in v10:
time: 379 us; the launch traced here: 375 us
  waiting for transfers between devices  168 us (44%)
  matrix products  81.1 us (21%)
  blocking collectives  40.1 us (11%)
  local copies, waits for them, and re-layouts  33.3 us (9%)
  other arithmetic  28.5 us (8%)
  between operations  14 us (4%)
  starting transfers between devices  10.1 us (3%)
    all_gather x1, waiting for transfers between devices, local(): lax.all_gather(jnp.concatenate([tokens, cotangent[:, :half_width], meta],...  95.1 us
    all_to_all x1, blocking collectives, local(): lax.all_to_all(grad_pair.astype(jnp.bfloat16).reshape(groups, share_rows,...  40.1 us
    all_to_all x1, waiting for transfers between devices, local(): lax.all_to_all(jnp.broadcast_to(new_pair, (groups, share_rows, pair_width...  35.2 us
    reduce_scatter x1, waiting for transfers between devices, local(): lax.psum_scatter(dense.reshape(expert_count * local_tokens, model_width),...  27.4 us
    dot_general x1, matrix products, local(): jnp.einsum('srt,stc->src', pick_b, first, preferred_element_type=jnp.floa...  15.4 us
    dot_general x2, local copies, waits for them, and re-layouts, expert_backward(): jnp.dot(hidden_act.T, part, preferred_element_type=jnp.float32)  13.5 us
    dot_general x1, matrix products, expert_backward(): jnp.dot(inputs.T, pair_grad, preferred_element_type=jnp.float32)  10.8 us
    dot_general x2, matrix products, expert_backward(): jnp.dot(hidden_act.T, part, preferred_element_type=jnp.float32)  10.7 us
  transfers between devices with their start and end apart: 6, of which 4 were waited for; matrix products, arithmetic and copies ran while one was open for 28% of the time, Pallas kernels for 0%

profile of v10, /device:TPU:50, one launch (start us, length us, event | category | flops | bytes accessed | tf_op | source)
XLA Modules:
  0.0 375.4 jit_solution(14918053915880986856)
XLA Ops:
  7.2 0.0 copy-start.7
  7.2 0.0 all-gather.8.cloned.1.call-start
  7.2 0.7 reduce-precision_convert_fusion.1
  8.0 0.7 convert_convert_fusion.2
  8.7 0.1 copy.23
  8.8 1.0 slice.39
  9.8 2.0 fusion.24
  11.8 0.0 all-gather.8.cloned.1.call-update
  11.8 0.0 all-gather.10.cloned.1.call-start
  11.8 95.1 %all-gather.8.cloned.1.call-done = bf16[4096,3200]{1,0:T(8,128)(2,1)} async-done(((bf16[128,3200]{1,0:T(8,128)(2,1)}), bf16[4096,3200]{1,0:T(8,128)(2,1)}) %all-gather.8.cloned.1.call-update) | async-done | bytes 26214416 | tf_op jit(solution)/shard_map/all_gather | solution.py:87
  106.9 0.7 slice.47
  107.7 0.0 all-gather.10.cloned.1.call-update
  107.7 1.5 slice_convert_fusion.1
  109.2 3.0 fusion.5
  112.1 0.6 reduce_or.9
  112.8 0.0 copy-start.10
  112.8 0.1 fusion.37
  112.9 0.5 copy-done.10
  113.4 15.4 %convolution_convert_fusion.1 = bf16[32,72,3200]{2,1,0:T(8,128)(2,1)} fusion(bf16[32,128,3200]{2,1,0:T(8,128)(2,1)} %bitcast.61, f32[32,128]{1,0:T(8,128)S(1)} %fusion.37, pred[32,128]{1,0:T(8,128)(4,1)S(1)} %convert_compare_fusion), kind=kOutput, calls=%fused_computation.1 | convolution fusion | flops 1895399424 | bytes 40980480 | tf_op jit(solution)/shard_map/srt,stc->src/dot_general | solution.py:107
  128.8 9.5 %slice.59 = bf16[32,72,2048]{2,1,0:T(8,128)(2,1)} slice(bf16[32,72,3200]{2,1,0:T(8,128)(2,1)} %convolution_convert_fusion.1), slice={[0:32], [0:72], [0:2048]} | slice | bytes 18874368 | tf_op jit(solution)/shard_map/slice | solution.py:110
  138.3 10.0 %fusion.2 = f32[2304,768]{0,1:T(8,128)S(1)} fusion(bf16[2304,2048]{1,0:T(8,128)(2,1)} %bitcast.66, bf16[1,2048,768]{2,1,0:T(8,128)(2,1)S(1)} %copy-done.8), kind=kOutput, calls=%fused_computation.16 | convolution fusion | flops 7247757312 | bytes 19660800 | tf_op jit(solution)/shard_map/dot_general | solution.py:15
  148.3 0.0 copy-start.11
  148.3 0.0 copy-start.13
  148.3 3.2 fusion
  151.6 0.6 select_reduce_fusion
  152.2 0.0 copy-start.9
  152.2 5.5 %multiply_convert_fusion.1 = bf16[32,72,1024]{2,1,0:T(8,128)(2,1)} fusion(bf16[32,72,3200]{2,1,0:T(8,128)(2,1)} %convolution_convert_fusion.1, f32[32,72]{1,0:T(8,128)S(1)} %select_reduce_fusion), kind=kLoop, calls=%fused_computation.4 | loop fusion | flops 7077888 | bytes 9446400 | tf_op jit(solution)/shard_map/convert_element_type | solution.py:117
  157.7 6.7 %copy.20 = bf16[1024,2304]{1,0:T(8,128)(2,1)} copy(bf16[1024,2304]{0,1:T(8,128)(2,1)} %bitcast.63) | data formatting | bytes 9437184 | tf_op jit(solution)/shard_map/dot_general | solution.py:33
  164.4 5.8 %fusion.14 = bf16[384,2,512]{2,0,1:T(8,128)(2,1)} fusion(bf16[2,512,2304]{2,1,0:T(8,128)(2,1)} %bitcast.70, bf16[2304,384]{0,1:T(8,128)(2,1)} %get-tuple-element.16), kind=kOutput, calls=%fused_computation.37 | convolution fusion | flops 1812332544 | bytes 7274496 | tf_op jit(solution)/shard_map/dot_general | solution.py:33
  170.2 7.0 %multiply_convert_fusion = bf16[32,72,1024]{2,1,0:T(8,128)(2,1)} fusion(f32[32,72]{1,0:T(8,128)} %copy-done.9, bf16[32,128,1024]{2,1,0:T(8,128)(2,1)} %bitcast.68, f32[32,128]{1,0:T(8,128)S(1)} %fusion.37, pred[32,128]{1,0:T(8,128)(4,1)} %copy-done.10), kind=kOutput, calls=%fused_computation.3 | convolution fusion | flops 614006784 | bytes 13136896 | tf_op jit(solution)/shard_map/srt,stc->src/dot_general | solution.py:112
  177.2 6.8 %copy.21 = bf16[1024,2304]{1,0:T(8,128)(2,1)} copy(bf16[1024,2304]{0,1:T(8,128)(2,1)} %bitcast.56) | data formatting | bytes 9437184 | tf_op jit(solution)/shard_map/dot_general | solution.py:33
  183.9 5.0 %fusion.17 = bf16[384,2,512]{2,0,1:T(8,128)(2,1)S(1)} fusion(bf16[2,512,2304]{2,1,0:T(8,128)(2,1)} %bitcast.69, bf16[2304,384]{0,1:T(8,128)(2,1)} %get-tuple-element.16), kind=kOutput, calls=%fused_computation.38 | convolution fusion | flops 1812332544 | bytes 7274496 | tf_op jit(solution)/shard_map/dot_general | solution.py:33
  188.9 0.0 copy-done.6
  188.9 1.3 pad_maximum_fusion.3
  190.2 4.9 %all-to-all-start.2 = ((bf16[384,4,512]{2,0,1:T(8,128)(2,1)}), bf16[384,4,512]{2,0,1:T(8,128)(2,1)}, u32[]{:S(2)}, u32[]{:S(2)}) async-start(bf16[384,4,512]{2,0,1:T(8,128)(2,1)} %pad_maximum_fusion.3), calls=%async_computation.3 | async-start | bytes 3145728 | tf_op jit(solution)/shard_map/all_to_all | solution.py:151
  195.1 0.0 copy-start.5
  195.1 4.7 %fusion.27 = f32[2304,384]{0,1:T(8,128)S(1)} fusion(bf16[2304,1024]{1,0:T(8,128)(2,1)} %bitcast.64, bf16[384,2048]{1,0:T(8,128)(2,1)} %bitcast.72), kind=kOutput, calls=%fused_computation.47 | convolution fusion | flops 1811939328 | bytes 9043968 | tf_op jit(solution)/shard_map/dot_general | solution.py:22
  199.9 0.3 copy-done
  200.2 0.4 copy-done.5
  200.6 4.2 %multiply_convert_fusion.3 = (bf16[2304,384]{0,1:T(8,128)(2,1)}, bf16[2304,384]{0,1:T(8,128)(2,1)}) fusion(f32[2304,384]{0,1:T(8,128)S(1)} %copy-done, f32[2304,384]{0,1:T(8,128)S(1)} %get-tuple-element.15, f32[2304,384]{0,1:T(8,128)S(1)} %fusion.27, bf16[2304,1024]{1,0:T(8,128)(2,1)S(1)} %bitcast.59, bf16[384,2048]{1,0:T(8,128)(2,1)S(1)} %bitcast.73), kind=kOutput, calls=%fused_computation.9 | convolution fusion | flops 1816363008 | bytes 19660800 | tf_op jit(solution)/shard_map/dot_general | solution.py:22
  204.8 10.5 %all-to-all-done.2 = bf16[384,4,512]{2,0,1:T(8,128)(2,1)} async-done(((bf16[384,4,512]{2,0,1:T(8,128)(2,1)}), bf16[384,4,512]{2,0,1:T(8,128)(2,1)}, u32[]{:S(2)}, u32[]{:S(2)}) %all-to-all-start.2) | async-done | bytes 1572896 | tf_op jit(solution)/shard_map/all_to_all | solution.py:151
  215.3 1.7 convert_reduce_fusion.1
  217.0 0.0 copy-start.1
  217.0 3.3 subtract_convert_fusion.1
  220.3 0.0 all-gather.6.cloned.1.call-update
  220.3 0.0 reduce-scatter.2.cloned.1.call-start
  220.4 0.0 copy-start.12
  220.4 9.9 %convolution_convert_fusion.2 = bf16[2304,2048]{1,0:T(8,128)(2,1)S(1)} fusion(bf16[1,2048,768]{2,1,0:T(8,128)(2,1)} %param.14, bf16[2304,384]{0,1:T(8,128)(2,1)} %get-tuple-element.29, bf16[2304,384]{0,1:T(8,128)(2,1)S(1)} %copy-done.1), kind=kOutput, calls=%fused_computation.2 | convolution fusion | flops 7259553792 | bytes 16121856 | tf_op jit(solution)/shard_map/dot_general | solution.py:37
  230.2 0.0 copy-done.12
  230.3 8.3 %convolution_convert_fusion = bf16[32,128,2048]{2,1,0:T(8,128)(2,1)} fusion(bf16[32,72,2048]{2,1,0:T(8,128)(2,1)S(1)} %bitcast.62, f32[32,128]{1,0:T(8,128)S(1)} %fusion.37, pred[32,128]{1,0:T(8,128)(4,1)S(1)} %copy-done.12), kind=kOutput, calls=%fused_computation | convolution fusion | flops 1216937984 | bytes 26234880 | tf_op jit(solution)/shard_map/srt,src->stc/dot_general | solution.py:130
  238.5 0.0 reduce-scatter.2.cloned.1.call-update
  238.5 10.8 %convolution_convert_fusion.3 = bf16[2048,768]{1,0:T(8,128)(2,1)S(1)} fusion(bf16[2304,2048]{1,0:T(8,128)(2,1)} %bitcast.67, bf16[2304,384]{0,1:T(8,128)(2,1)} %get-tuple-element.29, bf16[2304,384]{0,1:T(8,128)(2,1)S(1)} %copy-done.1), kind=kOutput, calls=%fused_computation.14 | convolution fusion | flops 7256408064 | bytes 16121856 | tf_op jit(solution)/shard_map/dot_general | solution.py:36
  249.4 40.1 %all_to_all.15 = bf16[4,512,768]{2,1,0:T(8,128)(2,1)S(1)} all-to-all(bf16[4,512,768]{2,1,0:T(8,128)(2,1)S(1)} %bitcast.71), channel_id=1, replica_groups=mesh['group'=4,'expert'=32] {'group'}, dimensions={0} | all-to-all | bytes 6291456 | tf_op jit(solution)/shard_map/all_to_all | solution.py:147
  289.5 0.5 convert_reduce_fusion
  289.9 1.1 copy-done.2
  291.0 0.6 copy-done.3
  291.6 3.9 %fusion.30 = (bf16[512,768]{1,0:T(8,128)(2,1)S(1)}, f32[1,512,768]{2,1,0:T(8,128)}, f32[1,512,768]{2,1,0:T(8,128)}) fusion(bf16[1,2048,768]{2,1,0:T(8,128)(2,1)} %param.14, s32[]{:T(128)S(6)} %select_n.14, f32[512,768]{1,0:T(8,128)S(1)} %convert_reduce_fusion, f32[1,512,768]{2,1,0:T(8,128)S(1)} %copy-done.2, f32[1,512,768]{2,1,0:T(8,128)S(1)} %copy-done.3), kind=kLoop, calls=%fused_computation.52 | loop fusion | flops 5111808 | bytes 9437188 | tf_op jit(solution)/shard_map/broadcast_in_dim | solution.py:165
  295.5 1.9 broadcast_in_dim.37
  297.4 5.1 %all-to-all-start.1 = ((bf16[4,512,768]{2,1,0:T(8,128)(2,1)}), bf16[4,512,768]{2,1,0:T(8,128)(2,1)S(1)}, u32[]{:S(2)}, u32[]{:S(2)}) async-start(bf16[4,512,768]{2,1,0:T(8,128)(2,1)} %broadcast_in_dim.37), calls=%async_computation.2 | async-start | bytes 6291456 | tf_op jit(solution)/shard_map/all_to_all | solution.py:164
  302.5 35.2 %all-to-all-done.1 = bf16[4,512,768]{2,1,0:T(8,128)(2,1)S(1)} async-done(((bf16[4,512,768]{2,1,0:T(8,128)(2,1)}), bf16[4,512,768]{2,1,0:T(8,128)(2,1)S(1)}, u32[]{:S(2)}, u32[]{:S(2)}) %all-to-all-start.1) | async-done | bytes 3145760 | tf_op jit(solution)/shard_map/all_to_all | solution.py:164
  337.7 27.4 %reduce-scatter.2.cloned.1.call-done = bf16[128,2048]{1,0:T(8,128)(2,1)} async-done(((bf16[4096,2048]{1,0:T(8,128)(2,1)}), bf16[128,2048]{1,0:T(8,128)(2,1)}) %reduce-scatter.2.cloned.1.call-update) | async-done | bytes 524304 | tf_op jit(solution)/shard_map/reduce_scatter | solution.py:136
  365.2 1.7 copy.26
  366.8 0.9 copy-done.4
  367.7 1.1 copy.27
  (22 shorter events, 0.1 us)
Async XLA Ops:
  7.2 99.8 %copy-start.7 = (bf16[128,2048]{1,0:T(8,128)(2,1)S(1)}, bf16[128,2048]{1,0:T(8,128)(2,1)}, u32[]{:S(2)}) copy-start(bf16[128,2048]{1,0:T(8,128)(2,1)} %param.11) | copy-start | bytes 1572868
  7.2 99.8 %all-gather.8.cloned.1.call-start = ((), (), s32[]{:S(2)}) async-start(), calls=%async_computation.6 | async-start | bytes 27033600 | tf_op jit(solution)/shard_map/all_gather | solution.py:87
  11.8 158.4 %all-gather.10.cloned.1.call-start = ((), (), s32[]{:S(2)}) async-start(), calls=%async_computation.7 | async-start | bytes 8650752 | tf_op jit(solution)/shard_map/all_gather | solution.py:91
  112.8 0.6 copy-start.10
  128.8 9.5 %copy-start.8 = (bf16[1,2048,768]{2,1,0:T(8,128)(2,1)S(1)}, bf16[1,2048,768]{2,1,0:T(8,128)(2,1)}, u32[]{:S(2)}) copy-start(bf16[1,2048,768]{2,1,0:T(8,128)(2,1)} %param.14) | copy-start | bytes 9437188
  148.3 3.3 copy-start.11
  148.3 3.2 copy-start.13
  152.2 5.5 %copy-start.9 = (f32[32,72]{1,0:T(8,128)}, f32[32,72]{1,0:T(8,128)S(1)}, u32[]{:S(2)}) copy-start(f32[32,72]{1,0:T(8,128)S(1)} %select_reduce_fusion) | copy-start | bytes 27652
  183.9 5.0 %copy-start.6 = (bf16[384,2,512]{2,0,1:T(8,128)(2,1)S(1)}, bf16[384,2,512]{2,0,1:T(8,128)(2,1)}, u32[]{:S(2)}) copy-start(bf16[384,2,512]{2,0,1:T(8,128)(2,1)} %fusion.14) | copy-start | bytes 2359300
  190.2 25.1 %all-to-all-start.2 = ((bf16[384,4,512]{2,0,1:T(8,128)(2,1)}), bf16[384,4,512]{2,0,1:T(8,128)(2,1)}, u32[]{:S(2)}, u32[]{:S(2)}) async-start(bf16[384,4,512]{2,0,1:T(8,128)(2,1)} %pad_maximum_fusion.3), calls=%async_computation.3 | async-start | bytes 3145728 | tf_op jit(solution)/shard_map/all_to_all | solution.py:151
  195.1 107.4 %all-gather.6.cloned.1.call-start = ((), (), s32[]{:S(2)}) async-start(), calls=%async_computation.5 | async-start | bytes 1966080 | tf_op jit(solution)/shard_map/all_gather | solution.py:167
  195.1 4.8 %slice-start = ((s8[4718592]{0:T(1024)(128)(4,1)}), s8[4194304]{0:T(1024)(128)(4,1)S(1)}, s32[]{:S(2)}) async-start(s8[4718592]{0:T(1024)(128)(4,1)} %bitcast.57), calls=%async_computation.8 | async-start | bytes 8388608
  195.1 4.8 %slice-start.1 = ((s8[4718592]{0:T(1024)(128)(4,1)}), s8[524288]{0:T(1024)(128)(4,1)S(1)}, s32[]{:S(2)}) async-start(s8[4718592]{0:T(1024)(128)(4,1)} %bitcast.57), calls=%async_computation.9 | async-start | bytes 1048576
  195.1 5.1 %copy-start = (f32[2304,384]{0,1:T(8,128)S(1)}, f32[2304,384]{0,1:T(8,128)}, u32[]{:S(2)}) copy-start(f32[2304,384]{0,1:T(8,128)} %get-tuple-element.14) | copy-start | bytes 10616836
  195.1 5.5 %copy-start.5 = (bf16[1,384,2048]{2,1,0:T(8,128)(2,1)S(1)}, bf16[1,384,2048]{2,1,0:T(8,128)(2,1)}, u32[]{:S(2)}) copy-start(bf16[1,384,2048]{2,1,0:T(8,128)(2,1)} %param.15) | copy-start | bytes 4718596
  217.0 3.3 copy-start.1
  220.3 144.8 %reduce-scatter.2.cloned.1.call-start = ((), (), s32[]{:S(2)}) async-start(), calls=%async_computation.4 | async-start | bytes 17301504 | tf_op jit(solution)/shard_map/reduce_scatter | solution.py:136
  220.4 9.9 %copy-start.12 = (pred[32,128]{1,0:T(8,128)(4,1)S(1)}, pred[32,128]{1,0:T(8,128)(4,1)}, u32[]{:S(2)}) copy-start(pred[32,128]{1,0:T(8,128)(4,1)} %copy-done.10) | copy-start | bytes 12292
  289.5 1.6 copy-start.2
  289.5 2.2 copy-start.3
  297.4 40.3 %all-to-all-start.1 = ((bf16[4,512,768]{2,1,0:T(8,128)(2,1)}), bf16[4,512,768]{2,1,0:T(8,128)(2,1)S(1)}, u32[]{:S(2)}, u32[]{:S(2)}) async-start(bf16[4,512,768]{2,1,0:T(8,128)(2,1)} %broadcast_in_dim.37), calls=%async_computation.2 | async-start | bytes 6291456 | tf_op jit(solution)/shard_map/all_to_all | solution.py:164
  365.2 2.5 copy-start.4
Sparse Core Ops, SparseCore 0:
  11.9 94.9 all-gather.7
  109.8 52.5 all-gather.9
  220.4 25.4 all-gather.5
  250.3 114.7 reduce-scatter.1

commit v11 on v10

--- a/solution.py
+++ b/solution.py
@@ -154,6 +154,7 @@
     )
     sum_pair = jnp.sum(pair_parts.astype(jnp.float32), axis=0)[None]
     sum_down = jnp.sum(down_parts.astype(jnp.float32), axis=1)[None]
+    token_grad, sum_down = lax.optimization_barrier((token_grad, sum_down))
     group_index = lax.axis_index("group")
     own_pair = lax.dynamic_slice_in_dim(gate_up, group_index * share_rows, share_rows, 1)
     own_down = lax.dynamic_slice_in_dim(down_weight, group_index * share_rows, share_rows, 2)

time: 379 us -> 358 us (0.945)
  blocking collectives: 40.1 us -> 0 us
  waiting for transfers between devices: 168 us -> 181 us
  starting transfers between devices: 10.1 us -> 15.2 us
    all_to_all x1 -> x0, blocking collectives: 40.1 us -> none  [local(): lax.all_to_all(grad_pair.astype(jnp.bfloat16).reshape(groups, share_rows,...]
    all_to_all x0 -> x1, waiting for transfers between devices: none -> 33.1 us  [local(): lax.all_to_all(grad_pair.astype(jnp.bfloat16).reshape(groups, share_rows,...]
    reduce_scatter x1, waiting for transfers between devices: 27.4 us -> 10.2 us  [local(): lax.psum_scatter(dense.reshape(expert_count * local_tokens, model_width),...]
    all_to_all x0 -> x1, starting transfers between devices: none -> 5.13 us  [local(): lax.all_to_all(grad_pair.astype(jnp.bfloat16).reshape(groups, share_rows,...]
    all_to_all x1, waiting for transfers between devices: 35.2 us -> 31.2 us  [local(): lax.all_to_all(jnp.broadcast_to(new_pair, (groups, share_rows, pair_width...]
    unnamed x35 -> x47, local copies, waits for them, and re-layouts: 6.75 us -> 9.97 us
  transfers between devices with their start and end apart: 6 -> 7, of which waited for: 4 -> 7; matrix products, arithmetic and copies ran while one was open for 28% -> 29% of each run, Pallas kernels for 0% -> 0%
where the time goes in v11:
time: 358 us; the launch traced here: 353 us
  waiting for transfers between devices  181 us (51%)
  matrix products  78.7 us (22%)
  local copies, waits for them, and re-layouts  36.8 us (10%)
  other arithmetic  27.3 us (8%)
  starting transfers between devices  15.2 us (4%)
  between operations  14 us (4%)
    all_gather x1, waiting for transfers between devices, local(): lax.all_gather(jnp.concatenate([tokens, cotangent[:, :half_width], meta],...  95.1 us
    all_to_all x1, waiting for transfers between devices, local(): lax.all_to_all(grad_pair.astype(jnp.bfloat16).reshape(groups, share_rows,...  33.1 us
    all_to_all x1, waiting for transfers between devices, local(): lax.all_to_all(jnp.broadcast_to(new_pair, (groups, share_rows, pair_width...  31.2 us
    dot_general x1, matrix products, local(): jnp.einsum('srt,stc->src', pick_b, first, preferred_element_type=jnp.floa...  15.5 us
    dot_general x2, local copies, waits for them, and re-layouts, expert_backward(): jnp.dot(hidden_act.T, part, preferred_element_type=jnp.float32)  13.8 us
    dot_general x1, matrix products, expert_backward(): jnp.dot(inputs.T, pair_grad, preferred_element_type=jnp.float32)  12.5 us
    dot_general x1, matrix products, expert_backward(): jnp.dot(pair_grad, weight_gate_up.T, preferred_element_type=jnp.float32)  11.2 us
    reduce_scatter x1, waiting for transfers between devices, local(): lax.psum_scatter(dense.reshape(expert_count * local_tokens, model_width),...  10.2 us
  transfers between devices with their start and end apart: 7, of which 7 were waited for; matrix products, arithmetic and copies ran while one was open for 29% of the time, Pallas kernels for 0%

profile of v11, /device:TPU:50, one launch (start us, length us, event | category | flops | bytes accessed | tf_op | source)
XLA Modules:
  0.0 352.9 jit_solution(5573102743973560029)
XLA Ops:
  7.2 0.0 copy-start.15
  7.2 0.0 all-gather.8.cloned.1.call-start
  7.2 0.7 reduce-precision_convert_fusion.1
  8.0 0.7 convert_convert_fusion.2
  8.7 0.1 copy.23
  8.8 1.0 slice.39
  9.8 2.0 fusion.24
  11.8 0.0 all-gather.8.cloned.1.call-update
  11.8 0.0 all-gather.10.cloned.1.call-start
  11.8 95.1 %all-gather.8.cloned.1.call-done = bf16[4096,3200]{1,0:T(8,128)(2,1)} async-done(((bf16[128,3200]{1,0:T(8,128)(2,1)}), bf16[4096,3200]{1,0:T(8,128)(2,1)}) %all-gather.8.cloned.1.call-update) | async-done | bytes 26214416 | tf_op jit(solution)/shard_map/all_gather | solution.py:87
  106.9 0.7 slice.47
  107.7 0.0 all-gather.10.cloned.1.call-update
  107.7 0.0 reduce-scatter.2.cloned.1.call-start
  107.7 1.5 slice_convert_fusion.1
  109.2 3.0 fusion.5
  112.2 0.6 reduce_or.9
  112.8 0.1 fusion.36
  113.0 0.5 copy-done.18
  113.4 15.5 %convolution_convert_fusion.1 = bf16[32,72,3200]{2,1,0:T(8,128)(2,1)} fusion(bf16[32,128,3200]{2,1,0:T(8,128)(2,1)} %bitcast.53, f32[32,128]{1,0:T(8,128)S(1)} %fusion.36, pred[32,128]{1,0:T(8,128)(4,1)S(1)} %convert_compare_fusion), kind=kOutput, calls=%fused_computation.1 | convolution fusion | flops 1895399424 | bytes 40980480 | tf_op jit(solution)/shard_map/srt,stc->src/dot_general | solution.py:107
  128.9 9.5 %slice.59 = bf16[32,72,2048]{2,1,0:T(8,128)(2,1)} slice(bf16[32,72,3200]{2,1,0:T(8,128)(2,1)} %convolution_convert_fusion.1), slice={[0:32], [0:72], [0:2048]} | slice | bytes 18874368 | tf_op jit(solution)/shard_map/slice | solution.py:110
  138.4 10.0 %fusion.2 = f32[2304,768]{0,1:T(8,128)S(1)} fusion(bf16[2304,2048]{1,0:T(8,128)(2,1)} %bitcast.58, bf16[1,2048,768]{2,1,0:T(8,128)(2,1)S(1)} %copy-done.16), kind=kOutput, calls=%fused_computation.16 | convolution fusion | flops 7247757312 | bytes 19660800 | tf_op jit(solution)/shard_map/dot_general | solution.py:15
  148.4 0.0 copy-start.19
  148.4 3.2 fusion
  151.6 0.6 select_reduce_fusion
  152.3 0.0 copy-start.17
  152.3 0.0 copy-start.12
  152.3 3.5 multiply_convert_fusion.1
  155.8 2.1 copy-done.2
  157.9 3.8 %fusion.27 = f32[2304,384]{0,1:T(8,128)} fusion(bf16[2304,1024]{1,0:T(8,128)(2,1)S(1)} %bitcast.55, bf16[384,2048]{1,0:T(8,128)(2,1)S(1)} %bitcast.65), kind=kOutput, calls=%fused_computation.47 | convolution fusion | flops 1811939328 | bytes 9043968 | tf_op jit(solution)/shard_map/dot_general | solution.py:22
  161.7 0.7 all-gather.10.cloned.1.call-done
  162.3 4.9 %multiply_convert_fusion = bf16[32,72,1024]{2,1,0:T(8,128)(2,1)S(1)} fusion(f32[32,72]{1,0:T(8,128)} %copy-done.17, bf16[32,128,1024]{2,1,0:T(8,128)(2,1)} %bitcast.60, f32[32,128]{1,0:T(8,128)S(1)} %fusion.36, pred[32,128]{1,0:T(8,128)(4,1)} %copy-done.18), kind=kOutput, calls=%fused_computation.3 | convolution fusion | flops 614006784 | bytes 13136896 | tf_op jit(solution)/shard_map/srt,stc->src/dot_general | solution.py:112
  167.3 0.5 copy-done.3
  167.8 0.4 copy-done.13
  168.2 2.4 multiply_convert_fusion.3
  170.7 11.2 %convolution_convert_fusion.2 = bf16[2304,2048]{1,0:T(8,128)(2,1)S(1)} fusion(bf16[1,2048,768]{2,1,0:T(8,128)(2,1)} %param.14, bf16[2304,384]{0,1:T(8,128)(2,1)S(1)} %get-tuple-element.33, bf16[2304,384]{0,1:T(8,128)(2,1)S(1)} %get-tuple-element.32), kind=kOutput, calls=%fused_computation.2 | convolution fusion | flops 7259553792 | bytes 16121856 | tf_op jit(solution)/shard_map/dot_general | solution.py:37
  181.9 8.2 %convolution_convert_fusion = bf16[32,128,2048]{2,1,0:T(8,128)(2,1)} fusion(bf16[32,72,2048]{2,1,0:T(8,128)(2,1)S(1)} %bitcast.54, f32[32,128]{1,0:T(8,128)S(1)} %fusion.36, pred[32,128]{1,0:T(8,128)(4,1)S(1)} %copy-done.20), kind=kOutput, calls=%fused_computation | convolution fusion | flops 1216937984 | bytes 26234880 | tf_op jit(solution)/shard_map/srt,src->stc/dot_general | solution.py:130
  190.1 0.0 reduce-scatter.2.cloned.1.call-update
  190.1 0.0 copy-start.8
  190.1 6.9 %copy.20 = bf16[1024,2304]{1,0:T(8,128)(2,1)} copy(bf16[1024,2304]{0,1:T(8,128)(2,1)} %bitcast.56) | data formatting | bytes 9437184 | tf_op jit(solution)/shard_map/dot_general | solution.py:33
  197.0 5.2 %fusion.14 = bf16[384,2,512]{2,0,1:T(8,128)(2,1)} fusion(bf16[2,512,2304]{2,1,0:T(8,128)(2,1)} %bitcast.62, bf16[2304,384]{0,1:T(8,128)(2,1)S(1)} %copy-done.8), kind=kOutput, calls=%fused_computation.37 | convolution fusion | flops 1812332544 | bytes 7274496 | tf_op jit(solution)/shard_map/dot_general | solution.py:33
  202.2 7.0 %copy.21 = bf16[1024,2304]{1,0:T(8,128)(2,1)} copy(bf16[1024,2304]{0,1:T(8,128)(2,1)} %bitcast.51) | data formatting | bytes 9437184 | tf_op jit(solution)/shard_map/dot_general | solution.py:33
  209.2 4.9 %fusion.17 = bf16[384,2,512]{2,0,1:T(8,128)(2,1)S(1)} fusion(bf16[2,512,2304]{2,1,0:T(8,128)(2,1)} %bitcast.61, bf16[2304,384]{0,1:T(8,128)(2,1)S(1)} %copy-done.8), kind=kOutput, calls=%fused_computation.38 | convolution fusion | flops 1812332544 | bytes 7274496 | tf_op jit(solution)/shard_map/dot_general | solution.py:33
  214.1 1.3 pad_maximum_fusion.3
  215.4 4.8 %all-to-all-start = ((bf16[384,4,512]{2,0,1:T(8,128)(2,1)}), bf16[384,4,512]{2,0,1:T(8,128)(2,1)S(1)}, u32[]{:S(2)}, u32[]{:S(2)}) async-start(bf16[384,4,512]{2,0,1:T(8,128)(2,1)} %pad_maximum_fusion.3), calls=%async_computation.1 | async-start | bytes 3145728 | tf_op jit(solution)/shard_map/all_to_all | solution.py:151
  220.2 12.5 %convolution_convert_fusion.3 = bf16[2048,768]{1,0:T(8,128)(2,1)} fusion(bf16[2304,2048]{1,0:T(8,128)(2,1)} %bitcast.59, bf16[2304,384]{0,1:T(8,128)(2,1)} %copy-done.7, bf16[2304,384]{0,1:T(8,128)(2,1)S(1)} %copy-done.6), kind=kOutput, calls=%fused_computation.14 | convolution fusion | flops 7256408064 | bytes 16121856 | tf_op jit(solution)/shard_map/dot_general | solution.py:36
  232.7 7.2 %all-to-all-done = bf16[384,4,512]{2,0,1:T(8,128)(2,1)S(1)} async-done(((bf16[384,4,512]{2,0,1:T(8,128)(2,1)}), bf16[384,4,512]{2,0,1:T(8,128)(2,1)S(1)}, u32[]{:S(2)}, u32[]{:S(2)}) %all-to-all-start) | async-done | bytes 1572896 | tf_op jit(solution)/shard_map/all_to_all | solution.py:151
  239.9 1.1 copy-done.4
  241.1 5.1 %all-to-all-start.1 = ((bf16[4,512,768]{2,1,0:T(8,128)(2,1)}), bf16[4,512,768]{2,1,0:T(8,128)(2,1)S(1)}, u32[]{:S(2)}, u32[]{:S(2)}) async-start(bf16[4,512,768]{2,1,0:T(8,128)(2,1)} %bitcast.63), calls=%async_computation.2 | async-start | bytes 6291456 | tf_op jit(solution)/shard_map/all_to_all | solution.py:147
  246.2 2.6 convert_reduce_fusion.1
  248.8 33.1 %all-to-all-done.1 = bf16[4,512,768]{2,1,0:T(8,128)(2,1)S(1)} async-done(((bf16[4,512,768]{2,1,0:T(8,128)(2,1)}), bf16[4,512,768]{2,1,0:T(8,128)(2,1)S(1)}, u32[]{:S(2)}, u32[]{:S(2)}) %all-to-all-start.1) | async-done | bytes 3145760 | tf_op jit(solution)/shard_map/all_to_all | solution.py:147
  281.9 0.4 convert_reduce_fusion
  282.3 1.0 copy-done.9
  283.3 0.5 copy-done.10
  283.8 3.8 %fusion.29 = (bf16[512,768]{1,0:T(8,128)(2,1)S(1)}, f32[1,512,768]{2,1,0:T(8,128)}, f32[1,512,768]{2,1,0:T(8,128)}) fusion(bf16[1,2048,768]{2,1,0:T(8,128)(2,1)} %param.14, s32[]{:T(128)S(6)} %select_n.14, f32[512,768]{1,0:T(8,128)S(1)} %convert_reduce_fusion, f32[1,512,768]{2,1,0:T(8,128)S(1)} %copy-done.9, f32[1,512,768]{2,1,0:T(8,128)S(1)} %copy-done.10), kind=kLoop, calls=%fused_computation.51 | loop fusion | flops 5111808 | bytes 9437188 | tf_op jit(solution)/shard_map/broadcast_in_dim | solution.py:166
  287.6 1.9 broadcast_in_dim.40
  289.5 5.1 %all-to-all-start.2 = ((bf16[4,512,768]{2,1,0:T(8,128)(2,1)}), bf16[4,512,768]{2,1,0:T(8,128)(2,1)S(1)}, u32[]{:S(2)}, u32[]{:S(2)}) async-start(bf16[4,512,768]{2,1,0:T(8,128)(2,1)} %broadcast_in_dim.40), calls=%async_computation.3 | async-start | bytes 6291456 | tf_op jit(solution)/shard_map/all_to_all | solution.py:165
  294.6 10.2 %reduce-scatter.2.cloned.1.call-done = bf16[128,2048]{1,0:T(8,128)(2,1)} async-done(((bf16[4096,2048]{1,0:T(8,128)(2,1)}), bf16[128,2048]{1,0:T(8,128)(2,1)}) %reduce-scatter.2.cloned.1.call-update) | async-done | bytes 524304 | tf_op jit(solution)/shard_map/reduce_scatter | solution.py:136
  304.8 3.3 subtract_convert_fusion.1
  308.1 0.0 all-gather.6.cloned.1.call-update
  308.2 31.2 %all-to-all-done.2 = bf16[4,512,768]{2,1,0:T(8,128)(2,1)S(1)} async-done(((bf16[4,512,768]{2,1,0:T(8,128)(2,1)}), bf16[4,512,768]{2,1,0:T(8,128)(2,1)S(1)}, u32[]{:S(2)}, u32[]{:S(2)}) %all-to-all-start.2) | async-done | bytes 3145760 | tf_op jit(solution)/shard_map/all_to_all | solution.py:165
  339.3 3.4 all-gather.6.cloned.1.call-done
  342.7 1.7 copy.26
  344.4 0.9 copy-done.11
  345.2 1.1 copy.27
  (34 shorter events, 0.1 us)
Async XLA Ops:
  7.2 99.8 %copy-start.15 = (bf16[128,2048]{1,0:T(8,128)(2,1)S(1)}, bf16[128,2048]{1,0:T(8,128)(2,1)}, u32[]{:S(2)}) copy-start(bf16[128,2048]{1,0:T(8,128)(2,1)} %param.11) | copy-start | bytes 1572868
  7.2 99.8 %all-gather.8.cloned.1.call-start = ((), (), s32[]{:S(2)}) async-start(), calls=%async_computation.6 | async-start | bytes 27033600 | tf_op jit(solution)/shard_map/all_gather | solution.py:87
  11.8 150.5 %all-gather.10.cloned.1.call-start = ((), (), s32[]{:S(2)}) async-start(), calls=%async_computation.7 | async-start | bytes 8650752 | tf_op jit(solution)/shard_map/all_gather | solution.py:91
  107.7 197.1 %reduce-scatter.2.cloned.1.call-start = ((), (), s32[]{:S(2)}) async-start(), calls=%async_computation.4 | async-start | bytes 17301504 | tf_op jit(solution)/shard_map/reduce_scatter | solution.py:136
  112.8 0.6 copy-start.18
  128.9 9.5 %copy-start.16 = (bf16[1,2048,768]{2,1,0:T(8,128)(2,1)S(1)}, bf16[1,2048,768]{2,1,0:T(8,128)(2,1)}, u32[]{:S(2)}) copy-start(bf16[1,2048,768]{2,1,0:T(8,128)(2,1)} %param.14) | copy-start | bytes 9437188
  148.4 3.2 copy-start.19
  148.4 3.2 copy-start.21
  152.3 3.5 copy-start.17
  152.3 5.6 %copy-start.12 = (bf16[1,384,2048]{2,1,0:T(8,128)(2,1)S(1)}, bf16[1,384,2048]{2,1,0:T(8,128)(2,1)}, u32[]{:S(2)}) copy-start(bf16[1,384,2048]{2,1,0:T(8,128)(2,1)} %param.15) | copy-start | bytes 4718596
  155.8 2.1 copy-start.2
  162.3 5.0 %copy-start.1 = (f32[2304,384]{0,1:T(8,128)S(1)}, f32[2304,384]{0,1:T(8,128)}, u32[]{:S(2)}) copy-start(f32[2304,384]{0,1:T(8,128)} %get-tuple-element.16) | copy-start | bytes 10616836
  162.3 5.5 %copy-start.3 = (f32[2304,384]{0,1:T(8,128)S(1)}, f32[2304,384]{0,1:T(8,128)}, u32[]{:S(2)}) copy-start(f32[2304,384]{0,1:T(8,128)} %fusion.27) | copy-start | bytes 10616836
  162.3 5.9 %copy-start.13 = (bf16[1,384,2048]{2,1,0:T(8,128)(2,1)S(1)}, bf16[1,384,2048]{2,1,0:T(8,128)(2,1)}, u32[]{:S(2)}) copy-start(bf16[1,384,2048]{2,1,0:T(8,128)(2,1)} %param.15) | copy-start | bytes 4718596
  167.3 3.4 copy-start
  170.6 11.2 %copy-start.5 = (bf16[2304,384]{0,1:T(8,128)(2,1)}, bf16[2304,384]{0,1:T(8,128)(2,1)S(1)}, u32[]{:S(2)}) copy-start(bf16[2304,384]{0,1:T(8,128)(2,1)S(1)} %get-tuple-element.32) | copy-start | bytes 5308420
  170.7 11.2 %copy-start.7 = (bf16[2304,384]{0,1:T(8,128)(2,1)}, bf16[2304,384]{0,1:T(8,128)(2,1)S(1)}, u32[]{:S(2)}) copy-start(bf16[2304,384]{0,1:T(8,128)(2,1)S(1)} %get-tuple-element.33) | copy-start | bytes 5308420
  170.7 11.2 %copy-start.20 = (pred[32,128]{1,0:T(8,128)(4,1)S(1)}, pred[32,128]{1,0:T(8,128)(4,1)}, u32[]{:S(2)}) copy-start(pred[32,128]{1,0:T(8,128)(4,1)} %copy-done.18) | copy-start | bytes 12292
  190.1 6.9 %copy-start.8 = (bf16[2304,384]{0,1:T(8,128)(2,1)S(1)}, bf16[2304,384]{0,1:T(8,128)(2,1)}, u32[]{:S(2)}) copy-start(bf16[2304,384]{0,1:T(8,128)(2,1)} %get-tuple-element.18) | copy-start | bytes 5308420
  209.2 4.9 %copy-start.14 = (bf16[384,2,512]{2,0,1:T(8,128)(2,1)S(1)}, bf16[384,2,512]{2,0,1:T(8,128)(2,1)}, u32[]{:S(2)}) copy-start(bf16[384,2,512]{2,0,1:T(8,128)(2,1)} %fusion.14) | copy-start | bytes 2359300
  214.1 6.1 %copy-start.6 = (bf16[2304,384]{0,1:T(8,128)(2,1)S(1)}, bf16[2304,384]{0,1:T(8,128)(2,1)}, u32[]{:S(2)}) copy-start(bf16[2304,384]{0,1:T(8,128)(2,1)} %copy-done.5) | copy-start | bytes 5308420
  215.4 24.5 %all-to-all-start = ((bf16[384,4,512]{2,0,1:T(8,128)(2,1)}), bf16[384,4,512]{2,0,1:T(8,128)(2,1)S(1)}, u32[]{:S(2)}, u32[]{:S(2)}) async-start(bf16[384,4,512]{2,0,1:T(8,128)(2,1)} %pad_maximum_fusion.3), calls=%async_computation.1 | async-start | bytes 3145728 | tf_op jit(solution)/shard_map/all_to_all | solution.py:151
  239.9 1.1 copy-start.4
  241.1 40.8 %all-to-all-start.1 = ((bf16[4,512,768]{2,1,0:T(8,128)(2,1)}), bf16[4,512,768]{2,1,0:T(8,128)(2,1)S(1)}, u32[]{:S(2)}, u32[]{:S(2)}) async-start(bf16[4,512,768]{2,1,0:T(8,128)(2,1)} %bitcast.63), calls=%async_computation.2 | async-start | bytes 6291456 | tf_op jit(solution)/shard_map/all_to_all | solution.py:147
  281.9 1.4 copy-start.9
  281.9 1.9 copy-start.10
  289.5 49.9 %all-to-all-start.2 = ((bf16[4,512,768]{2,1,0:T(8,128)(2,1)}), bf16[4,512,768]{2,1,0:T(8,128)(2,1)S(1)}, u32[]{:S(2)}, u32[]{:S(2)}) async-start(bf16[4,512,768]{2,1,0:T(8,128)(2,1)} %broadcast_in_dim.40), calls=%async_computation.3 | async-start | bytes 6291456 | tf_op jit(solution)/shard_map/all_to_all | solution.py:165
  294.6 48.1 %all-gather.6.cloned.1.call-start = ((), (), s32[]{:S(2)}) async-start(), calls=%async_computation.5 | async-start | bytes 1966080 | tf_op jit(solution)/shard_map/all_gather | solution.py:168
  342.7 2.5 copy-start.11
Sparse Core Ops, SparseCore 0:
  11.9 94.9 all-gather.7
  109.8 52.5 all-gather.9
  190.3 114.4 reduce-scatter.1
  308.3 34.3 all-gather.5

commit v12 on v11

--- a/solution.py
+++ b/solution.py
@@ -29,9 +29,8 @@
     pair_grad = jnp.concatenate(
         [hidden_grad * up_slope, hidden_grad * activated], axis=1
     ).astype(jnp.bfloat16)
-    down_grad = jnp.concatenate(
-        [jnp.dot(hidden_act.T, part, preferred_element_type=jnp.float32) for part in scaled_parts],
-        axis=1,
+    down_grad = jnp.dot(
+        hidden_act.T, jnp.concatenate(scaled_parts, axis=1), preferred_element_type=jnp.float32
     )
     gate_up_grad = jnp.dot(inputs.T, pair_grad, preferred_element_type=jnp.float32)
     input_grad = jnp.dot(pair_grad, weight_gate_up.T, preferred_element_type=jnp.float32).astype(

time: 358 us -> 348 us (0.972)
  local copies, waits for them, and re-layouts: 36.8 us -> 25.9 us
  waiting for transfers between devices: 181 us -> 187 us
    all_to_all x1, waiting for transfers between devices: 31.2 us -> 6.3 us  [local(): lax.all_to_all(jnp.broadcast_to(new_pair, (groups, share_rows, pair_width...]
    all_gather x1, waiting for transfers between devices: 3.36 us -> 20.2 us  [local(): full_down = lax.all_gather(new_down, 'group', axis=2, tiled=True)]
    reduce_scatter x1, waiting for transfers between devices: 10.2 us -> 25.1 us  [local(): lax.psum_scatter(dense.reshape(expert_count * local_tokens, model_width),...]
    dot_general x2 -> x0, local copies, waits for them, and re-layouts: 13.8 us -> none  [expert_backward(): jnp.dot(hidden_act.T, part, preferred_element_type=jnp.float32)]
    dot_general x2 -> x1, matrix products: 10.1 us -> 7.59 us  [expert_backward(): jnp.dot(hidden_act.T, jnp.concatenate(scaled_parts, axis=1), preferred_el...]
    unnamed x47 -> x45, local copies, waits for them, and re-layouts: 9.97 us -> 11.6 us
  transfers between devices with their start and end apart: 7 -> 7, of which waited for: 7 -> 7; matrix products, arithmetic and copies ran while one was open for 29% -> 25% of each run, Pallas kernels for 0% -> 0%
where the time goes in v12:
time: 348 us; the launch traced here: 345 us
  waiting for transfers between devices  187 us (54%)
  matrix products  76.2 us (22%)
  other arithmetic  26.2 us (8%)
  local copies, waits for them, and re-layouts  25.9 us (7%)
  starting transfers between devices  15.3 us (4%)
  between operations  14 us (4%)
    all_gather x1, waiting for transfers between devices, local(): lax.all_gather(jnp.concatenate([tokens, cotangent[:, :half_width], meta],...  95.1 us
    all_to_all x1, waiting for transfers between devices, local(): lax.all_to_all(grad_pair.astype(jnp.bfloat16).reshape(groups, share_rows,...  33 us
    reduce_scatter x1, waiting for transfers between devices, local(): lax.psum_scatter(dense.reshape(expert_count * local_tokens, model_width),...  25.1 us
    all_gather x1, waiting for transfers between devices, local(): full_down = lax.all_gather(new_down, 'group', axis=2, tiled=True)  20.2 us
    dot_general x1, matrix products, local(): jnp.einsum('srt,stc->src', pick_b, first, preferred_element_type=jnp.floa...  15.5 us
    dot_general x1, matrix products, expert_backward(): jnp.dot(inputs.T, pair_grad, preferred_element_type=jnp.float32)  12.5 us
    unnamed x45, local copies, waits for them, and re-layouts  11.6 us
    dot_general x1, matrix products, expert_backward(): jnp.dot(pair_grad, weight_gate_up.T, preferred_element_type=jnp.float32)  11.2 us
  transfers between devices with their start and end apart: 7, of which 7 were waited for; matrix products, arithmetic and copies ran while one was open for 25% of the time, Pallas kernels for 0%

profile of v12, /device:TPU:50, one launch (start us, length us, event | category | flops | bytes accessed | tf_op | source)
XLA Modules:
  0.0 345.0 jit_solution(9185191989546034513)
XLA Ops:
  7.2 0.0 copy-start.14
  7.2 0.0 all-gather.8.cloned.1.call-start
  7.2 0.7 reduce-precision_convert_fusion.1
  8.0 0.7 convert_convert_fusion.2
  8.7 0.1 copy.25
  8.8 1.0 slice.39
  9.8 2.0 fusion.21
  11.8 0.0 all-gather.8.cloned.1.call-update
  11.8 0.0 all-gather.10.cloned.1.call-start
  11.8 95.1 %all-gather.8.cloned.1.call-done = bf16[4096,3200]{1,0:T(8,128)(2,1)} async-done(((bf16[128,3200]{1,0:T(8,128)(2,1)}), bf16[4096,3200]{1,0:T(8,128)(2,1)}) %all-gather.8.cloned.1.call-update) | async-done | bytes 26214416 | tf_op jit(solution)/shard_map/all_gather | solution.py:86
  106.9 0.7 slice.47
  107.7 0.0 all-gather.10.cloned.1.call-update
  107.7 0.0 reduce-scatter.2.cloned.1.call-start
  107.7 1.5 slice_convert_fusion.1
  109.2 3.0 fusion.12
  112.2 0.6 reduce_or.9
  112.8 0.0 copy-start.17
  112.8 0.1 fusion.33
  113.0 0.5 copy-done.17
  113.4 15.5 %convolution_convert_fusion.1 = bf16[32,72,3200]{2,1,0:T(8,128)(2,1)} fusion(bf16[32,128,3200]{2,1,0:T(8,128)(2,1)} %bitcast.41, f32[32,128]{1,0:T(8,128)S(1)} %fusion.33, pred[32,128]{1,0:T(8,128)(4,1)S(1)} %convert_compare_fusion), kind=kOutput, calls=%fused_computation.1 | convolution fusion | flops 1895399424 | bytes 40980480 | tf_op jit(solution)/shard_map/srt,stc->src/dot_general | solution.py:106
  128.9 9.5 %slice.59 = bf16[32,72,2048]{2,1,0:T(8,128)(2,1)} slice(bf16[32,72,3200]{2,1,0:T(8,128)(2,1)} %convolution_convert_fusion.1), slice={[0:32], [0:72], [0:2048]} | slice | bytes 18874368 | tf_op jit(solution)/shard_map/slice | solution.py:109
  138.4 10.0 %fusion.6 = f32[2304,768]{0,1:T(8,128)S(1)} fusion(bf16[2304,2048]{1,0:T(8,128)(2,1)} %bitcast.44, bf16[1,2048,768]{2,1,0:T(8,128)(2,1)S(1)} %copy-done.15), kind=kOutput, calls=%fused_computation.20 | convolution fusion | flops 7247757312 | bytes 19660800 | tf_op jit(solution)/shard_map/dot_general | solution.py:15
  148.4 0.0 copy-start.18
  148.4 0.0 copy-start.20
  148.4 3.2 fusion.4
  151.6 0.6 select_reduce_fusion
  152.3 0.0 copy-start.16
  152.3 0.0 copy-start.12
  152.3 3.5 %multiply_convert_fusion.1 = bf16[32,72,1024]{2,1,0:T(8,128)(2,1)S(1)} fusion(bf16[32,72,3200]{2,1,0:T(8,128)(2,1)} %convolution_convert_fusion.1, f32[32,72]{1,0:T(8,128)S(1)} %select_reduce_fusion), kind=kLoop, calls=%fused_computation.8 | loop fusion | flops 7077888 | bytes 9446400 | tf_op jit(solution)/shard_map/convert_element_type | solution.py:116
  155.8 2.2 copy-done.7
  158.0 3.8 %fusion.24 = f32[2304,384]{0,1:T(8,128)} fusion(bf16[2304,1024]{1,0:T(8,128)(2,1)S(1)} %bitcast.47, bf16[384,2048]{1,0:T(8,128)(2,1)S(1)} %bitcast.52), kind=kOutput, calls=%fused_computation.46 | convolution fusion | flops 1811939328 | bytes 9043968 | tf_op jit(solution)/shard_map/dot_general | solution.py:22
  161.8 0.5 all-gather.10.cloned.1.call-done
  162.3 4.9 %multiply_convert_fusion = bf16[32,72,1024]{2,1,0:T(8,128)(2,1)S(1)} fusion(f32[32,72]{1,0:T(8,128)} %copy-done.16, bf16[32,128,1024]{2,1,0:T(8,128)(2,1)} %bitcast.46, f32[32,128]{1,0:T(8,128)S(1)} %fusion.33, pred[32,128]{1,0:T(8,128)(4,1)} %copy-done.17), kind=kOutput, calls=%fused_computation.7 | convolution fusion | flops 614006784 | bytes 13136896 | tf_op jit(solution)/shard_map/srt,stc->src/dot_general | solution.py:111
  167.3 0.5 copy-done.2
  167.8 0.4 copy-done.13
  168.2 2.4 multiply_convert_fusion.3
  170.7 0.0 copy-start.19
  170.7 11.2 %convolution_convert_fusion.2 = bf16[2304,2048]{1,0:T(8,128)(2,1)S(1)} fusion(bf16[1,2048,768]{2,1,0:T(8,128)(2,1)} %param.14, bf16[2304,384]{0,1:T(8,128)(2,1)S(1)} %get-tuple-element.33, bf16[2304,384]{0,1:T(8,128)(2,1)S(1)} %get-tuple-element.32), kind=kOutput, calls=%fused_computation.2 | convolution fusion | flops 7259553792 | bytes 16121856 | tf_op jit(solution)/shard_map/dot_general | solution.py:36
  181.9 8.2 %convolution_convert_fusion = bf16[32,128,2048]{2,1,0:T(8,128)(2,1)} fusion(bf16[32,72,2048]{2,1,0:T(8,128)(2,1)S(1)} %bitcast.42, f32[32,128]{1,0:T(8,128)S(1)} %fusion.33, pred[32,128]{1,0:T(8,128)(4,1)S(1)} %copy-done.19), kind=kOutput, calls=%fused_computation | convolution fusion | flops 1216937984 | bytes 26234880 | tf_op jit(solution)/shard_map/srt,src->stc/dot_general | solution.py:129
  190.1 0.0 reduce-scatter.2.cloned.1.call-update
  190.1 1.4 copy-done.8
  191.6 7.6 %fusion.8 = bf16[384,2048]{1,0:T(8,128)(2,1)S(1)} fusion(bf16[2304,384]{0,1:T(8,128)(2,1)S(1)} %copy-done.8, bf16[2304,1024]{1,0:T(8,128)(2,1)} %bitcast.39, bf16[2304,1024]{1,0:T(8,128)(2,1)} %bitcast.48), kind=kOutput, calls=%fused_computation.23 | convolution fusion | flops 3643539456 | bytes 12779520 | tf_op jit(solution)/shard_map/dot_general | solution.py:32
  199.2 1.3 copy.28
  200.5 4.8 %all-to-all-start = ((bf16[384,4,512]{2,0,1:T(8,128)(2,1)}), bf16[384,4,512]{2,0,1:T(8,128)(2,1)S(1)}, u32[]{:S(2)}, u32[]{:S(2)}) async-start(bf16[384,4,512]{2,0,1:T(8,128)(2,1)} %bitcast.36), calls=%async_computation.1 | async-start | bytes 3145728 | tf_op jit(solution)/shard_map/all_to_all | solution.py:150
  205.3 12.5 %convolution_convert_fusion.3 = bf16[2048,768]{1,0:T(8,128)(2,1)} fusion(bf16[2304,2048]{1,0:T(8,128)(2,1)} %bitcast.45, bf16[2304,384]{0,1:T(8,128)(2,1)} %copy-done.6, bf16[2304,384]{0,1:T(8,128)(2,1)S(1)} %copy-done.5), kind=kOutput, calls=%fused_computation.18 | convolution fusion | flops 7256408064 | bytes 16121856 | tf_op jit(solution)/shard_map/dot_general | solution.py:35
  217.7 7.2 %all-to-all-done = bf16[384,4,512]{2,0,1:T(8,128)(2,1)S(1)} async-done(((bf16[384,4,512]{2,0,1:T(8,128)(2,1)}), bf16[384,4,512]{2,0,1:T(8,128)(2,1)S(1)}, u32[]{:S(2)}, u32[]{:S(2)}) %all-to-all-start) | async-done | bytes 1572896 | tf_op jit(solution)/shard_map/all_to_all | solution.py:150
  225.0 1.1 copy-done.3
  226.1 5.2 %all-to-all-start.1 = ((bf16[4,512,768]{2,1,0:T(8,128)(2,1)}), bf16[4,512,768]{2,1,0:T(8,128)(2,1)S(1)}, u32[]{:S(2)}, u32[]{:S(2)}) async-start(bf16[4,512,768]{2,1,0:T(8,128)(2,1)} %bitcast.49), calls=%async_computation.2 | async-start | bytes 6291456 | tf_op jit(solution)/shard_map/all_to_all | solution.py:146
  231.3 2.7 convert_reduce_fusion.1
  234.1 33.0 %all-to-all-done.1 = bf16[4,512,768]{2,1,0:T(8,128)(2,1)S(1)} async-done(((bf16[4,512,768]{2,1,0:T(8,128)(2,1)}), bf16[4,512,768]{2,1,0:T(8,128)(2,1)S(1)}, u32[]{:S(2)}, u32[]{:S(2)}) %all-to-all-start.1) | async-done | bytes 3145760 | tf_op jit(solution)/shard_map/all_to_all | solution.py:146
  267.0 0.4 convert_reduce_fusion
  267.5 1.0 copy-done.9
  268.4 0.5 copy-done.10
  269.0 3.9 %fusion.26 = (bf16[512,768]{1,0:T(8,128)(2,1)S(1)}, f32[1,512,768]{2,1,0:T(8,128)}, f32[1,512,768]{2,1,0:T(8,128)}) fusion(bf16[1,2048,768]{2,1,0:T(8,128)(2,1)} %param.14, s32[]{:T(128)S(6)} %select_n.14, f32[512,768]{1,0:T(8,128)S(1)} %convert_reduce_fusion, f32[1,512,768]{2,1,0:T(8,128)S(1)} %copy-done.9, f32[1,512,768]{2,1,0:T(8,128)S(1)} %copy-done.10), kind=kLoop, calls=%fused_computation.50 | loop fusion | flops 5111808 | bytes 9437188 | tf_op jit(solution)/shard_map/broadcast_in_dim | solution.py:165
  272.8 1.9 broadcast_in_dim.40
  274.7 5.1 %all-to-all-start.2 = ((bf16[4,512,768]{2,1,0:T(8,128)(2,1)}), bf16[4,512,768]{2,1,0:T(8,128)(2,1)S(1)}, u32[]{:S(2)}, u32[]{:S(2)}) async-start(bf16[4,512,768]{2,1,0:T(8,128)(2,1)} %broadcast_in_dim.40), calls=%async_computation.3 | async-start | bytes 6291456 | tf_op jit(solution)/shard_map/all_to_all | solution.py:164
  279.8 25.1 %reduce-scatter.2.cloned.1.call-done = bf16[128,2048]{1,0:T(8,128)(2,1)} async-done(((bf16[4096,2048]{1,0:T(8,128)(2,1)}), bf16[128,2048]{1,0:T(8,128)(2,1)}) %reduce-scatter.2.cloned.1.call-update) | async-done | bytes 524304 | tf_op jit(solution)/shard_map/reduce_scatter | solution.py:135
  304.9 3.3 subtract_convert_fusion.1
  308.2 0.0 all-gather.6.cloned.1.call-update
  308.3 6.3 %all-to-all-done.2 = bf16[4,512,768]{2,1,0:T(8,128)(2,1)S(1)} async-done(((bf16[4,512,768]{2,1,0:T(8,128)(2,1)}), bf16[4,512,768]{2,1,0:T(8,128)(2,1)S(1)}, u32[]{:S(2)}, u32[]{:S(2)}) %all-to-all-start.2) | async-done | bytes 3145760 | tf_op jit(solution)/shard_map/all_to_all | solution.py:164
  314.6 20.2 %all-gather.6.cloned.1.call-done = bf16[1,384,2048]{2,1,0:T(8,128)(2,1)} async-done(((bf16[1,384,512]{2,1,0:T(8,128)(2,1)}), bf16[1,384,2048]{2,1,0:T(8,128)(2,1)}) %all-gather.6.cloned.1.call-update) | async-done | bytes 1572880 | tf_op jit(solution)/shard_map/all_gather | solution.py:167
  334.8 1.7 copy.31
  336.5 0.9 copy-done.11
  337.4 1.1 copy.32
  (29 shorter events, 0.1 us)
Async XLA Ops:
  7.2 99.8 %copy-start.14 = (bf16[128,2048]{1,0:T(8,128)(2,1)S(1)}, bf16[128,2048]{1,0:T(8,128)(2,1)}, u32[]{:S(2)}) copy-start(bf16[128,2048]{1,0:T(8,128)(2,1)} %param.11) | copy-start | bytes 1572868
  7.2 99.8 %all-gather.8.cloned.1.call-start = ((), (), s32[]{:S(2)}) async-start(), calls=%async_computation.6 | async-start | bytes 27033600 | tf_op jit(solution)/shard_map/all_gather | solution.py:86
  11.8 150.5 %all-gather.10.cloned.1.call-start = ((), (), s32[]{:S(2)}) async-start(), calls=%async_computation.7 | async-start | bytes 8650752 | tf_op jit(solution)/shard_map/all_gather | solution.py:90
  107.7 197.2 %reduce-scatter.2.cloned.1.call-start = ((), (), s32[]{:S(2)}) async-start(), calls=%async_computation.4 | async-start | bytes 17301504 | tf_op jit(solution)/shard_map/reduce_scatter | solution.py:135
  112.8 0.6 copy-start.17
  128.9 9.5 %copy-start.15 = (bf16[1,2048,768]{2,1,0:T(8,128)(2,1)S(1)}, bf16[1,2048,768]{2,1,0:T(8,128)(2,1)}, u32[]{:S(2)}) copy-start(bf16[1,2048,768]{2,1,0:T(8,128)(2,1)} %param.14) | copy-start | bytes 9437188
  148.4 3.2 copy-start.18
  148.4 3.2 copy-start.20
  152.3 3.5 %copy-start.16 = (f32[32,72]{1,0:T(8,128)}, f32[32,72]{1,0:T(8,128)S(1)}, u32[]{:S(2)}) copy-start(f32[32,72]{1,0:T(8,128)S(1)} %select_reduce_fusion) | copy-start | bytes 27652
  152.3 5.7 %copy-start.12 = (bf16[1,384,2048]{2,1,0:T(8,128)(2,1)S(1)}, bf16[1,384,2048]{2,1,0:T(8,128)(2,1)}, u32[]{:S(2)}) copy-start(bf16[1,384,2048]{2,1,0:T(8,128)(2,1)} %param.15) | copy-start | bytes 4718596
  155.8 2.2 copy-start.7
  162.3 5.0 %copy-start.1 = (f32[2304,384]{0,1:T(8,128)S(1)}, f32[2304,384]{0,1:T(8,128)}, u32[]{:S(2)}) copy-start(f32[2304,384]{0,1:T(8,128)} %get-tuple-element.16) | copy-start | bytes 10616836
  162.3 5.5 %copy-start.2 = (f32[2304,384]{0,1:T(8,128)S(1)}, f32[2304,384]{0,1:T(8,128)}, u32[]{:S(2)}) copy-start(f32[2304,384]{0,1:T(8,128)} %fusion.24) | copy-start | bytes 10616836
  162.3 5.9 %copy-start.13 = (bf16[1,384,2048]{2,1,0:T(8,128)(2,1)S(1)}, bf16[1,384,2048]{2,1,0:T(8,128)(2,1)}, u32[]{:S(2)}) copy-start(bf16[1,384,2048]{2,1,0:T(8,128)(2,1)} %param.15) | copy-start | bytes 4718596
  167.3 3.4 copy-start
  170.6 11.2 %copy-start.4 = (bf16[2304,384]{0,1:T(8,128)(2,1)}, bf16[2304,384]{0,1:T(8,128)(2,1)S(1)}, u32[]{:S(2)}) copy-start(bf16[2304,384]{0,1:T(8,128)(2,1)S(1)} %get-tuple-element.32) | copy-start | bytes 5308420
  170.7 11.2 %copy-start.6 = (bf16[2304,384]{0,1:T(8,128)(2,1)}, bf16[2304,384]{0,1:T(8,128)(2,1)S(1)}, u32[]{:S(2)}) copy-start(bf16[2304,384]{0,1:T(8,128)(2,1)S(1)} %get-tuple-element.33) | copy-start | bytes 5308420
  170.7 11.2 %copy-start.19 = (pred[32,128]{1,0:T(8,128)(4,1)S(1)}, pred[32,128]{1,0:T(8,128)(4,1)}, u32[]{:S(2)}) copy-start(pred[32,128]{1,0:T(8,128)(4,1)} %copy-done.17) | copy-start | bytes 12292
  190.1 1.5 copy-start.8
  199.2 6.1 %copy-start.5 = (bf16[2304,384]{0,1:T(8,128)(2,1)S(1)}, bf16[2304,384]{0,1:T(8,128)(2,1)}, u32[]{:S(2)}) copy-start(bf16[2304,384]{0,1:T(8,128)(2,1)} %copy-done.4) | copy-start | bytes 5308420
  200.5 24.5 %all-to-all-start = ((bf16[384,4,512]{2,0,1:T(8,128)(2,1)}), bf16[384,4,512]{2,0,1:T(8,128)(2,1)S(1)}, u32[]{:S(2)}, u32[]{:S(2)}) async-start(bf16[384,4,512]{2,0,1:T(8,128)(2,1)} %bitcast.36), calls=%async_computation.1 | async-start | bytes 3145728 | tf_op jit(solution)/shard_map/all_to_all | solution.py:150
  225.0 1.1 copy-start.3
  226.1 40.9 %all-to-all-start.1 = ((bf16[4,512,768]{2,1,0:T(8,128)(2,1)}), bf16[4,512,768]{2,1,0:T(8,128)(2,1)S(1)}, u32[]{:S(2)}, u32[]{:S(2)}) async-start(bf16[4,512,768]{2,1,0:T(8,128)(2,1)} %bitcast.49), calls=%async_computation.2 | async-start | bytes 6291456 | tf_op jit(solution)/shard_map/all_to_all | solution.py:146
  267.0 1.4 copy-start.9
  267.0 1.9 copy-start.10
  274.7 39.9 %all-to-all-start.2 = ((bf16[4,512,768]{2,1,0:T(8,128)(2,1)}), bf16[4,512,768]{2,1,0:T(8,128)(2,1)S(1)}, u32[]{:S(2)}, u32[]{:S(2)}) async-start(bf16[4,512,768]{2,1,0:T(8,128)(2,1)} %broadcast_in_dim.40), calls=%async_computation.3 | async-start | bytes 6291456 | tf_op jit(solution)/shard_map/all_to_all | solution.py:164
  279.8 55.0 %all-gather.6.cloned.1.call-start = ((), (), s32[]{:S(2)}) async-start(), calls=%async_computation.5 | async-start | bytes 1966080 | tf_op jit(solution)/shard_map/all_gather | solution.py:167
  334.8 2.5 copy-start.11
Sparse Core Ops, SparseCore 0:
  11.9 94.9 all-gather.7
  109.8 52.5 all-gather.9
  190.3 114.6 reduce-scatter.1
  308.4 26.3 all-gather.5

commit v13 on v12

--- a/solution.py
+++ b/solution.py
@@ -164,7 +164,13 @@
     full_pair = lax.all_to_all(
         jnp.broadcast_to(new_pair, (groups, share_rows, pair_width)), "group", 0, 0, tiled=True
     ).reshape(1, model_width, pair_width)
-    full_down = lax.all_gather(new_down, "group", axis=2, tiled=True)
+    by_shift = [new_down[0]]
+    for shift in range(1, groups):
+        pairs = [(i, (i + shift) % groups) for i in range(groups)]
+        by_shift.append(lax.ppermute(new_down[0], "group", pairs))
+    ahead = jnp.stack([by_shift[(-k) % groups] for k in range(groups)])
+    by_member = jnp.roll(ahead, group_index, axis=0)
+    full_down = by_member.transpose(1, 0, 2).reshape(1, hidden_count, model_width)
     return (token_grad, full_pair, full_down, first_pair, second_pair, first_down, second_down)
 
 

time: 348 us -> 357 us (1.026)
  local copies, waits for them, and re-layouts: 25.9 us -> 39.6 us
  waiting for transfers between devices: 187 us -> 176 us
  starting transfers between devices: 15.3 us -> 20 us
    all_gather x1 -> x0, waiting for transfers between devices: 20.2 us -> none  [local(): full_down = lax.all_gather(new_down, 'group', axis=2, tiled=True)]
    ppermute x0 -> x3, waiting for transfers between devices: none -> 14.3 us  [local(): by_shift.append(lax.ppermute(new_down[0], 'group', pairs))]
    unnamed x45 -> x47, local copies, waits for them, and re-layouts: 11.6 us -> 19.2 us
    all_to_all x1, waiting for transfers between devices: 33 us -> 26.1 us  [local(): lax.all_to_all(grad_pair.astype(jnp.bfloat16).reshape(groups, share_rows,...]
    all_to_all x1, waiting for transfers between devices: 7.22 us -> 13.1 us  [local(): lax.all_to_all(grad_down.astype(jnp.bfloat16).reshape(hidden_count, group...]
    all_to_all x1, waiting for transfers between devices: 6.3 us -> 0.58 us  [local(): lax.all_to_all(jnp.broadcast_to(new_pair, (groups, share_rows, pair_width...]
    transpose x0 -> x2, local copies, waits for them, and re-layouts: none -> 5.23 us  [local(): by_member.transpose(1, 0, 2).reshape(1, hidden_count, model_width)]
    ppermute x0 -> x3, starting transfers between devices: none -> 4.15 us  [local(): by_shift.append(lax.ppermute(new_down[0], 'group', pairs))]
  transfers between devices with their start and end apart: 7 -> 9, of which waited for: 7 -> 8; matrix products, arithmetic and copies ran while one was open for 25% -> 25% of each run, Pallas kernels for 0% -> 0%
where the time goes in v13:
time: 357 us; the launch traced here: 352 us
  waiting for transfers between devices  176 us (49%)
  matrix products  76.5 us (21%)
  local copies, waits for them, and re-layouts  39.6 us (11%)
  other arithmetic  26.1 us (7%)
  starting transfers between devices  20 us (6%)
  between operations  14 us (4%)
    all_gather x1, waiting for transfers between devices, local(): lax.all_gather(jnp.concatenate([tokens, cotangent[:, :half_width], meta],...  95.1 us
    all_to_all x1, waiting for transfers between devices, local(): lax.all_to_all(grad_pair.astype(jnp.bfloat16).reshape(groups, share_rows,...  26.1 us
    reduce_scatter x1, waiting for transfers between devices, local(): lax.psum_scatter(dense.reshape(expert_count * local_tokens, model_width),...  25.9 us
    unnamed x47, local copies, waits for them, and re-layouts  19.2 us
    dot_general x1, matrix products, local(): jnp.einsum('srt,stc->src', pick_b, first, preferred_element_type=jnp.floa...  15.5 us
    ppermute x3, waiting for transfers between devices, local(): by_shift.append(lax.ppermute(new_down[0], 'group', pairs))  14.3 us
    all_to_all x1, waiting for transfers between devices, local(): lax.all_to_all(grad_down.astype(jnp.bfloat16).reshape(hidden_count, group...  13.1 us
    dot_general x1, matrix products, expert_backward(): jnp.dot(inputs.T, pair_grad, preferred_element_type=jnp.float32)  11.2 us
  transfers between devices with their start and end apart: 9, of which 8 were waited for; matrix products, arithmetic and copies ran while one was open for 25% of the time, Pallas kernels for 0%

profile of v13, /device:TPU:50, one launch (start us, length us, event | category | flops | bytes accessed | tf_op | source)
XLA Modules:
  0.0 351.9 jit_solution(17879531022807213033)
XLA Ops:
  7.2 0.7 reduce-precision_convert_fusion.1
  8.0 0.7 convert_convert_fusion.2
  8.7 0.1 copy.38
  8.8 1.0 slice.39
  9.8 2.0 fusion.21
  11.8 0.0 all-gather.7.cloned.1.call-start
  11.8 95.1 %all-gather.5.cloned.1.call-done = bf16[4096,3200]{1,0:T(8,128)(2,1)} async-done(((bf16[128,3200]{1,0:T(8,128)(2,1)}), bf16[4096,3200]{1,0:T(8,128)(2,1)}) %all-gather.5.cloned.1.call-update) | async-done | bytes 26214416 | tf_op jit(solution)/shard_map/all_gather | solution.py:86
  106.9 0.7 slice.47
  107.7 0.0 reduce-scatter.2.cloned.1.call-start
  107.7 1.5 slice_convert_fusion.1
  109.2 3.0 fusion.12
  112.2 0.6 reduce_or.9
  112.8 0.1 fusion.33
  113.0 0.5 copy-done.15
  113.4 15.5 %convolution_convert_fusion.1 = bf16[32,72,3200]{2,1,0:T(8,128)(2,1)} fusion(bf16[32,128,3200]{2,1,0:T(8,128)(2,1)} %bitcast.54, f32[32,128]{1,0:T(8,128)S(1)} %fusion.33, pred[32,128]{1,0:T(8,128)(4,1)S(1)} %convert_compare_fusion), kind=kOutput, calls=%fused_computation.1 | convolution fusion | flops 1895399424 | bytes 40980480 | tf_op jit(solution)/shard_map/srt,stc->src/dot_general | solution.py:106
  128.9 9.5 %slice.59 = bf16[32,72,2048]{2,1,0:T(8,128)(2,1)} slice(bf16[32,72,3200]{2,1,0:T(8,128)(2,1)} %convolution_convert_fusion.1), slice={[0:32], [0:72], [0:2048]} | slice | bytes 18874368 | tf_op jit(solution)/shard_map/slice | solution.py:109
  138.4 10.0 %fusion.6 = f32[2304,768]{0,1:T(8,128)S(1)} fusion(bf16[2304,2048]{1,0:T(8,128)(2,1)} %bitcast.57, bf16[1,2048,768]{2,1,0:T(8,128)(2,1)S(1)} %copy-done.13), kind=kOutput, calls=%fused_computation.20 | convolution fusion | flops 7247757312 | bytes 19660800 | tf_op jit(solution)/shard_map/dot_general | solution.py:15
  148.4 3.2 fusion.4
  151.7 0.6 select_reduce_fusion
  152.3 3.5 multiply_convert_fusion.1
  155.8 2.2 copy-done.7
  158.0 3.8 %fusion.24 = f32[2304,384]{0,1:T(8,128)} fusion(bf16[2304,1024]{1,0:T(8,128)(2,1)S(1)} %bitcast.62, bf16[384,2048]{1,0:T(8,128)(2,1)S(1)} %bitcast.67), kind=kOutput, calls=%fused_computation.47 | convolution fusion | flops 1811939328 | bytes 9043968 | tf_op jit(solution)/shard_map/dot_general | solution.py:22
  161.8 0.5 all-gather.7.cloned.1.call-done
  162.3 4.9 %multiply_convert_fusion = bf16[32,72,1024]{2,1,0:T(8,128)(2,1)S(1)} fusion(f32[32,72]{1,0:T(8,128)} %copy-done.14, bf16[32,128,1024]{2,1,0:T(8,128)(2,1)} %bitcast.59, f32[32,128]{1,0:T(8,128)S(1)} %fusion.33, pred[32,128]{1,0:T(8,128)(4,1)} %copy-done.15), kind=kOutput, calls=%fused_computation.7 | convolution fusion | flops 614006784 | bytes 13136896 | tf_op jit(solution)/shard_map/srt,stc->src/dot_general | solution.py:111
  167.3 0.5 copy-done.2
  167.8 0.4 copy-done.11
  168.2 2.4 multiply_convert_fusion.3
  170.7 11.2 %convolution_convert_fusion.2 = bf16[2304,2048]{1,0:T(8,128)(2,1)S(1)} fusion(bf16[1,2048,768]{2,1,0:T(8,128)(2,1)} %param.14, bf16[2304,384]{0,1:T(8,128)(2,1)S(1)} %get-tuple-element.48, bf16[2304,384]{0,1:T(8,128)(2,1)S(1)} %get-tuple-element.47), kind=kOutput, calls=%fused_computation.2 | convolution fusion | flops 7259553792 | bytes 16121856 | tf_op jit(solution)/shard_map/dot_general | solution.py:36
  181.9 8.2 %convolution_convert_fusion = bf16[32,128,2048]{2,1,0:T(8,128)(2,1)} fusion(bf16[32,72,2048]{2,1,0:T(8,128)(2,1)S(1)} %bitcast.55, f32[32,128]{1,0:T(8,128)S(1)} %fusion.33, pred[32,128]{1,0:T(8,128)(4,1)S(1)} %copy-done.17), kind=kOutput, calls=%fused_computation | convolution fusion | flops 1216937984 | bytes 26234880 | tf_op jit(solution)/shard_map/srt,src->stc/dot_general | solution.py:129
  190.1 1.4 copy-done.4
  191.6 0.5 copy-done.6
  192.1 11.2 %convolution_convert_fusion.3 = bf16[2048,768]{1,0:T(8,128)(2,1)} fusion(bf16[2304,2048]{1,0:T(8,128)(2,1)} %bitcast.58, bf16[2304,384]{0,1:T(8,128)(2,1)S(1)} %copy-done.6, bf16[2304,384]{0,1:T(8,128)(2,1)S(1)} %copy-done.4), kind=kOutput, calls=%fused_computation.18 | convolution fusion | flops 7256408064 | bytes 16121856 | tf_op jit(solution)/shard_map/dot_general | solution.py:35
  203.4 4.8 %all-to-all-start.1 = ((bf16[4,512,768]{2,1,0:T(8,128)(2,1)}), bf16[4,512,768]{2,1,0:T(8,128)(2,1)S(1)}, u32[]{:S(2)}, u32[]{:S(2)}) async-start(bf16[4,512,768]{2,1,0:T(8,128)(2,1)} %bitcast.64), calls=%async_computation.2 | async-start | bytes 6291456 | tf_op jit(solution)/shard_map/all_to_all | solution.py:146
  208.2 9.1 %fusion.8 = bf16[384,2048]{1,0:T(8,128)(2,1)S(1)} fusion(bf16[2304,384]{0,1:T(8,128)(2,1)} %get-tuple-element.18, bf16[2304,1024]{1,0:T(8,128)(2,1)} %bitcast.52, bf16[2304,1024]{1,0:T(8,128)(2,1)} %bitcast.63), kind=kOutput, calls=%fused_computation.23 | convolution fusion | flops 3643539456 | bytes 12779520 | tf_op jit(solution)/shard_map/dot_general | solution.py:32
  217.3 1.3 copy.41
  218.6 26.1 %all-to-all-done.1 = bf16[4,512,768]{2,1,0:T(8,128)(2,1)S(1)} async-done(((bf16[4,512,768]{2,1,0:T(8,128)(2,1)}), bf16[4,512,768]{2,1,0:T(8,128)(2,1)S(1)}, u32[]{:S(2)}, u32[]{:S(2)}) %all-to-all-start.1) | async-done | bytes 3145760 | tf_op jit(solution)/shard_map/all_to_all | solution.py:146
  244.7 5.8 %all-to-all-start = ((bf16[384,4,512]{2,0,1:T(8,128)(2,1)}), bf16[384,4,512]{2,0,1:T(8,128)(2,1)}, u32[]{:S(2)}, u32[]{:S(2)}) async-start(bf16[384,4,512]{2,0,1:T(8,128)(2,1)} %bitcast.60), calls=%async_computation.1 | async-start | bytes 3145728 | tf_op jit(solution)/shard_map/all_to_all | solution.py:150
  250.5 0.4 convert_reduce_fusion
  250.9 1.0 copy-done.8
  251.9 0.5 copy-done.9
  252.5 3.9 %fusion.26 = (bf16[512,768]{1,0:T(8,128)(2,1)S(1)}, f32[1,512,768]{2,1,0:T(8,128)}, f32[1,512,768]{2,1,0:T(8,128)}) fusion(bf16[1,2048,768]{2,1,0:T(8,128)(2,1)} %param.14, s32[]{:T(128)S(6)} %select_n.27, f32[512,768]{1,0:T(8,128)S(1)} %convert_reduce_fusion, f32[1,512,768]{2,1,0:T(8,128)S(1)} %copy-done.8, f32[1,512,768]{2,1,0:T(8,128)S(1)} %copy-done.9), kind=kLoop, calls=%fused_computation.51 | loop fusion | flops 5111808 | bytes 9437188 | tf_op jit(solution)/shard_map/broadcast_in_dim | solution.py:165
  256.3 13.1 %all-to-all-done = bf16[384,4,512]{2,0,1:T(8,128)(2,1)} async-done(((bf16[384,4,512]{2,0,1:T(8,128)(2,1)}), bf16[384,4,512]{2,0,1:T(8,128)(2,1)}, u32[]{:S(2)}, u32[]{:S(2)}) %all-to-all-start) | async-done | bytes 1572896 | tf_op jit(solution)/shard_map/all_to_all | solution.py:150
  269.4 1.9 broadcast_in_dim.40
  271.3 5.1 %all-to-all-start.2 = ((bf16[4,512,768]{2,1,0:T(8,128)(2,1)}), bf16[4,512,768]{2,1,0:T(8,128)(2,1)S(1)}, u32[]{:S(2)}, u32[]{:S(2)}) async-start(bf16[4,512,768]{2,1,0:T(8,128)(2,1)} %broadcast_in_dim.40), calls=%async_computation.3 | async-start | bytes 6291456 | tf_op jit(solution)/shard_map/all_to_all | solution.py:164
  276.4 2.6 convert_reduce_fusion.1
  279.0 25.9 %reduce-scatter.2.cloned.1.call-done = bf16[128,2048]{1,0:T(8,128)(2,1)} async-done(((bf16[4096,2048]{1,0:T(8,128)(2,1)}), bf16[128,2048]{1,0:T(8,128)(2,1)}) %reduce-scatter.2.cloned.1.call-update) | async-done | bytes 524304 | tf_op jit(solution)/shard_map/reduce_scatter | solution.py:135
  304.9 3.5 constant_dynamic-update-slice_fusion.1
  308.4 0.6 collective-permute-start
  309.0 2.3 collective-permute-start.1
  311.3 0.6 all-to-all-done.2
  311.9 1.2 collective-permute-start.2
  313.1 8.4 %collective-permute-done = bf16[384,512]{1,0:T(8,128)(2,1)S(1)} collective-permute-done((bf16[384,512]{1,0:T(8,128)(2,1)}, bf16[384,512]{1,0:T(8,128)(2,1)S(1)}, u32[]{:S(2)}, u32[]{:S(2)}) %collective-permute-start) | collective-permute-done | bytes 393248 | tf_op jit(solution)/shard_map/ppermute | solution.py:170
  321.6 0.8 bitcast_dynamic-update-slice_fusion.4
  322.3 5.8 %collective-permute-done.1 = bf16[384,512]{1,0:T(8,128)(2,1)} collective-permute-done((bf16[384,512]{1,0:T(8,128)(2,1)}, bf16[384,512]{1,0:T(8,128)(2,1)}, u32[]{:S(2)}, u32[]{:S(2)}) %collective-permute-start.1) | collective-permute-done | bytes 393248 | tf_op jit(solution)/shard_map/ppermute | solution.py:170
  328.2 1.8 bitcast_dynamic-update-slice_fusion.2
  329.9 0.8 bitcast_dynamic-update-slice_fusion
  330.7 1.8 constant_dynamic-update-slice_fusion
  332.5 0.8 bitcast_dynamic-update-slice_fusion.5
  333.3 1.8 bitcast_dynamic-update-slice_fusion.3
  335.1 0.8 bitcast_dynamic-update-slice_fusion.1
  335.9 2.7 dynamic-slice_bitcast_fusion
  338.5 2.6 copy.34
  341.1 2.6 copy.35
  343.7 1.7 copy.50
  (37 shorter events, 0.2 us)
Async XLA Ops:
  7.2 99.8 %copy-start.12 = (bf16[128,2048]{1,0:T(8,128)(2,1)S(1)}, bf16[128,2048]{1,0:T(8,128)(2,1)}, u32[]{:S(2)}) copy-start(bf16[128,2048]{1,0:T(8,128)(2,1)} %param.11) | copy-start | bytes 1572868
  7.2 99.8 %all-gather.5.cloned.1.call-start = ((), (), s32[]{:S(2)}) async-start(), calls=%async_computation.5 | async-start | bytes 27033600 | tf_op jit(solution)/shard_map/all_gather | solution.py:86
  11.8 150.5 %all-gather.7.cloned.1.call-start = ((), (), s32[]{:S(2)}) async-start(), calls=%async_computation.6 | async-start | bytes 8650752 | tf_op jit(solution)/shard_map/all_gather | solution.py:90
  107.7 197.2 %reduce-scatter.2.cloned.1.call-start = ((), (), s32[]{:S(2)}) async-start(), calls=%async_computation.4 | async-start | bytes 17301504 | tf_op jit(solution)/shard_map/reduce_scatter | solution.py:135
  112.8 0.6 copy-start.15
  128.9 9.5 %copy-start.13 = (bf16[1,2048,768]{2,1,0:T(8,128)(2,1)S(1)}, bf16[1,2048,768]{2,1,0:T(8,128)(2,1)}, u32[]{:S(2)}) copy-start(bf16[1,2048,768]{2,1,0:T(8,128)(2,1)} %param.14) | copy-start | bytes 9437188
  148.4 3.3 copy-start.16
  148.4 3.2 copy-start.18
  152.3 3.5 copy-start.14
  152.3 5.7 %copy-start.10 = (bf16[1,384,2048]{2,1,0:T(8,128)(2,1)S(1)}, bf16[1,384,2048]{2,1,0:T(8,128)(2,1)}, u32[]{:S(2)}) copy-start(bf16[1,384,2048]{2,1,0:T(8,128)(2,1)} %param.15) | copy-start | bytes 4718596
  155.8 2.2 copy-start.7
  162.3 5.0 %copy-start.1 = (f32[2304,384]{0,1:T(8,128)S(1)}, f32[2304,384]{0,1:T(8,128)}, u32[]{:S(2)}) copy-start(f32[2304,384]{0,1:T(8,128)} %get-tuple-element.16) | copy-start | bytes 10616836
  162.3 5.5 %copy-start.2 = (f32[2304,384]{0,1:T(8,128)S(1)}, f32[2304,384]{0,1:T(8,128)}, u32[]{:S(2)}) copy-start(f32[2304,384]{0,1:T(8,128)} %fusion.24) | copy-start | bytes 10616836
  162.3 5.9 %copy-start.11 = (bf16[1,384,2048]{2,1,0:T(8,128)(2,1)S(1)}, bf16[1,384,2048]{2,1,0:T(8,128)(2,1)}, u32[]{:S(2)}) copy-start(bf16[1,384,2048]{2,1,0:T(8,128)(2,1)} %param.15) | copy-start | bytes 4718596
  167.3 3.4 copy-start
  170.6 11.2 %copy-start.3 = (bf16[2304,384]{0,1:T(8,128)(2,1)}, bf16[2304,384]{0,1:T(8,128)(2,1)S(1)}, u32[]{:S(2)}) copy-start(bf16[2304,384]{0,1:T(8,128)(2,1)S(1)} %get-tuple-element.47) | copy-start | bytes 5308420
  170.7 11.2 %copy-start.5 = (bf16[2304,384]{0,1:T(8,128)(2,1)}, bf16[2304,384]{0,1:T(8,128)(2,1)S(1)}, u32[]{:S(2)}) copy-start(bf16[2304,384]{0,1:T(8,128)(2,1)S(1)} %get-tuple-element.48) | copy-start | bytes 5308420
  170.7 11.2 %copy-start.17 = (pred[32,128]{1,0:T(8,128)(4,1)S(1)}, pred[32,128]{1,0:T(8,128)(4,1)}, u32[]{:S(2)}) copy-start(pred[32,128]{1,0:T(8,128)(4,1)} %copy-done.15) | copy-start | bytes 12292
  190.1 1.5 copy-start.4
  190.1 2.0 copy-start.6
  203.4 41.3 %all-to-all-start.1 = ((bf16[4,512,768]{2,1,0:T(8,128)(2,1)}), bf16[4,512,768]{2,1,0:T(8,128)(2,1)S(1)}, u32[]{:S(2)}, u32[]{:S(2)}) async-start(bf16[4,512,768]{2,1,0:T(8,128)(2,1)} %bitcast.64), calls=%async_computation.2 | async-start | bytes 6291456 | tf_op jit(solution)/shard_map/all_to_all | solution.py:146
  244.7 24.7 %all-to-all-start = ((bf16[384,4,512]{2,0,1:T(8,128)(2,1)}), bf16[384,4,512]{2,0,1:T(8,128)(2,1)}, u32[]{:S(2)}, u32[]{:S(2)}) async-start(bf16[384,4,512]{2,0,1:T(8,128)(2,1)} %bitcast.60), calls=%async_computation.1 | async-start | bytes 3145728 | tf_op jit(solution)/shard_map/all_to_all | solution.py:150
  250.5 1.4 copy-start.8
  250.5 2.0 copy-start.9
  271.3 40.6 %all-to-all-start.2 = ((bf16[4,512,768]{2,1,0:T(8,128)(2,1)}), bf16[4,512,768]{2,1,0:T(8,128)(2,1)S(1)}, u32[]{:S(2)}, u32[]{:S(2)}) async-start(bf16[4,512,768]{2,1,0:T(8,128)(2,1)} %broadcast_in_dim.40), calls=%async_computation.3 | async-start | bytes 6291456 | tf_op jit(solution)/shard_map/all_to_all | solution.py:164
  308.4 13.2 %collective-permute-start = (bf16[384,512]{1,0:T(8,128)(2,1)}, bf16[384,512]{1,0:T(8,128)(2,1)S(1)}, u32[]{:S(2)}, u32[]{:S(2)}) collective-permute-start(bf16[384,512]{1,0:T(8,128)(2,1)} %bitcast.14), channel_id=1, source_target_pairs={{0,96},{32,0},{64,32},{96,64},{1,97},{33,1},{65,33},{97,65},{2,98}... | collective-permute-start | bytes 1179656 | tf_op jit(solution)/shard_map/ppermute | solution.py:170
  309.0 19.2 %collective-permute-start.1 = (bf16[384,512]{1,0:T(8,128)(2,1)}, bf16[384,512]{1,0:T(8,128)(2,1)}, u32[]{:S(2)}, u32[]{:S(2)}) collective-permute-start(bf16[384,512]{1,0:T(8,128)(2,1)} %bitcast.14), channel_id=1, source_target_pairs={{0,64},{32,96},{64,0},{96,32},{1,65},{33,97},{65,1},{97,33},{2,66}... | collective-permute-start | bytes 1179656 | tf_op jit(solution)/shard_map/ppermute | solution.py:170
  311.9 18.0 %collective-permute-start.2 = (bf16[384,512]{1,0:T(8,128)(2,1)}, bf16[384,512]{1,0:T(8,128)(2,1)S(1)}, u32[]{:S(2)}, u32[]{:S(2)}) collective-permute-start(bf16[384,512]{1,0:T(8,128)(2,1)} %bitcast.14), channel_id=1, source_target_pairs={{0,32},{32,64},{64,96},{96,0},{1,33},{33,65},{65,97},{97,1},{2,34}... | collective-permute-start | bytes 1179656 | tf_op jit(solution)/shard_map/ppermute | solution.py:170
Sparse Core Ops, SparseCore 0:
  11.9 94.9 all-gather.4
  109.8 52.5 all-gather.6
  190.3 114.6 reduce-scatter.1

commit v14 on v12

--- a/solution.py
+++ b/solution.py
@@ -23,9 +23,7 @@
         for i, part in enumerate(scaled_parts)
     )
     slope = sigmoid_gate * (1.0 + gate_part * (1.0 - sigmoid_gate))
-    hidden_act, up_slope, activated = lax.optimization_barrier(
-        (hidden_act, up_part * slope, activated)
-    )
+    up_slope = up_part * slope
     pair_grad = jnp.concatenate(
         [hidden_grad * up_slope, hidden_grad * activated], axis=1
     ).astype(jnp.bfloat16)

time: 348 us -> 352 us (1.011)
  other arithmetic: 26.2 us -> 22.1 us
  matrix products: 76.2 us -> 79.8 us
    unnamed x45 -> x33, local copies, waits for them, and re-layouts: 11.6 us -> 12.1 us
  transfers between devices with their start and end apart: 7 -> 7, of which waited for: 7 -> 7; matrix products, arithmetic and copies ran while one was open for 25% -> 24% of each run, Pallas kernels for 0% -> 0%
where the time goes in v14:
time: 352 us; the launch traced here: 349 us
  waiting for transfers between devices  190 us (54%)
  matrix products  79.8 us (23%)
  local copies, waits for them, and re-layouts  27.3 us (8%)
  other arithmetic  22.1 us (6%)
  starting transfers between devices  15.3 us (4%)
  between operations  13.9 us (4%)
    all_gather x1, waiting for transfers between devices, local(): lax.all_gather(jnp.concatenate([tokens, cotangent[:, :half_width], meta],...  95.1 us
    all_to_all x1, waiting for transfers between devices, local(): lax.all_to_all(grad_pair.astype(jnp.bfloat16).reshape(groups, share_rows,...  32.9 us
    reduce_scatter x1, waiting for transfers between devices, local(): lax.psum_scatter(dense.reshape(expert_count * local_tokens, model_width),...  24.6 us
    all_gather x1, waiting for transfers between devices, local(): full_down = lax.all_gather(new_down, 'group', axis=2, tiled=True)  19.7 us
    dot_general x1, matrix products, local(): jnp.einsum('srt,stc->src', pick_b, first, preferred_element_type=jnp.floa...  15.5 us
    dot_general x1, matrix products, expert_backward(): jnp.dot(inputs.T, pair_grad, preferred_element_type=jnp.float32)  12.4 us
    unnamed x33, local copies, waits for them, and re-layouts  12.1 us
    dot_general x1, matrix products, expert_backward(): jnp.dot(pair_grad, weight_gate_up.T, preferred_element_type=jnp.float32)  9.9 us
  transfers between devices with their start and end apart: 7, of which 7 were waited for; matrix products, arithmetic and copies ran while one was open for 24% of the time, Pallas kernels for 0%

profile of v14, /device:TPU:50, one launch (start us, length us, event | category | flops | bytes accessed | tf_op | source)
XLA Modules:
  0.0 348.6 jit_solution(8283989378113404226)
XLA Ops:
  7.2 0.0 all-gather.8.cloned.1.call-start
  7.2 0.7 reduce-precision_convert_fusion.1
  7.9 0.7 convert_convert_fusion.2
  8.6 0.1 copy.20
  8.7 1.0 slice.39
  9.7 2.0 fusion.21
  11.7 0.0 all-gather.8.cloned.1.call-update
  11.7 0.0 all-gather.10.cloned.1.call-start
  11.8 95.1 %all-gather.8.cloned.1.call-done = bf16[4096,3200]{1,0:T(8,128)(2,1)} async-done(((bf16[128,3200]{1,0:T(8,128)(2,1)}), bf16[4096,3200]{1,0:T(8,128)(2,1)}) %all-gather.8.cloned.1.call-update) | async-done | bytes 26214416 | tf_op jit(solution)/shard_map/all_gather | solution.py:84
  106.9 1.7 slice.47
  108.6 0.0 all-gather.10.cloned.1.call-update
  108.6 0.0 reduce-scatter.2.cloned.1.call-start
  108.6 1.5 slice_convert_fusion.1
  110.1 2.4 fusion.12
  112.5 0.6 reduce_or.9
  113.1 0.1 fusion.34
  113.2 15.5 %convolution_convert_fusion.1 = bf16[32,72,3200]{2,1,0:T(8,128)(2,1)} fusion(bf16[32,128,3200]{2,1,0:T(8,128)(2,1)} %bitcast.38, f32[32,128]{1,0:T(8,128)S(1)} %fusion.34, pred[32,128]{1,0:T(8,128)(4,1)S(1)} %convert_compare_fusion), kind=kOutput, calls=%fused_computation.1 | convolution fusion | flops 1895399424 | bytes 40980480 | tf_op jit(solution)/shard_map/srt,stc->src/dot_general | solution.py:104
  128.8 9.4 %slice.59 = bf16[32,72,2048]{2,1,0:T(8,128)(2,1)} slice(bf16[32,72,3200]{2,1,0:T(8,128)(2,1)} %convolution_convert_fusion.1), slice={[0:32], [0:72], [0:2048]} | slice | bytes 18874368 | tf_op jit(solution)/shard_map/slice | solution.py:107
  138.2 0.6 select_reduce_fusion
  138.9 0.0 slice-start
  138.9 0.0 slice-start.1
  138.9 3.3 multiply_convert_fusion.1
  142.2 0.0 copy-start.1
  142.2 0.0 copy-done.8
  142.2 0.0 slice-start.2
  142.3 0.0 copy-start.6
  142.3 3.8 %fusion.24 = f32[2304,384]{0,1:T(8,128)} fusion(bf16[2304,1024]{1,0:T(8,128)(2,1)S(1)} %bitcast.46, bf16[384,2048]{1,0:T(8,128)(2,1)S(1)} %bitcast.53), kind=kOutput, calls=%fused_computation.45 | convolution fusion | flops 1811939328 | bytes 9043968 | tf_op jit(solution)/shard_map/dot_general | solution.py:22
  146.1 0.3 copy-done.1
  146.3 0.8 slice-done.1
  147.2 0.6 slice-done.2
  147.7 1.1 copy-done.6
  148.8 9.6 %fusion.6 = f32[2304,768]{0,1:T(8,128)} fusion(bf16[2304,2048]{1,0:T(8,128)(2,1)S(1)} %bitcast.44, bf16[1,2048,768]{2,1,0:T(8,128)(2,1)S(1)} %copy-done.6), kind=kOutput, calls=%fused_computation.19 | convolution fusion | flops 7247757312 | bytes 19660800 | tf_op jit(solution)/shard_map/dot_general | solution.py:15
  158.4 3.8 %all-gather.10.cloned.1.call-done = bf16[4096,1024]{1,0:T(8,128)(2,1)} async-done(((bf16[128,1024]{1,0:T(8,128)(2,1)}), bf16[4096,1024]{1,0:T(8,128)(2,1)}) %all-gather.10.cloned.1.call-update) | async-done | bytes 8388624 | tf_op jit(solution)/shard_map/all_gather | solution.py:88
  162.3 4.9 %multiply_convert_fusion = bf16[32,72,1024]{2,1,0:T(8,128)(2,1)S(1)} fusion(f32[32,72]{1,0:T(8,128)S(1)} %select_reduce_fusion, bf16[32,128,1024]{2,1,0:T(8,128)(2,1)} %bitcast.45, f32[32,128]{1,0:T(8,128)S(1)} %fusion.34, pred[32,128]{1,0:T(8,128)(4,1)S(1)} %convert_compare_fusion), kind=kOutput, calls=%fused_computation.7 | convolution fusion | flops 614006784 | bytes 13136896 | tf_op jit(solution)/shard_map/srt,stc->src/dot_general | solution.py:109
  167.2 0.0 copy-start.2
  167.2 2.8 copy-done.10
  170.0 5.6 %multiply_convert_fusion.4 = (bf16[2304,384]{0,1:T(8,128)(2,1)}, bf16[2304,384]{0,1:T(8,128)(2,1)}) fusion(f32[2304,768]{0,1:T(8,128)S(1)} %copy-done.10, f32[2304,384]{0,1:T(8,128)S(1)} %copy-done.9, bf16[2304,1024]{1,0:T(8,128)(2,1)S(1)} %bitcast.48, bf16[384,2048]{1,0:T(8,128)(2,1)S(1)} %bitcast.54), kind=kOutput, calls=%fused_computation.14 | convolution fusion | flops 1824325632 | bytes 19660800 | tf_op jit(solution)/shard_map/dot_general | solution.py:22
  175.6 9.9 %convolution_convert_fusion.2 = bf16[2304,2048]{1,0:T(8,128)(2,1)S(1)} fusion(bf16[1,2048,768]{2,1,0:T(8,128)(2,1)S(1)} %copy-done.7, bf16[2304,384]{0,1:T(8,128)(2,1)} %get-tuple-element.24, bf16[2304,384]{0,1:T(8,128)(2,1)} %get-tuple-element.23), kind=kOutput, calls=%fused_computation.2 | convolution fusion | flops 7259553792 | bytes 16121856 | tf_op jit(solution)/shard_map/dot_general | solution.py:34
  185.5 8.2 %convolution_convert_fusion = bf16[32,128,2048]{2,1,0:T(8,128)(2,1)} fusion(bf16[32,72,2048]{2,1,0:T(8,128)(2,1)S(1)} %bitcast.39, f32[32,128]{1,0:T(8,128)S(1)} %fusion.34, pred[32,128]{1,0:T(8,128)(4,1)S(1)} %convert_compare_fusion), kind=kOutput, calls=%fused_computation | convolution fusion | flops 1216937984 | bytes 26234880 | tf_op jit(solution)/shard_map/srt,src->stc/dot_general | solution.py:127
  193.7 0.0 reduce-scatter.2.cloned.1.call-update
  193.7 9.6 %fusion.8 = bf16[384,2048]{1,0:T(8,128)(2,1)S(1)} fusion(bf16[2304,1024]{1,0:T(8,128)(2,1)} %bitcast.49, bf16[2304,1024]{1,0:T(8,128)(2,1)} %bitcast.47, f32[2304,768]{0,1:T(8,128)} %fusion.6), kind=kOutput, calls=%fused_computation.22 | convolution fusion | flops 3648847872 | bytes 18087936 | tf_op jit(solution)/shard_map/dot_general | solution.py:30
  203.4 0.0 copy-start.11
  203.4 1.3 copy.23
  204.7 4.8 %all-to-all-start = ((bf16[384,4,512]{2,0,1:T(8,128)(2,1)}), bf16[384,4,512]{2,0,1:T(8,128)(2,1)S(1)}, u32[]{:S(2)}, u32[]{:S(2)}) async-start(bf16[384,4,512]{2,0,1:T(8,128)(2,1)} %bitcast.35), calls=%async_computation.1 | async-start | bytes 3145728 | tf_op jit(solution)/shard_map/all_to_all | solution.py:148
  209.5 12.4 %convolution_convert_fusion.3 = bf16[2048,768]{1,0:T(8,128)(2,1)} fusion(bf16[2304,2048]{1,0:T(8,128)(2,1)} %bitcast.41, bf16[2304,384]{0,1:T(8,128)(2,1)} %get-tuple-element.24, bf16[2304,384]{0,1:T(8,128)(2,1)S(1)} %copy-done.11), kind=kOutput, calls=%fused_computation.17 | convolution fusion | flops 7256408064 | bytes 16121856 | tf_op jit(solution)/shard_map/dot_general | solution.py:33
  221.9 7.2 %all-to-all-done = bf16[384,4,512]{2,0,1:T(8,128)(2,1)S(1)} async-done(((bf16[384,4,512]{2,0,1:T(8,128)(2,1)}), bf16[384,4,512]{2,0,1:T(8,128)(2,1)S(1)}, u32[]{:S(2)}, u32[]{:S(2)}) %all-to-all-start) | async-done | bytes 1572896 | tf_op jit(solution)/shard_map/all_to_all | solution.py:148
  229.2 1.1 copy-done
  230.3 5.2 %all-to-all-start.1 = ((bf16[4,512,768]{2,1,0:T(8,128)(2,1)}), bf16[4,512,768]{2,1,0:T(8,128)(2,1)S(1)}, u32[]{:S(2)}, u32[]{:S(2)}) async-start(bf16[4,512,768]{2,1,0:T(8,128)(2,1)} %bitcast.50), calls=%async_computation.2 | async-start | bytes 6291456 | tf_op jit(solution)/shard_map/all_to_all | solution.py:144
  235.5 2.7 convert_reduce_fusion.1
  238.3 32.9 %all-to-all-done.1 = bf16[4,512,768]{2,1,0:T(8,128)(2,1)S(1)} async-done(((bf16[4,512,768]{2,1,0:T(8,128)(2,1)}), bf16[4,512,768]{2,1,0:T(8,128)(2,1)S(1)}, u32[]{:S(2)}, u32[]{:S(2)}) %all-to-all-start.1) | async-done | bytes 3145760 | tf_op jit(solution)/shard_map/all_to_all | solution.py:144
  271.2 0.4 convert_reduce_fusion
  271.6 1.0 copy-done.3
  272.7 0.5 copy-done.4
  273.2 3.9 %fusion.26 = (bf16[512,768]{1,0:T(8,128)(2,1)S(1)}, f32[1,512,768]{2,1,0:T(8,128)}, f32[1,512,768]{2,1,0:T(8,128)}) fusion(bf16[1,2048,768]{2,1,0:T(8,128)(2,1)} %param.14, s32[]{:T(128)S(6)} %select_n.14, f32[512,768]{1,0:T(8,128)S(1)} %convert_reduce_fusion, f32[1,512,768]{2,1,0:T(8,128)S(1)} %copy-done.3, f32[1,512,768]{2,1,0:T(8,128)S(1)} %copy-done.4), kind=kLoop, calls=%fused_computation.49 | loop fusion | flops 5111808 | bytes 9437188 | tf_op jit(solution)/shard_map/broadcast_in_dim | solution.py:163
  277.0 1.9 broadcast_in_dim.40
  278.9 5.1 %all-to-all-start.2 = ((bf16[4,512,768]{2,1,0:T(8,128)(2,1)}), bf16[4,512,768]{2,1,0:T(8,128)(2,1)S(1)}, u32[]{:S(2)}, u32[]{:S(2)}) async-start(bf16[4,512,768]{2,1,0:T(8,128)(2,1)} %broadcast_in_dim.40), calls=%async_computation.3 | async-start | bytes 6291456 | tf_op jit(solution)/shard_map/all_to_all | solution.py:162
  284.0 24.6 %reduce-scatter.2.cloned.1.call-done = bf16[128,2048]{1,0:T(8,128)(2,1)} async-done(((bf16[4096,2048]{1,0:T(8,128)(2,1)}), bf16[128,2048]{1,0:T(8,128)(2,1)}) %reduce-scatter.2.cloned.1.call-update) | async-done | bytes 524304 | tf_op jit(solution)/shard_map/reduce_scatter | solution.py:133
  308.5 3.3 subtract_convert_fusion.1
  311.9 0.0 all-gather.6.cloned.1.call-update
  311.9 6.8 %all-to-all-done.2 = bf16[4,512,768]{2,1,0:T(8,128)(2,1)S(1)} async-done(((bf16[4,512,768]{2,1,0:T(8,128)(2,1)}), bf16[4,512,768]{2,1,0:T(8,128)(2,1)S(1)}, u32[]{:S(2)}, u32[]{:S(2)}) %all-to-all-start.2) | async-done | bytes 3145760 | tf_op jit(solution)/shard_map/all_to_all | solution.py:162
  318.7 19.7 %all-gather.6.cloned.1.call-done = bf16[1,384,2048]{2,1,0:T(8,128)(2,1)} async-done(((bf16[1,384,512]{2,1,0:T(8,128)(2,1)}), bf16[1,384,2048]{2,1,0:T(8,128)(2,1)}) %all-gather.6.cloned.1.call-update) | async-done | bytes 1572880 | tf_op jit(solution)/shard_map/all_gather | solution.py:165
  338.4 1.7 copy.26
  340.1 0.9 copy-done.5
  341.0 1.1 copy.27
  (17 shorter events, 0.0 us)
Async XLA Ops:
  7.2 99.7 %all-gather.8.cloned.1.call-start = ((), (), s32[]{:S(2)}) async-start(), calls=%async_computation.6 | async-start | bytes 27033600 | tf_op jit(solution)/shard_map/all_gather | solution.py:84
  11.7 150.5 %all-gather.10.cloned.1.call-start = ((), (), s32[]{:S(2)}) async-start(), calls=%async_computation.7 | async-start | bytes 8650752 | tf_op jit(solution)/shard_map/all_gather | solution.py:88
  108.6 200.0 %reduce-scatter.2.cloned.1.call-start = ((), (), s32[]{:S(2)}) async-start(), calls=%async_computation.4 | async-start | bytes 17301504 | tf_op jit(solution)/shard_map/reduce_scatter | solution.py:133
  128.8 13.4 %copy-start.8 = (bf16[1,384,2048]{2,1,0:T(8,128)(2,1)S(1)}, bf16[1,384,2048]{2,1,0:T(8,128)(2,1)}, u32[]{:S(2)}) copy-start(bf16[1,384,2048]{2,1,0:T(8,128)(2,1)} %param.15) | copy-start | bytes 4718596
  138.9 7.5 %slice-start = ((s8[9437184]{0:T(1024)(128)(4,1)}), s8[4194304]{0:T(1024)(128)(4,1)S(1)}, s32[]{:S(2)}) async-start(s8[9437184]{0:T(1024)(128)(4,1)} %bitcast.42), calls=%async_computation.8 | async-start | bytes 8388608
  138.9 8.3 %slice-start.1 = ((s8[9437184]{0:T(1024)(128)(4,1)}), s8[4194304]{0:T(1024)(128)(4,1)S(1)}, s32[]{:S(2)}) async-start(s8[9437184]{0:T(1024)(128)(4,1)} %bitcast.42), calls=%async_computation.9 | async-start | bytes 8388608
  142.2 4.1 %copy-start.1 = (bf16[32,72,1024]{2,1,0:T(8,128)(2,1)}, bf16[32,72,1024]{2,1,0:T(8,128)(2,1)S(1)}, u32[]{:S(2)}) copy-start(bf16[32,72,1024]{2,1,0:T(8,128)(2,1)S(1)} %multiply_convert_fusion.1) | copy-start | bytes 14155780
  142.2 5.5 %slice-start.2 = ((s8[9437184]{0:T(1024)(128)(4,1)}), s8[1048576]{0:T(1024)(128)(4,1)S(1)}, s32[]{:S(2)}) async-start(s8[9437184]{0:T(1024)(128)(4,1)} %bitcast.42), calls=%async_computation.10 | async-start | bytes 2097152
  142.3 6.6 %copy-start.6 = (bf16[1,2048,768]{2,1,0:T(8,128)(2,1)S(1)}, bf16[1,2048,768]{2,1,0:T(8,128)(2,1)}, u32[]{:S(2)}) copy-start(bf16[1,2048,768]{2,1,0:T(8,128)(2,1)} %param.14) | copy-start | bytes 9437188
  162.3 5.0 %copy-start.9 = (f32[2304,384]{0,1:T(8,128)S(1)}, f32[2304,384]{0,1:T(8,128)}, u32[]{:S(2)}) copy-start(f32[2304,384]{0,1:T(8,128)} %fusion.24) | copy-start | bytes 10616836
  162.3 7.7 %copy-start.10 = (f32[2304,768]{0,1:T(8,128)S(1)}, f32[2304,768]{0,1:T(8,128)}, u32[]{:S(2)}) copy-start(f32[2304,768]{0,1:T(8,128)} %fusion.6) | copy-start | bytes 21233668
  167.2 8.4 %copy-start.2 = (bf16[32,72,1024]{2,1,0:T(8,128)(2,1)}, bf16[32,72,1024]{2,1,0:T(8,128)(2,1)S(1)}, u32[]{:S(2)}) copy-start(bf16[32,72,1024]{2,1,0:T(8,128)(2,1)S(1)} %multiply_convert_fusion) | copy-start | bytes 14155780
  170.0 5.6 %copy-start.7 = (bf16[1,2048,768]{2,1,0:T(8,128)(2,1)S(1)}, bf16[1,2048,768]{2,1,0:T(8,128)(2,1)}, u32[]{:S(2)}) copy-start(bf16[1,2048,768]{2,1,0:T(8,128)(2,1)} %param.14) | copy-start | bytes 9437188
  203.4 6.1 %copy-start.11 = (bf16[2304,384]{0,1:T(8,128)(2,1)S(1)}, bf16[2304,384]{0,1:T(8,128)(2,1)}, u32[]{:S(2)}) copy-start(bf16[2304,384]{0,1:T(8,128)(2,1)} %get-tuple-element.23) | copy-start | bytes 5308420
  204.7 24.5 %all-to-all-start = ((bf16[384,4,512]{2,0,1:T(8,128)(2,1)}), bf16[384,4,512]{2,0,1:T(8,128)(2,1)S(1)}, u32[]{:S(2)}, u32[]{:S(2)}) async-start(bf16[384,4,512]{2,0,1:T(8,128)(2,1)} %bitcast.35), calls=%async_computation.1 | async-start | bytes 3145728 | tf_op jit(solution)/shard_map/all_to_all | solution.py:148
  229.2 1.1 copy-start
  230.3 40.9 %all-to-all-start.1 = ((bf16[4,512,768]{2,1,0:T(8,128)(2,1)}), bf16[4,512,768]{2,1,0:T(8,128)(2,1)S(1)}, u32[]{:S(2)}, u32[]{:S(2)}) async-start(bf16[4,512,768]{2,1,0:T(8,128)(2,1)} %bitcast.50), calls=%async_computation.2 | async-start | bytes 6291456 | tf_op jit(solution)/shard_map/all_to_all | solution.py:144
  271.2 1.5 copy-start.3
  271.2 2.0 copy-start.4
  278.9 39.8 %all-to-all-start.2 = ((bf16[4,512,768]{2,1,0:T(8,128)(2,1)}), bf16[4,512,768]{2,1,0:T(8,128)(2,1)S(1)}, u32[]{:S(2)}, u32[]{:S(2)}) async-start(bf16[4,512,768]{2,1,0:T(8,128)(2,1)} %broadcast_in_dim.40), calls=%async_computation.3 | async-start | bytes 6291456 | tf_op jit(solution)/shard_map/all_to_all | solution.py:162
  284.0 54.4 %all-gather.6.cloned.1.call-start = ((), (), s32[]{:S(2)}) async-start(), calls=%async_computation.5 | async-start | bytes 1966080 | tf_op jit(solution)/shard_map/all_gather | solution.py:165
  338.4 2.5 copy-start.5
Sparse Core Ops, SparseCore 0:
  11.8 94.9 all-gather.7
  109.7 52.5 all-gather.9
  193.8 114.6 reduce-scatter.1
  312.0 26.3 all-gather.5
